TPU v7x, 512 devices: a whole 4x8x8 slice. The times are simulated.
512 devices in a mesh: req: 64 (over x, z, core), tp: 8 (over y).
Axes of the slice: x: 4, y: 8, z: 8, core: 2. Of those that a mesh axis runs over, the one named last changes fastest.
Arguments:
- queries: bfloat16 [1280, 2048], P('req', 'tp')
- new_keys: bfloat16 [1280, 2048], P('req', 'tp'), may hold values from -6 to 6
- new_values: bfloat16 [1280, 2048], P('req', 'tp'), may hold values from -6 to 6
- cache_keys: bfloat16 [256, 384, 2048], P('req', None, 'tp'), may hold values from -6 to 6
- cache_values: bfloat16 [256, 384, 2048], P('req', None, 'tp'), may hold values from -6 to 6
- cache_lengths: int32 [256], P('req'), may hold values from 1 to 384, as said below
- hidden_in: bfloat16 [1280, 2048], P('req'), may hold values from -6 to 6
- out_weight: bfloat16 [2048, 2048], P('tp'), may hold values from -0.125 to 0.125
- norm_gain: float32 [2048], replicated, may hold values from 0.25 to 1.75
- routes: int32 [1280, 6], P('req'), may hold values from 0 to 63, all different within a row; in each aligned block of 20 rows (0 to 19, 20 to 39, ...) at most 3 rows name the same one
- route_gates: float32 [1280, 6], P('req'), may hold values from 0.05 to 0.5
- gate_weight: bfloat16 [64, 2048, 1408], P('req', None, 'tp'), may hold values from -0.125 to 0.125
- up_weight: bfloat16 [64, 2048, 1408], P('req', None, 'tp'), may hold values from -0.125 to 0.125
- down_weight: bfloat16 [64, 1408, 2048], P('req', 'tp'), may hold values from -0.15625 to 0.15625
Outputs:
- hidden_out: bfloat16 [1280, 2048], P('req', 'tp')
Inputs may be any that keep to these rules, and one draw needn't show every extreme that they name: `cache_lengths`: at least one request has all 384 slots live. `routes`: each token names 6 different experts; within each aligned block of 20 tokens (the tokens of one index of req) no expert is named more than 3 times.
All inputs are finite; a program needn't handle non-finite values.
Results may differ from a plain program's by a relative error of at most 0.008.
Values may be sent and summed in bfloat16 or wider, within the bound.
No kernel may reach another device: no remote copies, remote signals or barrier semaphores. Data moves between devices by JAX's collectives and lax.ppermute only.
A program may use at most 64 MiB of HBM per device.

v0:
```python
import jax
import jax.numpy as jnp
from jax import lax
from jax.sharding import PartitionSpec as P

HD = 128
EXPERTS = 64
POS = 5
CACHE = 384
CAP = 3


def slot_tables(local_routes, local_gates):
    flat_routes = local_routes.reshape(-1)
    expert_ids = jnp.arange(EXPERTS, dtype=jnp.int32)
    onehot = (flat_routes[:, None] == expert_ids[None, :]).astype(jnp.int32)
    before = jnp.cumsum(onehot, axis=0) - onehot
    ranks = jnp.sum(before * onehot, axis=1)
    slot_ids = (flat_routes * CAP + ranks).reshape(local_routes.shape)
    slot_range = jnp.arange(EXPERTS * CAP, dtype=jnp.int32)
    matches = slot_ids[None, :, :] == slot_range[:, None, None]
    dispatch = jnp.any(matches, axis=-1).astype(jnp.bfloat16)
    combine = jnp.sum(jnp.where(matches, local_gates[None, :, :], 0.0), axis=-1).T
    return (dispatch, combine)


def attend_local(queries, new_keys, new_values, cache_keys, cache_values, cache_lengths):
    req_count = cache_keys.shape[0]
    head_count = queries.shape[1] // HD
    all_keys = jnp.concatenate([cache_keys, new_keys.reshape(req_count, POS, -1)], axis=1).reshape(
        req_count, CACHE + POS, head_count, HD
    )
    all_values = jnp.concatenate(
        [cache_values, new_values.reshape(req_count, POS, -1)], axis=1
    ).reshape(req_count, CACHE + POS, head_count, HD)
    local_q = queries.reshape(req_count, POS, head_count, HD)
    scores = jnp.einsum(
        "rphd,rjhd->rhpj", local_q, all_keys, preferred_element_type=jnp.float32
    ) * HD ** (-0.5)
    key_pos = jnp.arange(CACHE + POS, dtype=jnp.int32)
    query_pos = jnp.arange(POS, dtype=jnp.int32)
    cache_live = key_pos[None, None, :] < cache_lengths[:, None, None]
    fresh_live = key_pos[None, None, :] - CACHE <= query_pos[None, :, None]
    live = jnp.where(key_pos[None, None, :] < CACHE, cache_live, fresh_live)
    scores = jnp.where(live[:, None, :, :], scores, -1e30)
    top = jnp.max(scores, axis=-1, keepdims=True)
    expo = jnp.exp(scores - top)
    weights = (expo / jnp.sum(expo, axis=-1, keepdims=True)).astype(jnp.bfloat16)
    attended = jnp.einsum(
        "rhpj,rjhd->rphd", weights, all_values, preferred_element_type=jnp.float32
    )
    return attended.astype(jnp.bfloat16).reshape(req_count * POS, head_count * HD)


def expert_apply(slot_rows, gate_weight, up_weight, down_weight):
    gated = jnp.einsum("secd,edf->secf", slot_rows, gate_weight, preferred_element_type=jnp.float32)
    upward = jnp.einsum("secd,edf->secf", slot_rows, up_weight, preferred_element_type=jnp.float32)
    activation = (jax.nn.silu(gated) * upward).astype(jnp.bfloat16)
    return jnp.einsum("secf,efd->secd", activation, down_weight, preferred_element_type=jnp.float32)


def local(
    queries,
    new_keys,
    new_values,
    cache_keys,
    cache_values,
    cache_lengths,
    hidden_in,
    out_weight,
    norm_gain,
    routes,
    route_gates,
    gate_weight,
    up_weight,
    down_weight,
):
    attended = attend_local(queries, new_keys, new_values, cache_keys, cache_values, cache_lengths)
    partial_value = jnp.dot(attended, out_weight, preferred_element_type=jnp.float32)
    model_width = partial_value.shape[1]
    tp_count = lax.axis_size("tp")
    columns = model_width // tp_count
    offset = lax.axis_index("tp") * columns
    holders = lax.axis_size("req")
    dispatch, combine = slot_tables(routes, route_gates)
    summed = lax.psum(partial_value, "tp") + hidden_in.astype(jnp.float32)
    mean_square = jnp.mean(summed * summed, axis=-1, keepdims=True)
    normed = (summed * lax.rsqrt(mean_square + 1e-06) * norm_gain[None, :]).astype(jnp.bfloat16)
    outbound = jnp.dot(dispatch, normed, preferred_element_type=jnp.float32).astype(jnp.bfloat16)
    outbound = outbound.reshape(holders, -1, CAP, model_width)
    produced = expert_apply(
        lax.all_to_all(outbound, "req", split_axis=0, concat_axis=0, tiled=True),
        gate_weight,
        up_weight,
        down_weight,
    )
    returned = lax.all_to_all(
        produced.astype(jnp.bfloat16), "req", split_axis=0, concat_axis=0, tiled=True
    ).astype(produced.dtype)
    expert_sum = jnp.dot(
        combine,
        returned.reshape(-1, model_width),
        precision=lax.Precision.HIGHEST,
        preferred_element_type=jnp.float32,
    )
    expert_cols = lax.psum_scatter(
        expert_sum.astype(jnp.bfloat16), "tp", scatter_dimension=1, tiled=True
    ).astype(jnp.float32)
    summed_cols = lax.dynamic_slice_in_dim(summed, offset, columns, 1)
    return (summed_cols + expert_cols).astype(jnp.bfloat16)


def solution(mesh):
    in_specs = (
        P("req", "tp"),
        P("req", "tp"),
        P("req", "tp"),
        P("req", None, "tp"),
        P("req", None, "tp"),
        P("req"),
        P("req", None),
        P("tp", None),
        P(),
        P("req", None),
        P("req", None),
        P("req", None, "tp"),
        P("req", None, "tp"),
        P("req", "tp", None),
    )
    out_specs = P("req", "tp")
    return jax.shard_map(local, mesh=mesh, in_specs=in_specs, out_specs=out_specs, check_vma=False)
```

profile of v0, /device:TPU:2, one launch (start us, length us, event | category | flops | bytes accessed | tf_op | source)
XLA Modules:
  0.0 220.3 jit_solution(8481350041058466535)
XLA Ops:
  6.5 1.6 copy.64
  8.2 0.4 copy.65
  8.6 0.2 copy-done.4
  9.0 0.3 copy-done.1
  9.3 0.4 copy.61
  9.7 0.4 copy.62
  10.1 0.3 copy-done.6
  10.4 0.6 fusion.71
  11.0 0.6 fusion.9
  11.7 0.9 fusion.76
  12.7 0.1 copy.69
  12.8 0.1 eq.28
  13.0 0.2 reduce_window_sum.11
  13.1 0.2 select_reduce_fusion.1
  13.3 0.1 reduce_sum.40
  13.4 0.1 copy.70
  13.5 0.1 fusion.33
  13.6 81.7 %all-reduce.2.cloned.1.call-done = f32[20,2048]{1,0:T(8,128)} async-done(((f32[20,2048]{1,0:T(8,128)}), f32[20,2048]{1,0:T(8,128)}) %all-reduce.2.cloned.1.call-update) | async-done | bytes 163856 | tf_op jit(solution)/shard_map/psum | solution.py:86
  95.3 1.1 multiply_reduce_fusion
  96.4 0.4 convolution_convert_fusion.1
  96.8 0.5 reshape.120
  97.4 37.8 %all_to_all.10 = bf16[64,1,3,2048]{3,2,1,0:T(4,128)(2,1)S(1)} all-to-all(bf16[64,1,3,2048]{3,2,1,0:T(4,128)(2,1)S(1)} %bitcast.79), channel_id=1, replica_groups=mesh['req'=64,'tp'=8] {'req'}, dimensions={0} | all-to-all | bytes 1572864 | tf_op jit(solution)/shard_map/all_to_all | solution.py:92
  135.2 1.0 convolution_bitcast_fusion.1
  136.2 2.6 %fusion.1 = bf16[64,1,3,2048]{3,0,2,1:T(8,128)(2,1)S(1)} fusion(bf16[1,176,2048]{2,1,0:T(8,128)(2,1)} %param.27, bf16[1,2048,176]{1,2,0:T(8,128)(2,1)} %param.26, bf16[64,1,3,2048]{3,2,1,0:T(4,128)(2,1)S(1)} %all_to_all.10, f32[64,1,3,176]{3,0,2,1:T(8,128)S(1)} %convolution_bitcast_fusion.1), kind=kOutput, calls=%fused_computation.3 | convolution fusion | flops 277420032 | bytes 3149824 | tf_op jit(solution)/shard_map/secf,efd->secd/dot_general | solution.py:59
  138.8 1.7 copy.73
  140.5 7.9 %all-to-all-start.1 = ((bf16[64,1,3,2048]{3,2,1,0:T(4,128)(2,1)}), bf16[64,1,3,2048]{3,2,1,0:T(4,128)(2,1)S(1)}, u32[]{:S(2)}, u32[]{:S(2)}) async-start(bf16[64,1,3,2048]{3,2,1,0:T(4,128)(2,1)} %copy.73), calls=%async_computation.1 | async-start | bytes 2097152 | tf_op jit(solution)/shard_map/all_to_all | solution.py:97
  148.4 0.1 select_reduce_fusion
  148.5 26.8 %all-to-all-done.1 = bf16[64,1,3,2048]{3,2,1,0:T(4,128)(2,1)S(1)} async-done(((bf16[64,1,3,2048]{3,2,1,0:T(4,128)(2,1)}), bf16[64,1,3,2048]{3,2,1,0:T(4,128)(2,1)S(1)}, u32[]{:S(2)}, u32[]{:S(2)}) %all-to-all-start.1) | async-done | bytes 786464 | tf_op jit(solution)/shard_map/all_to_all | solution.py:97
  175.3 0.7 reshape.126
  176.0 1.1 convolution_convert_fusion.2
  177.1 35.1 %reduce-scatter.2.cloned.1.call-done = bf16[20,256]{1,0:T(8,128)(2,1)} async-done(((bf16[20,2048]{1,0:T(8,128)(2,1)}), bf16[20,256]{1,0:T(8,128)(2,1)}) %reduce-scatter.2.cloned.1.call-update) | async-done | bytes 10256 | tf_op jit(solution)/shard_map/reduce_scatter | solution.py:106
  212.2 1.3 add_convert_fusion
  (39 shorter events, 0.4 us)
Async XLA Ops:
  6.5 5.2 %copy-start = (bf16[256,2048]{1,0:T(8,128)(2,1)S(1)}, bf16[256,2048]{1,0:T(8,128)(2,1)}, u32[]{:S(2)}) copy-start(bf16[256,2048]{1,0:T(8,128)(2,1)} %param.21) | copy-start | bytes 3145732
  6.5 88.8 %all-reduce.2.cloned.1.call-start = ((), (), s32[]{:S(2)}) async-start(), calls=%async_computation.3 | async-start | bytes 393216 | tf_op jit(solution)/shard_map/psum | solution.py:86
  8.1 0.7 copy-start.4
  8.1 0.7 copy-start.9
  8.2 0.8 copy-start.5
  8.2 1.1 copy-start.1
  9.7 0.7 copy-start.6
  11.6 1.1 copy-start.3
  11.6 83.7 %copy-start.2 = (bf16[20,2048]{1,0:T(8,128)(2,1)S(1)}, bf16[20,2048]{1,0:T(8,128)(2,1)}, u32[]{:S(2)}) copy-start(bf16[20,2048]{1,0:T(8,128)(2,1)} %param.20) | copy-start | bytes 245764
  11.7 84.7 %copy-start.7 = (f32[2048]{0:T(1024)S(1)}, f32[2048]{0:T(1024)}, u32[]{:S(2)}) copy-start(f32[2048]{0:T(1024)} %param.22) | copy-start | bytes 24580
  97.4 37.8 %copy-start.10 = (bf16[1,2048,176]{1,2,0:T(8,128)(2,1)S(1)}, bf16[1,2048,176]{1,2,0:T(8,128)(2,1)}, u32[]{:S(2)}) copy-start(bf16[1,2048,176]{1,2,0:T(8,128)(2,1)} %param.25) | copy-start | bytes 2162692
  140.5 8.0 %copy-start.8 = (f32[20,6]{0,1:T(8,128)S(1)}, f32[20,6]{0,1:T(8,128)}, u32[]{:S(2)}) copy-start(f32[20,6]{0,1:T(8,128)} %param.24) | copy-start | bytes 1444
  140.5 34.9 %all-to-all-start.1 = ((bf16[64,1,3,2048]{3,2,1,0:T(4,128)(2,1)}), bf16[64,1,3,2048]{3,2,1,0:T(4,128)(2,1)S(1)}, u32[]{:S(2)}, u32[]{:S(2)}) async-start(bf16[64,1,3,2048]{3,2,1,0:T(4,128)(2,1)} %copy.73), calls=%async_computation.1 | async-start | bytes 2097152 | tf_op jit(solution)/shard_map/all_to_all | solution.py:97
  148.4 63.8 %reduce-scatter.2.cloned.1.call-start = ((), (), s32[]{:S(2)}) async-start(), calls=%async_computation.4 | async-start | bytes 110592 | tf_op jit(solution)/shard_map/reduce_scatter | solution.py:106
Sparse Core Ops, SparseCore 0:
  12.8 82.4 all-reduce.1
  177.2 34.9 reduce-scatter.1
where the time goes:
time: 221 us; the launch traced here: 220 us
  waiting for transfers between devices  144 us (65%)
  blocking collectives  37.8 us (17%)
  between operations  13.7 us (6%)
  starting transfers between devices  7.95 us (4%)
  matrix products  7.21 us (3%)
  local copies, waits for them, and re-layouts  6.98 us (3%)
  other arithmetic  3.12 us (1%)
    psum x1, waiting for transfers between devices, local(): summed = lax.psum(partial_value, 'tp') + hidden_in.astype(jnp.float32)  81.7 us
    all_to_all x1, blocking collectives, local(): lax.all_to_all(outbound, 'req', split_axis=0, concat_axis=0, tiled=True)  37.8 us
    reduce_scatter x1, waiting for transfers between devices, local(): lax.psum_scatter(expert_sum.astype(jnp.bfloat16), 'tp', scatter_dimension...  35.1 us
    all_to_all x1, waiting for transfers between devices, local(): lax.all_to_all(produced.astype(jnp.bfloat16), 'req', split_axis=0, concat...  26.8 us
    all_to_all x1, starting transfers between devices, local(): lax.all_to_all(produced.astype(jnp.bfloat16), 'req', split_axis=0, concat...  7.9 us
  transfers between devices with their start and end apart: 3, of which 3 were waited for; matrix products, arithmetic and copies ran while one was open for 0% of the time, Pallas kernels for 0%

commit v1 on v0

--- a/solution.py
+++ b/solution.py
@@ -59,6 +59,20 @@
     return jnp.einsum("secf,efd->secd", activation, down_weight, preferred_element_type=jnp.float32)
 
 
+def scatter_sum(value, tp_count):
+    rows, width = value.shape
+    pieces = value.reshape(rows, tp_count, width // tp_count).transpose(1, 0, 2)
+    pieces = lax.all_to_all(pieces, "tp", split_axis=0, concat_axis=0, tiled=True)
+    return jnp.sum(pieces.astype(jnp.float32), axis=0)
+
+
+def gather_cols(value, tp_count):
+    rows, columns = value.shape
+    pieces = jnp.broadcast_to(value[None], (tp_count, rows, columns))
+    pieces = lax.all_to_all(pieces, "tp", split_axis=0, concat_axis=0, tiled=True)
+    return pieces.transpose(1, 0, 2).reshape(rows, tp_count * columns)
+
+
 def local(
     queries,
     new_keys,
@@ -83,7 +97,9 @@
     offset = lax.axis_index("tp") * columns
     holders = lax.axis_size("req")
     dispatch, combine = slot_tables(routes, route_gates)
-    summed = lax.psum(partial_value, "tp") + hidden_in.astype(jnp.float32)
+    hidden_cols = lax.dynamic_slice_in_dim(hidden_in, offset, columns, 1).astype(jnp.float32)
+    summed_cols = scatter_sum(partial_value, tp_count) + hidden_cols
+    summed = gather_cols(summed_cols, tp_count)
     mean_square = jnp.mean(summed * summed, axis=-1, keepdims=True)
     normed = (summed * lax.rsqrt(mean_square + 1e-06) * norm_gain[None, :]).astype(jnp.bfloat16)
     outbound = jnp.dot(dispatch, normed, preferred_element_type=jnp.float32).astype(jnp.bfloat16)
@@ -103,10 +119,7 @@
         precision=lax.Precision.HIGHEST,
         preferred_element_type=jnp.float32,
     )
-    expert_cols = lax.psum_scatter(
-        expert_sum.astype(jnp.bfloat16), "tp", scatter_dimension=1, tiled=True
-    ).astype(jnp.float32)
-    summed_cols = lax.dynamic_slice_in_dim(summed, offset, columns, 1)
+    expert_cols = scatter_sum(expert_sum.astype(jnp.bfloat16), tp_count)
     return (summed_cols + expert_cols).astype(jnp.bfloat16)
 
 

time: 221 us -> 140 us (0.63)
  the two profiles are of different devices: /device:TPU:2 before, /device:TPU:7 now
where the time goes in v1:
time: 140 us; the launch traced here: 138 us
  blocking collectives  55.6 us (40%)
  waiting for transfers between devices  44.9 us (32%)
  starting transfers between devices  16.7 us (12%)
  local copies, waits for them, and re-layouts  9.74 us (7%)
  matrix products  8.88 us (6%)
  other arithmetic  2.23 us (2%)
    all_to_all x1, blocking collectives, local(): lax.all_to_all(outbound, 'req', split_axis=0, concat_axis=0, tiled=True)  45.5 us
    all_to_all x1, waiting for transfers between devices, local(): lax.all_to_all(produced.astype(jnp.bfloat16), 'req', split_axis=0, concat...  28.3 us
    all_to_all x1, blocking collectives, scatter_sum(): lax.all_to_all(pieces, 'tp', split_axis=0, concat_axis=0, tiled=True)  10.1 us
    all_to_all x1, waiting for transfers between devices, gather_cols(): lax.all_to_all(pieces, 'tp', split_axis=0, concat_axis=0, tiled=True)  8.44 us
    all_to_all x1, waiting for transfers between devices, scatter_sum(): lax.all_to_all(pieces, 'tp', split_axis=0, concat_axis=0, tiled=True)  8.17 us
    all_to_all x1, starting transfers between devices, scatter_sum(): lax.all_to_all(pieces, 'tp', split_axis=0, concat_axis=0, tiled=True)  6.82 us
    all_to_all x1, starting transfers between devices, local(): lax.all_to_all(produced.astype(jnp.bfloat16), 'req', split_axis=0, concat...  6.45 us
    all_to_all x1, starting transfers between devices, gather_cols(): lax.all_to_all(pieces, 'tp', split_axis=0, concat_axis=0, tiled=True)  3.39 us
  transfers between devices with their start and end apart: 3, of which 3 were waited for; matrix products, arithmetic and copies ran while one was open for 1% of the time, Pallas kernels for 0%

profile of v1, /device:TPU:7, one launch (start us, length us, event | category | flops | bytes accessed | tf_op | source)
XLA Modules:
  0.0 138.3 jit_solution(15719114661209773780)
XLA Ops:
  0.0 0.8 concatenate.17
  0.8 1.5 %copy.69 = bf16[4,384,256]{1,2,0:T(8,128)(2,1)S(1)} copy(bf16[4,384,256]{2,1,0:T(8,128)(2,1)} %param.18) | data formatting | bytes 1572864 | tf_op args[4]
  2.3 1.2 copy.70
  3.5 0.4 copy.72
  3.9 1.2 copy.73
  5.2 1.8 %fusion.71 = f32[4,2,5]{2,1,0:T(2,128)S(1)} fusion(bf16[4,5,2,128]{3,1,2,0:T(8,128)(2,1)S(1)} %copy.74, bf16[4,384,2,128]{3,1,2,0:T(8,128)(2,1)} %copy.73, pred[4,5,389]{2,1,0:T(8,128)(4,1)S(1)} %broadcast_select_fusion, bf16[4,5,2,128]{3,2,1,0:T(2,128)(2,1)S(1)} %reshape.127), kind=kOutput, calls=%fused_computation.71 | convolution fusion | flops 5639332 | bytes 814852 | tf_op jit(solution)/shard_map/sub | solution.py:47
  7.0 1.8 %fusion.9 = bf16[4,5,2,128]{3,1,2,0:T(8,128)(2,1)S(1)} fusion(bf16[4,5,2,128]{3,1,2,0:T(8,128)(2,1)S(1)} %copy.71, bf16[4,384,2,128]{3,1,2,0:T(8,128)(2,1)S(1)} %copy-done.3, f32[4,2,5]{2,1,0:T(2,128)S(1)} %fusion.71, bf16[4,5,2,128]{3,1,2,0:T(8,128)(2,1)S(1)} %copy.74, bf16[4,384,2,128]{3,1,2,0:T(8,128)(2,1)} %copy.73, ...), kind=kOutput, calls=%fused_computation.17 | convolution fusion | flops 11236756 | bytes 1621764 | tf_op jit(solution)/shard_map/rhpj,rjhd->rphd/dot_general | solution.py:49
  8.9 0.5 copy.85
  9.5 1.1 convolution_bitcast_fusion
  10.5 6.8 %all-to-all-start = ((f32[8,20,256]{2,1,0:T(8,128)}), f32[8,20,256]{2,1,0:T(8,128)S(1)}, u32[]{:S(2)}, u32[]{:S(2)}) async-start(f32[8,20,256]{2,1,0:T(8,128)} %convolution_bitcast_fusion), calls=%async_computation | async-start | bytes 393216 | tf_op jit(solution)/shard_map/all_to_all | solution.py:65
  17.3 0.1 copy.78
  17.6 0.2 reduce_window_sum.11
  17.8 0.2 select_reduce_fusion.1
  18.2 8.2 %all-to-all-done = f32[8,20,256]{2,1,0:T(8,128)S(1)} async-done(((f32[8,20,256]{2,1,0:T(8,128)}), f32[8,20,256]{2,1,0:T(8,128)S(1)}, u32[]{:S(2)}, u32[]{:S(2)}) %all-to-all-start) | async-done | bytes 163872 | tf_op jit(solution)/shard_map/all_to_all | solution.py:65
  26.4 0.7 convert_add_fusion
  27.1 0.7 broadcast_in_dim.74
  27.8 3.4 %all-to-all-start.1 = ((f32[8,20,256]{2,1,0:T(8,128)}), f32[8,20,256]{2,1,0:T(8,128)S(1)}, u32[]{:S(2)}, u32[]{:S(2)}) async-start(f32[8,20,256]{2,1,0:T(8,128)} %broadcast_in_dim.74), calls=%async_computation.1 | async-start | bytes 393216 | tf_op jit(solution)/shard_map/all_to_all | solution.py:72
  31.3 8.4 %all-to-all-done.1 = f32[8,20,256]{2,1,0:T(8,128)S(1)} async-done(((f32[8,20,256]{2,1,0:T(8,128)}), f32[8,20,256]{2,1,0:T(8,128)S(1)}, u32[]{:S(2)}, u32[]{:S(2)}) %all-to-all-start.1) | async-done | bytes 163872 | tf_op jit(solution)/shard_map/all_to_all | solution.py:72
  39.9 0.1 multiply_reduce_fusion
  40.0 0.4 convolution_convert_fusion.1
  40.5 0.5 reshape.130
  41.0 45.5 %all_to_all.25 = bf16[64,1,3,2048]{3,2,1,0:T(4,128)(2,1)S(1)} all-to-all(bf16[64,1,3,2048]{3,2,1,0:T(4,128)(2,1)S(1)} %bitcast.90), channel_id=1, replica_groups=mesh['req'=64,'tp'=8] {'req'}, dimensions={0} | all-to-all | bytes 1572864 | tf_op jit(solution)/shard_map/all_to_all | solution.py:108
  86.5 1.0 convolution_bitcast_fusion.2
  87.6 2.3 %fusion.1 = bf16[64,1,3,2048]{3,0,2,1:T(8,128)(2,1)S(1)} fusion(bf16[1,176,2048]{2,1,0:T(8,128)(2,1)S(1)} %copy-done, bf16[1,2048,176]{1,2,0:T(8,128)(2,1)} %param.26, bf16[64,1,3,2048]{3,2,1,0:T(4,128)(2,1)S(1)} %all_to_all.25, f32[64,1,3,176]{3,0,2,1:T(8,128)S(1)} %convolution_bitcast_fusion.2), kind=kOutput, calls=%fused_computation.3 | convolution fusion | flops 277420032 | bytes 3149824 | tf_op jit(solution)/shard_map/secf,efd->secd/dot_general | solution.py:59
  89.9 1.7 %copy.83 = bf16[64,1,3,2048]{3,2,1,0:T(4,128)(2,1)} copy(bf16[64,1,3,2048]{3,0,2,1:T(8,128)(2,1)S(1)} %fusion.1) | data formatting | bytes 1572864 | tf_op jit(solution)/shard_map/convert_element_type | solution.py:114
  91.6 6.4 %all-to-all-start.3 = ((bf16[64,1,3,2048]{3,2,1,0:T(4,128)(2,1)}), bf16[64,1,3,2048]{3,2,1,0:T(4,128)(2,1)S(1)}, u32[]{:S(2)}, u32[]{:S(2)}) async-start(bf16[64,1,3,2048]{3,2,1,0:T(4,128)(2,1)} %copy.83), calls=%async_computation.3 | async-start | bytes 2097152 | tf_op jit(solution)/shard_map/all_to_all | solution.py:113
  98.0 0.1 select_reduce_fusion
  98.2 28.3 %all-to-all-done.3 = bf16[64,1,3,2048]{3,2,1,0:T(4,128)(2,1)S(1)} async-done(((bf16[64,1,3,2048]{3,2,1,0:T(4,128)(2,1)}), bf16[64,1,3,2048]{3,2,1,0:T(4,128)(2,1)S(1)}, u32[]{:S(2)}, u32[]{:S(2)}) %all-to-all-start.3) | async-done | bytes 786464 | tf_op jit(solution)/shard_map/all_to_all | solution.py:113
  126.4 0.7 reshape.136
  127.1 0.4 convolution_convert_fusion.2
  127.6 10.1 %all_to_all.26 = bf16[8,20,256]{2,1,0:T(8,128)(2,1)S(1)} all-to-all(bf16[8,20,256]{2,1,0:T(8,128)(2,1)S(1)} %bitcast.99), channel_id=1, replica_groups=mesh['req'=64,'tp'=8] {'tp'}, dimensions={0} | all-to-all | bytes 163840 | tf_op jit(solution)/shard_map/all_to_all | solution.py:65
  137.7 0.6 add_convert_fusion
  (48 shorter events, 0.9 us)
Async XLA Ops:
  0.0 87.5 %copy-start = (bf16[1,176,2048]{2,1,0:T(8,128)(2,1)S(1)}, bf16[1,176,2048]{2,1,0:T(8,128)(2,1)}, u32[]{:S(2)}) copy-start(bf16[1,176,2048]{2,1,0:T(8,128)(2,1)} %param.27) | copy-start | bytes 2162692
  2.3 1.2 copy-start.5
  2.3 1.2 copy-start.2
  3.9 1.2 copy-start.9
  3.9 1.3 copy-start.6
  5.1 1.9 %copy-start.3 = (bf16[4,384,2,128]{3,1,2,0:T(8,128)(2,1)S(1)}, bf16[4,384,2,128]{3,1,2,0:T(8,128)(2,1)}, u32[]{:S(2)}) copy-start(bf16[4,384,2,128]{3,1,2,0:T(8,128)(2,1)} %copy.70) | copy-start | bytes 2359300
  7.0 1.9 %copy-start.1 = (bf16[256,2048]{1,0:T(8,128)(2,1)S(1)}, bf16[256,2048]{1,0:T(8,128)(2,1)}, u32[]{:S(2)}) copy-start(bf16[256,2048]{1,0:T(8,128)(2,1)} %param.21) | copy-start | bytes 3145732
  9.4 7.9 %copy-start.4 = (s32[20,6]{0,1:T(8,128)S(1)}, s32[20,6]{0,1:T(8,128)}, u32[]{:S(2)}) copy-start(s32[20,6]{0,1:T(8,128)} %param.23) | copy-start | bytes 1444
  10.5 15.8 %all-to-all-start = ((f32[8,20,256]{2,1,0:T(8,128)}), f32[8,20,256]{2,1,0:T(8,128)S(1)}, u32[]{:S(2)}, u32[]{:S(2)}) async-start(f32[8,20,256]{2,1,0:T(8,128)} %convolution_bitcast_fusion), calls=%async_computation | async-start | bytes 393216 | tf_op jit(solution)/shard_map/all_to_all | solution.py:65
  26.3 13.7 %copy-start.7 = (f32[2048]{0:T(1024)S(1)}, f32[2048]{0:T(1024)}, u32[]{:S(2)}) copy-start(f32[2048]{0:T(1024)} %param.22) | copy-start | bytes 24580
  27.8 12.0 %all-to-all-start.1 = ((f32[8,20,256]{2,1,0:T(8,128)}), f32[8,20,256]{2,1,0:T(8,128)S(1)}, u32[]{:S(2)}, u32[]{:S(2)}) async-start(f32[8,20,256]{2,1,0:T(8,128)} %broadcast_in_dim.74), calls=%async_computation.1 | async-start | bytes 393216 | tf_op jit(solution)/shard_map/all_to_all | solution.py:72
  41.0 45.6 %copy-start.10 = (bf16[1,2048,176]{1,2,0:T(8,128)(2,1)S(1)}, bf16[1,2048,176]{1,2,0:T(8,128)(2,1)}, u32[]{:S(2)}) copy-start(bf16[1,2048,176]{1,2,0:T(8,128)(2,1)} %param.25) | copy-start | bytes 2162692
  91.6 6.5 %copy-start.8 = (f32[20,6]{0,1:T(8,128)S(1)}, f32[20,6]{0,1:T(8,128)}, u32[]{:S(2)}) copy-start(f32[20,6]{0,1:T(8,128)} %param.24) | copy-start | bytes 1444
  91.6 34.9 %all-to-all-start.3 = ((bf16[64,1,3,2048]{3,2,1,0:T(4,128)(2,1)}), bf16[64,1,3,2048]{3,2,1,0:T(4,128)(2,1)S(1)}, u32[]{:S(2)}, u32[]{:S(2)}) async-start(bf16[64,1,3,2048]{3,2,1,0:T(4,128)(2,1)} %copy.83), calls=%async_computation.3 | async-start | bytes 2097152 | tf_op jit(solution)/shard_map/all_to_all | solution.py:113

commit v2 on v1

--- a/solution.py
+++ b/solution.py
@@ -1,6 +1,8 @@
 import jax
 import jax.numpy as jnp
 from jax import lax
+from jax.experimental import pallas as pl
+from jax.experimental.pallas import tpu as pltpu
 from jax.sharding import PartitionSpec as P
 
 HD = 128
@@ -24,32 +26,59 @@
     return (dispatch, combine)
 
 
-def attend_local(queries, new_keys, new_values, cache_keys, cache_values, cache_lengths):
-    req_count = cache_keys.shape[0]
-    head_count = queries.shape[1] // HD
-    all_keys = jnp.concatenate([cache_keys, new_keys.reshape(req_count, POS, -1)], axis=1).reshape(
-        req_count, CACHE + POS, head_count, HD
-    )
-    all_values = jnp.concatenate(
-        [cache_values, new_values.reshape(req_count, POS, -1)], axis=1
-    ).reshape(req_count, CACHE + POS, head_count, HD)
-    local_q = queries.reshape(req_count, POS, head_count, HD)
-    scores = jnp.einsum(
-        "rphd,rjhd->rhpj", local_q, all_keys, preferred_element_type=jnp.float32
-    ) * HD ** (-0.5)
-    key_pos = jnp.arange(CACHE + POS, dtype=jnp.int32)
-    query_pos = jnp.arange(POS, dtype=jnp.int32)
-    cache_live = key_pos[None, None, :] < cache_lengths[:, None, None]
-    fresh_live = key_pos[None, None, :] - CACHE <= query_pos[None, :, None]
-    live = jnp.where(key_pos[None, None, :] < CACHE, cache_live, fresh_live)
-    scores = jnp.where(live[:, None, :, :], scores, -1e30)
-    top = jnp.max(scores, axis=-1, keepdims=True)
-    expo = jnp.exp(scores - top)
-    weights = (expo / jnp.sum(expo, axis=-1, keepdims=True)).astype(jnp.bfloat16)
-    attended = jnp.einsum(
-        "rhpj,rjhd->rphd", weights, all_values, preferred_element_type=jnp.float32
-    )
-    return attended.astype(jnp.bfloat16).reshape(req_count * POS, head_count * HD)
+def attend_project(queries, new_keys, new_values, cache_keys, cache_values, cache_lengths, out_weight, tp_count):
+    req_count, cache_len, width = cache_keys.shape
+    tokens = queries.shape[0]
+    model_width = out_weight.shape[1]
+    columns = model_width // tp_count
+    head_count = width // HD
+    flat_k = cache_keys.reshape(req_count * cache_len, width)
+    flat_v = cache_values.reshape(req_count * cache_len, width)
+
+    def kernel(len_ref, q_ref, nk_ref, nv_ref, ck_ref, cv_ref, ow_ref, out_ref):
+        row = lax.broadcasted_iota(jnp.int32, (tokens, 1), 0)
+        lo = jnp.zeros((tokens, 1), jnp.int32)
+        hi = jnp.zeros((tokens, 1), jnp.int32)
+        first = jnp.zeros((tokens, 1), jnp.int32)
+        for r in range(req_count):
+            mine = (row >= r * POS) & (row < (r + 1) * POS)
+            lo = jnp.where(mine, r * cache_len, lo)
+            hi = jnp.where(mine, r * cache_len + len_ref[r], hi)
+            first = jnp.where(mine, r * POS, first)
+        key_at = lax.broadcasted_iota(jnp.int32, (tokens, req_count * cache_len), 1)
+        live_c = (key_at >= lo) & (key_at < hi)
+        fresh_at = lax.broadcasted_iota(jnp.int32, (tokens, tokens), 1)
+        live_n = (fresh_at >= first) & (fresh_at <= row)
+        dims = (((1,), (1,)), ((), ()))
+        heads = []
+        for h in range(head_count):
+            cols = slice(h * HD, (h + 1) * HD)
+            q = q_ref[:, cols]
+            sc = lax.dot_general(q, ck_ref[:, cols], dims, preferred_element_type=jnp.float32) * HD ** (-0.5)
+            sn = lax.dot_general(q, nk_ref[:, cols], dims, preferred_element_type=jnp.float32) * HD ** (-0.5)
+            sc = jnp.where(live_c, sc, -1e30)
+            sn = jnp.where(live_n, sn, -1e30)
+            top = jnp.maximum(jnp.max(sc, axis=1, keepdims=True), jnp.max(sn, axis=1, keepdims=True))
+            ec = jnp.exp(sc - top)
+            en = jnp.exp(sn - top)
+            total = jnp.sum(ec, axis=1, keepdims=True) + jnp.sum(en, axis=1, keepdims=True)
+            wc = (ec / total).astype(jnp.bfloat16)
+            wn = (en / total).astype(jnp.bfloat16)
+            att = jnp.dot(wc, cv_ref[:, cols], preferred_element_type=jnp.float32)
+            att = att + jnp.dot(wn, nv_ref[:, cols], preferred_element_type=jnp.float32)
+            heads.append(att.astype(jnp.bfloat16))
+        attended = jnp.concatenate(heads, axis=1)
+        partial = jnp.dot(attended, ow_ref[...], preferred_element_type=jnp.float32)
+        for k in range(tp_count):
+            out_ref[k] = partial[:, k * columns:(k + 1) * columns]
+
+    vmem = pl.BlockSpec(memory_space=pltpu.VMEM)
+    return pl.pallas_call(
+        kernel,
+        out_shape=jax.ShapeDtypeStruct((tp_count, tokens, columns), jnp.float32),
+        in_specs=[pl.BlockSpec(memory_space=pltpu.SMEM)] + [vmem] * 6,
+        out_specs=vmem,
+    )(cache_lengths, queries, new_keys, new_values, flat_k, flat_v, out_weight)
 
 
 def expert_apply(slot_rows, gate_weight, up_weight, down_weight):
@@ -89,16 +118,18 @@
     up_weight,
     down_weight,
 ):
-    attended = attend_local(queries, new_keys, new_values, cache_keys, cache_values, cache_lengths)
-    partial_value = jnp.dot(attended, out_weight, preferred_element_type=jnp.float32)
-    model_width = partial_value.shape[1]
+    model_width = out_weight.shape[1]
     tp_count = lax.axis_size("tp")
+    pieces = attend_project(
+        queries, new_keys, new_values, cache_keys, cache_values, cache_lengths, out_weight, tp_count
+    )
     columns = model_width // tp_count
     offset = lax.axis_index("tp") * columns
     holders = lax.axis_size("req")
     dispatch, combine = slot_tables(routes, route_gates)
     hidden_cols = lax.dynamic_slice_in_dim(hidden_in, offset, columns, 1).astype(jnp.float32)
-    summed_cols = scatter_sum(partial_value, tp_count) + hidden_cols
+    pieces = lax.all_to_all(pieces, "tp", split_axis=0, concat_axis=0, tiled=True)
+    summed_cols = jnp.sum(pieces, axis=0) + hidden_cols
     summed = gather_cols(summed_cols, tp_count)
     mean_square = jnp.mean(summed * summed, axis=-1, keepdims=True)
     normed = (summed * lax.rsqrt(mean_square + 1e-06) * norm_gain[None, :]).astype(jnp.bfloat16)

time: 140 us -> 133 us (0.950)
  local copies, waits for them, and re-layouts: 9.74 us -> 4.12 us
  matrix products: 8.88 us -> 4.2 us
  Pallas kernels: 0 us -> 3.84 us
    pallas_call x0 -> x1, Pallas kernels: none -> 3.84 us  [attend_project(): pl.pallas_call(kernel, out_shape=jax.ShapeDtypeStruct((tp_count, tokens,...]
    concatenate x6 -> x0, local copies, waits for them, and re-layouts: 3.17 us -> none  [the longest x3 1.96 us: attend_local(): jnp.concatenate([cache_values, new_values.reshape(req_count, POS, -1)], a...]
    dot_general x2 -> x0, matrix products: 2.9 us -> none  [the longest x1 1.84 us: attend_local(): jnp.einsum('rhpj,rjhd->rphd', weights, all_values, preferred_element_type...]
    unnamed x28 -> x14, local copies, waits for them, and re-layouts: 2.11 us -> 0.23 us
    sub x1 -> x0, matrix products: 1.78 us -> none  [attend_local(): expo = jnp.exp(scores - top)]
where the time goes in v2:
time: 133 us; the launch traced here: 132 us
  blocking collectives  55.6 us (42%)
  waiting for transfers between devices  44.9 us (34%)
  starting transfers between devices  16.7 us (13%)
  matrix products  4.2 us (3%)
  local copies, waits for them, and re-layouts  4.12 us (3%)
  Pallas kernels  3.84 us (3%)
  other arithmetic  2.12 us (2%)
    all_to_all x1, blocking collectives, local(): lax.all_to_all(outbound, 'req', split_axis=0, concat_axis=0, tiled=True)  45.5 us
    all_to_all x1, waiting for transfers between devices, local(): lax.all_to_all(produced.astype(jnp.bfloat16), 'req', split_axis=0, concat...  28.3 us
    all_to_all x1, blocking collectives, scatter_sum(): lax.all_to_all(pieces, 'tp', split_axis=0, concat_axis=0, tiled=True)  10.1 us
    all_to_all x1, waiting for transfers between devices, gather_cols(): lax.all_to_all(pieces, 'tp', split_axis=0, concat_axis=0, tiled=True)  8.44 us
    all_to_all x1, waiting for transfers between devices, local(): lax.all_to_all(pieces, 'tp', split_axis=0, concat_axis=0, tiled=True)  8.17 us
    all_to_all x1, starting transfers between devices, local(): lax.all_to_all(pieces, 'tp', split_axis=0, concat_axis=0, tiled=True)  6.82 us
    all_to_all x1, starting transfers between devices, local(): lax.all_to_all(produced.astype(jnp.bfloat16), 'req', split_axis=0, concat...  6.45 us
    pallas_call x1, Pallas kernels, attend_project(): pl.pallas_call(kernel, out_shape=jax.ShapeDtypeStruct((tp_count, tokens,...  3.84 us
  transfers between devices with their start and end apart: 3, of which 3 were waited for; matrix products, arithmetic and copies ran while one was open for 1% of the time, Pallas kernels for 0%

profile of v2, /device:TPU:7, one launch (start us, length us, event | category | flops | bytes accessed | tf_op | source)
XLA Modules:
  0.0 131.7 jit_solution(10607551015131031468)
XLA Ops:
  0.0 3.8 %shard_map.136 = f32[8,20,256]{2,1,0:T(8,128)} custom-call(s32[4]{0:T(128)} %len_ref.1, bf16[20,256]{1,0:T(8,128)(2,1)} %q_ref.1, bf16[20,256]{1,0:T(8,128)(2,1)} %nk_ref.1, bf16[20,256]{1,0:T(8,128)(2,1)} %nv_ref.1, bf16[1536,256]{1,0:T(8,128)(2,1)} %bitcast.72, bf16[1536,256]{1,0:T(8,128)(2,1)} %bitcast.73, bf16[256,2048]{1,0:T(8,128)(2,1)} %ow_ref.1), custom_call_target="tpu_custom_call" | custom-call | tf_op jit(solution)/shard_map/pallas_call | solution.py:76
  3.8 6.8 %all-to-all-start = ((f32[8,20,256]{2,1,0:T(8,128)}), f32[8,20,256]{2,1,0:T(8,128)S(1)}, u32[]{:S(2)}, u32[]{:S(2)}) async-start(f32[8,20,256]{2,1,0:T(8,128)} %shard_map.136), calls=%async_computation | async-start | bytes 393216 | tf_op jit(solution)/shard_map/all_to_all | solution.py:131
  10.7 0.1 copy.40
  10.8 0.1 eq.28
  10.9 0.1 fusion.25
  11.0 0.2 reduce_window_sum.11
  11.1 0.2 select_reduce_fusion.1
  11.3 0.1 reduce_sum.49
  11.4 0.1 copy.41
  11.5 8.2 %all-to-all-done = f32[8,20,256]{2,1,0:T(8,128)S(1)} async-done(((f32[8,20,256]{2,1,0:T(8,128)}), f32[8,20,256]{2,1,0:T(8,128)S(1)}, u32[]{:S(2)}, u32[]{:S(2)}) %all-to-all-start) | async-done | bytes 163872 | tf_op jit(solution)/shard_map/all_to_all | solution.py:131
  19.7 0.0 copy-start.2
  19.7 0.7 convert_add_fusion
  20.4 0.7 broadcast_in_dim.16
  21.1 3.4 %all-to-all-start.1 = ((f32[8,20,256]{2,1,0:T(8,128)}), f32[8,20,256]{2,1,0:T(8,128)S(1)}, u32[]{:S(2)}, u32[]{:S(2)}) async-start(f32[8,20,256]{2,1,0:T(8,128)} %broadcast_in_dim.16), calls=%async_computation.1 | async-start | bytes 393216 | tf_op jit(solution)/shard_map/all_to_all | solution.py:101
  24.5 0.1 fusion.21
  24.6 8.4 %all-to-all-done.1 = f32[8,20,256]{2,1,0:T(8,128)S(1)} async-done(((f32[8,20,256]{2,1,0:T(8,128)}), f32[8,20,256]{2,1,0:T(8,128)S(1)}, u32[]{:S(2)}, u32[]{:S(2)}) %all-to-all-start.1) | async-done | bytes 163872 | tf_op jit(solution)/shard_map/all_to_all | solution.py:101
  33.1 0.1 copy.42
  33.1 0.1 copy.47
  33.2 0.1 multiply_reduce_fusion
  33.4 0.4 convolution_convert_fusion.1
  33.8 0.5 reshape.60
  34.3 45.5 %all_to_all.25 = bf16[64,1,3,2048]{3,2,1,0:T(4,128)(2,1)S(1)} all-to-all(bf16[64,1,3,2048]{3,2,1,0:T(4,128)(2,1)S(1)} %bitcast.68), channel_id=1, replica_groups=mesh['req'=64,'tp'=8] {'req'}, dimensions={0} | all-to-all | bytes 1572864 | tf_op jit(solution)/shard_map/all_to_all | solution.py:139
  79.9 1.0 convolution_bitcast_fusion.1
  80.9 2.3 %fusion = bf16[64,1,3,2048]{3,0,2,1:T(8,128)(2,1)S(1)} fusion(bf16[1,176,2048]{2,1,0:T(8,128)(2,1)S(1)} %copy-done, bf16[1,2048,176]{1,2,0:T(8,128)(2,1)} %param.26, bf16[64,1,3,2048]{3,2,1,0:T(4,128)(2,1)S(1)} %all_to_all.25, f32[64,1,3,176]{3,0,2,1:T(8,128)S(1)} %convolution_bitcast_fusion.1), kind=kOutput, calls=%fused_computation.2 | convolution fusion | flops 277420032 | bytes 3149824 | tf_op jit(solution)/shard_map/secf,efd->secd/dot_general | solution.py:88
  83.2 1.7 %copy.45 = bf16[64,1,3,2048]{3,2,1,0:T(4,128)(2,1)} copy(bf16[64,1,3,2048]{3,0,2,1:T(8,128)(2,1)S(1)} %fusion) | data formatting | bytes 1572864 | tf_op jit(solution)/shard_map/convert_element_type | solution.py:145
  84.9 6.4 %all-to-all-start.3 = ((bf16[64,1,3,2048]{3,2,1,0:T(4,128)(2,1)}), bf16[64,1,3,2048]{3,2,1,0:T(4,128)(2,1)S(1)}, u32[]{:S(2)}, u32[]{:S(2)}) async-start(bf16[64,1,3,2048]{3,2,1,0:T(4,128)(2,1)} %copy.45), calls=%async_computation.3 | async-start | bytes 2097152 | tf_op jit(solution)/shard_map/all_to_all | solution.py:144
  91.4 0.1 select_reduce_fusion
  91.5 28.3 %all-to-all-done.3 = bf16[64,1,3,2048]{3,2,1,0:T(4,128)(2,1)S(1)} async-done(((bf16[64,1,3,2048]{3,2,1,0:T(4,128)(2,1)}), bf16[64,1,3,2048]{3,2,1,0:T(4,128)(2,1)S(1)}, u32[]{:S(2)}, u32[]{:S(2)}) %all-to-all-start.3) | async-done | bytes 786464 | tf_op jit(solution)/shard_map/all_to_all | solution.py:144
  119.8 0.7 reshape.66
  120.5 0.4 convolution_convert_fusion.2
  121.0 10.1 %all_to_all.26 = bf16[8,20,256]{2,1,0:T(8,128)(2,1)S(1)} all-to-all(bf16[8,20,256]{2,1,0:T(8,128)(2,1)S(1)} %bitcast.75), channel_id=1, replica_groups=mesh['req'=64,'tp'=8] {'tp'}, dimensions={0} | all-to-all | bytes 163840 | tf_op jit(solution)/shard_map/all_to_all | solution.py:94
  131.1 0.6 add_convert_fusion
  (17 shorter events, 0.1 us)
Async XLA Ops:
  0.0 80.9 %copy-start = (bf16[1,176,2048]{2,1,0:T(8,128)(2,1)S(1)}, bf16[1,176,2048]{2,1,0:T(8,128)(2,1)}, u32[]{:S(2)}) copy-start(bf16[1,176,2048]{2,1,0:T(8,128)(2,1)} %param.27) | copy-start | bytes 2162692
  0.0 10.7 %copy-start.1 = (s32[20,6]{0,1:T(8,128)S(1)}, s32[20,6]{0,1:T(8,128)}, u32[]{:S(2)}) copy-start(s32[20,6]{0,1:T(8,128)} %param.23) | copy-start | bytes 1444
  3.8 15.8 %all-to-all-start = ((f32[8,20,256]{2,1,0:T(8,128)}), f32[8,20,256]{2,1,0:T(8,128)S(1)}, u32[]{:S(2)}, u32[]{:S(2)}) async-start(f32[8,20,256]{2,1,0:T(8,128)} %shard_map.136), calls=%async_computation | async-start | bytes 393216 | tf_op jit(solution)/shard_map/all_to_all | solution.py:131
  19.7 13.7 %copy-start.2 = (f32[2048]{0:T(1024)S(1)}, f32[2048]{0:T(1024)}, u32[]{:S(2)}) copy-start(f32[2048]{0:T(1024)} %param.22) | copy-start | bytes 24580
  21.1 12.0 %all-to-all-start.1 = ((f32[8,20,256]{2,1,0:T(8,128)}), f32[8,20,256]{2,1,0:T(8,128)S(1)}, u32[]{:S(2)}, u32[]{:S(2)}) async-start(f32[8,20,256]{2,1,0:T(8,128)} %broadcast_in_dim.16), calls=%async_computation.1 | async-start | bytes 393216 | tf_op jit(solution)/shard_map/all_to_all | solution.py:101
  34.3 45.6 %copy-start.4 = (bf16[1,2048,176]{1,2,0:T(8,128)(2,1)S(1)}, bf16[1,2048,176]{1,2,0:T(8,128)(2,1)}, u32[]{:S(2)}) copy-start(bf16[1,2048,176]{1,2,0:T(8,128)(2,1)} %param.25) | copy-start | bytes 2162692
  84.9 6.5 %copy-start.3 = (f32[20,6]{0,1:T(8,128)S(1)}, f32[20,6]{0,1:T(8,128)}, u32[]{:S(2)}) copy-start(f32[20,6]{0,1:T(8,128)} %param.24) | copy-start | bytes 1444
  84.9 34.9 %all-to-all-start.3 = ((bf16[64,1,3,2048]{3,2,1,0:T(4,128)(2,1)}), bf16[64,1,3,2048]{3,2,1,0:T(4,128)(2,1)S(1)}, u32[]{:S(2)}, u32[]{:S(2)}) async-start(bf16[64,1,3,2048]{3,2,1,0:T(4,128)(2,1)} %copy.45), calls=%async_computation.3 | async-start | bytes 2097152 | tf_op jit(solution)/shard_map/all_to_all | solution.py:144

commit v3 on v2

--- a/solution.py
+++ b/solution.py
@@ -134,15 +134,17 @@
     mean_square = jnp.mean(summed * summed, axis=-1, keepdims=True)
     normed = (summed * lax.rsqrt(mean_square + 1e-06) * norm_gain[None, :]).astype(jnp.bfloat16)
     outbound = jnp.dot(dispatch, normed, preferred_element_type=jnp.float32).astype(jnp.bfloat16)
-    outbound = outbound.reshape(holders, -1, CAP, model_width)
+    packed = (holders, CAP * model_width // 128, 128)
+    outbound = outbound.reshape(packed)
+    arrived = lax.all_to_all(outbound, "req", split_axis=0, concat_axis=0, tiled=True)
     produced = expert_apply(
-        lax.all_to_all(outbound, "req", split_axis=0, concat_axis=0, tiled=True),
+        arrived.reshape(holders, 1, CAP, model_width),
         gate_weight,
         up_weight,
         down_weight,
     )
     returned = lax.all_to_all(
-        produced.astype(jnp.bfloat16), "req", split_axis=0, concat_axis=0, tiled=True
+        produced.astype(jnp.bfloat16).reshape(packed), "req", split_axis=0, concat_axis=0, tiled=True
     ).astype(produced.dtype)
     expert_sum = jnp.dot(
         combine,

time: 133 us -> 123 us (0.925)
  waiting for transfers between devices: 44.9 us -> 39.3 us
  blocking collectives: 55.6 us -> 51 us
    all_to_all x1, blocking collectives: 45.5 us -> 39.8 us  [local(): lax.all_to_all(outbound, 'req', split_axis=0, concat_axis=0, tiled=True)]
    all_to_all x1, waiting for transfers between devices: 28.3 us -> 22.7 us  [local(): lax.all_to_all(produced.astype(jnp.bfloat16).reshape(packed), 'req', spli...]
    reshape x1 -> x2, local copies, waits for them, and re-layouts: 0.5 us -> 2.04 us  [the longest x1 1.68 us: local(): produced.astype(jnp.bfloat16).reshape(packed)]
where the time goes in v3:
time: 123 us
  blocking collectives  51 us (41%)
  waiting for transfers between devices  39.3 us (32%)
  starting transfers between devices  16.7 us (14%)
  local copies, waits for them, and re-layouts  5.41 us (4%)
  matrix products  4.2 us (3%)
  Pallas kernels  3.84 us (3%)
  other arithmetic  2.12 us (2%)
    all_to_all x1, blocking collectives, local(): lax.all_to_all(outbound, 'req', split_axis=0, concat_axis=0, tiled=True)  39.8 us
    all_to_all x1, waiting for transfers between devices, local(): lax.all_to_all(produced.astype(jnp.bfloat16).reshape(packed), 'req', spli...  22.7 us
    all_to_all x1, blocking collectives, scatter_sum(): lax.all_to_all(pieces, 'tp', split_axis=0, concat_axis=0, tiled=True)  11.3 us
    all_to_all x1, waiting for transfers between devices, gather_cols(): lax.all_to_all(pieces, 'tp', split_axis=0, concat_axis=0, tiled=True)  8.44 us
    all_to_all x1, waiting for transfers between devices, local(): lax.all_to_all(pieces, 'tp', split_axis=0, concat_axis=0, tiled=True)  8.17 us
    all_to_all x1, starting transfers between devices, local(): lax.all_to_all(pieces, 'tp', split_axis=0, concat_axis=0, tiled=True)  6.82 us
    all_to_all x1, starting transfers between devices, local(): lax.all_to_all(produced.astype(jnp.bfloat16).reshape(packed), 'req', spli...  6.49 us
    pallas_call x1, Pallas kernels, attend_project(): pl.pallas_call(kernel, out_shape=jax.ShapeDtypeStruct((tp_count, tokens,...  3.84 us
  transfers between devices with their start and end apart: 3, of which 3 were waited for; matrix products, arithmetic and copies ran while one was open for 1% of the time, Pallas kernels for 0%

profile of v3, /device:TPU:7, one launch (start us, length us, event | category | flops | bytes accessed | tf_op | source)
XLA Modules:
  0.0 122.8 jit_solution(6620680601550795111)
XLA Ops:
  0.0 3.8 %shard_map.136 = f32[8,20,256]{2,1,0:T(8,128)} custom-call(s32[4]{0:T(128)} %len_ref.1, bf16[20,256]{1,0:T(8,128)(2,1)} %q_ref.1, bf16[20,256]{1,0:T(8,128)(2,1)} %nk_ref.1, bf16[20,256]{1,0:T(8,128)(2,1)} %nv_ref.1, bf16[1536,256]{1,0:T(8,128)(2,1)} %bitcast.65, bf16[1536,256]{1,0:T(8,128)(2,1)} %bitcast.66, bf16[256,2048]{1,0:T(8,128)(2,1)} %ow_ref.1), custom_call_target="tpu_custom_call" | custom-call | tf_op jit(solution)/shard_map/pallas_call | solution.py:76
  3.8 6.8 %all-to-all-start = ((f32[8,20,256]{2,1,0:T(8,128)}), f32[8,20,256]{2,1,0:T(8,128)S(1)}, u32[]{:S(2)}, u32[]{:S(2)}) async-start(f32[8,20,256]{2,1,0:T(8,128)} %shard_map.136), calls=%async_computation | async-start | bytes 393216 | tf_op jit(solution)/shard_map/all_to_all | solution.py:131
  10.7 0.1 copy.40
  10.8 0.1 eq.28
  10.9 0.1 fusion.21
  11.0 0.2 reduce_window_sum.11
  11.1 0.2 select_reduce_fusion.1
  11.3 0.1 reduce_sum.49
  11.4 0.1 copy.41
  11.5 8.2 %all-to-all-done = f32[8,20,256]{2,1,0:T(8,128)S(1)} async-done(((f32[8,20,256]{2,1,0:T(8,128)}), f32[8,20,256]{2,1,0:T(8,128)S(1)}, u32[]{:S(2)}, u32[]{:S(2)}) %all-to-all-start) | async-done | bytes 163872 | tf_op jit(solution)/shard_map/all_to_all | solution.py:131
  19.7 0.7 convert_add_fusion
  20.4 0.7 broadcast_in_dim.16
  21.1 3.4 %all-to-all-start.1 = ((f32[8,20,256]{2,1,0:T(8,128)}), f32[8,20,256]{2,1,0:T(8,128)S(1)}, u32[]{:S(2)}, u32[]{:S(2)}) async-start(f32[8,20,256]{2,1,0:T(8,128)} %broadcast_in_dim.16), calls=%async_computation.1 | async-start | bytes 393216 | tf_op jit(solution)/shard_map/all_to_all | solution.py:101
  24.5 0.1 fusion.17
  24.6 8.4 %all-to-all-done.1 = f32[8,20,256]{2,1,0:T(8,128)S(1)} async-done(((f32[8,20,256]{2,1,0:T(8,128)}), f32[8,20,256]{2,1,0:T(8,128)S(1)}, u32[]{:S(2)}, u32[]{:S(2)}) %all-to-all-start.1) | async-done | bytes 163872 | tf_op jit(solution)/shard_map/all_to_all | solution.py:101
  33.2 0.1 multiply_reduce_fusion
  33.4 0.4 convolution_convert_fusion.1
  33.8 0.4 reshape.66
  34.2 39.8 %all_to_all.25 = bf16[64,48,128]{2,1,0:T(8,128)(2,1)S(1)} all-to-all(bf16[64,48,128]{2,1,0:T(8,128)(2,1)S(1)} %reshape.66), channel_id=1, replica_groups=mesh['req'=64,'tp'=8] {'req'}, dimensions={0} | all-to-all | bytes 1572864 | tf_op jit(solution)/shard_map/all_to_all | solution.py:139
  74.0 0.2 reshape.67
  74.2 0.9 copy-done.4
  75.1 1.0 convolution_bitcast_fusion.1
  76.1 2.3 %fusion = bf16[64,1,3,2048]{3,0,2,1:T(8,128)(2,1)S(1)} fusion(bf16[1,176,2048]{2,1,0:T(8,128)(2,1)S(1)} %copy-done, bf16[1,2048,176]{1,2,0:T(8,128)(2,1)} %param.26, bf16[64,3,2048]{2,1,0:T(4,128)(2,1)S(1)} %reshape.67, f32[64,1,3,176]{3,0,2,1:T(8,128)S(1)} %convolution_bitcast_fusion.1), kind=kOutput, calls=%fused_computation.2 | convolution fusion | flops 277420032 | bytes 3149824 | tf_op jit(solution)/shard_map/secf,efd->secd/dot_general | solution.py:88
  78.4 0.7 copy.45
  79.1 1.7 %reshape.72 = bf16[64,48,128]{2,1,0:T(8,128)(2,1)} reshape(bf16[64,1,3,2048]{3,2,0,1:T(4,128)(2,1)S(1)} %copy.45) | data formatting | bytes 1572864 | tf_op jit(solution)/shard_map/reshape | solution.py:147
  80.8 6.5 %all-to-all-start.3 = ((bf16[64,48,128]{2,1,0:T(8,128)(2,1)}), bf16[64,48,128]{2,1,0:T(8,128)(2,1)S(1)}, u32[]{:S(2)}, u32[]{:S(2)}) async-start(bf16[64,48,128]{2,1,0:T(8,128)(2,1)} %reshape.72), calls=%async_computation.3 | async-start | bytes 1572864 | tf_op jit(solution)/shard_map/all_to_all | solution.py:146
  87.3 0.1 select_reduce_fusion
  87.4 22.7 %all-to-all-done.3 = bf16[64,48,128]{2,1,0:T(8,128)(2,1)S(1)} async-done(((bf16[64,48,128]{2,1,0:T(8,128)(2,1)}), bf16[64,48,128]{2,1,0:T(8,128)(2,1)S(1)}, u32[]{:S(2)}, u32[]{:S(2)}) %all-to-all-start.3) | async-done | bytes 786464 | tf_op jit(solution)/shard_map/all_to_all | solution.py:146
  110.1 0.3 reshape.73
  110.4 0.4 convolution_convert_fusion.2
  110.9 11.3 %all_to_all.26 = bf16[8,20,256]{2,1,0:T(8,128)(2,1)S(1)} all-to-all(bf16[8,20,256]{2,1,0:T(8,128)(2,1)S(1)} %bitcast.68), channel_id=1, replica_groups=mesh['req'=64,'tp'=8] {'tp'}, dimensions={0} | all-to-all | bytes 163840 | tf_op jit(solution)/shard_map/all_to_all | solution.py:94
  122.2 0.6 add_convert_fusion
  (19 shorter events, 0.3 us)
Async XLA Ops:
  0.0 76.1 %copy-start = (bf16[1,176,2048]{2,1,0:T(8,128)(2,1)S(1)}, bf16[1,176,2048]{2,1,0:T(8,128)(2,1)}, u32[]{:S(2)}) copy-start(bf16[1,176,2048]{2,1,0:T(8,128)(2,1)} %param.27) | copy-start | bytes 2162692
  0.0 10.7 %copy-start.1 = (s32[20,6]{0,1:T(8,128)S(1)}, s32[20,6]{0,1:T(8,128)}, u32[]{:S(2)}) copy-start(s32[20,6]{0,1:T(8,128)} %param.23) | copy-start | bytes 1444
  3.8 15.8 %all-to-all-start = ((f32[8,20,256]{2,1,0:T(8,128)}), f32[8,20,256]{2,1,0:T(8,128)S(1)}, u32[]{:S(2)}, u32[]{:S(2)}) async-start(f32[8,20,256]{2,1,0:T(8,128)} %shard_map.136), calls=%async_computation | async-start | bytes 393216 | tf_op jit(solution)/shard_map/all_to_all | solution.py:131
  19.7 13.7 %copy-start.2 = (f32[2048]{0:T(1024)S(1)}, f32[2048]{0:T(1024)}, u32[]{:S(2)}) copy-start(f32[2048]{0:T(1024)} %param.22) | copy-start | bytes 24580
  21.1 12.0 %all-to-all-start.1 = ((f32[8,20,256]{2,1,0:T(8,128)}), f32[8,20,256]{2,1,0:T(8,128)S(1)}, u32[]{:S(2)}, u32[]{:S(2)}) async-start(f32[8,20,256]{2,1,0:T(8,128)} %broadcast_in_dim.16), calls=%async_computation.1 | async-start | bytes 393216 | tf_op jit(solution)/shard_map/all_to_all | solution.py:101
  73.9 1.1 copy-start.4
  80.8 6.5 %copy-start.3 = (f32[20,6]{0,1:T(8,128)S(1)}, f32[20,6]{0,1:T(8,128)}, u32[]{:S(2)}) copy-start(f32[20,6]{0,1:T(8,128)} %param.24) | copy-start | bytes 1444
  80.8 29.3 %all-to-all-start.3 = ((bf16[64,48,128]{2,1,0:T(8,128)(2,1)}), bf16[64,48,128]{2,1,0:T(8,128)(2,1)S(1)}, u32[]{:S(2)}, u32[]{:S(2)}) async-start(bf16[64,48,128]{2,1,0:T(8,128)(2,1)} %reshape.72), calls=%async_computation.3 | async-start | bytes 1572864 | tf_op jit(solution)/shard_map/all_to_all | solution.py:146

commit v4 on v3

--- a/solution.py
+++ b/solution.py
@@ -69,13 +69,15 @@
             heads.append(att.astype(jnp.bfloat16))
         attended = jnp.concatenate(heads, axis=1)
         partial = jnp.dot(attended, ow_ref[...], preferred_element_type=jnp.float32)
+        half = columns // 2
         for k in range(tp_count):
-            out_ref[k] = partial[:, k * columns:(k + 1) * columns]
+            out_ref[k, 0:tokens, :] = partial[:, k * columns:k * columns + half]
+            out_ref[k, tokens:2 * tokens, :] = partial[:, k * columns + half:(k + 1) * columns]
 
     vmem = pl.BlockSpec(memory_space=pltpu.VMEM)
     return pl.pallas_call(
         kernel,
-        out_shape=jax.ShapeDtypeStruct((tp_count, tokens, columns), jnp.float32),
+        out_shape=jax.ShapeDtypeStruct((tp_count, 2 * tokens, columns // 2), jnp.float32),
         in_specs=[pl.BlockSpec(memory_space=pltpu.SMEM)] + [vmem] * 6,
         out_specs=vmem,
     )(cache_lengths, queries, new_keys, new_values, flat_k, flat_v, out_weight)
@@ -88,18 +90,31 @@
     return jnp.einsum("secf,efd->secd", activation, down_weight, preferred_element_type=jnp.float32)
 
 
+def stack_halves(value):
+    half = value.shape[1] // 2
+    return jnp.concatenate([value[:, :half], value[:, half:]], axis=0)
+
+
+def unstack_halves(value):
+    rows = value.shape[0] // 2
+    return jnp.concatenate([value[:rows], value[rows:]], axis=1)
+
+
 def scatter_sum(value, tp_count):
     rows, width = value.shape
-    pieces = value.reshape(rows, tp_count, width // tp_count).transpose(1, 0, 2)
+    pieces = value.reshape(rows, tp_count, 2, width // tp_count // 2).transpose(1, 2, 0, 3)
+    pieces = pieces.reshape(tp_count, 2 * rows, width // tp_count // 2)
     pieces = lax.all_to_all(pieces, "tp", split_axis=0, concat_axis=0, tiled=True)
-    return jnp.sum(pieces.astype(jnp.float32), axis=0)
+    return unstack_halves(jnp.sum(pieces.astype(jnp.float32), axis=0))
 
 
 def gather_cols(value, tp_count):
     rows, columns = value.shape
-    pieces = jnp.broadcast_to(value[None], (tp_count, rows, columns))
+    stacked = stack_halves(value)
+    pieces = jnp.broadcast_to(stacked[None], (tp_count,) + stacked.shape)
     pieces = lax.all_to_all(pieces, "tp", split_axis=0, concat_axis=0, tiled=True)
-    return pieces.transpose(1, 0, 2).reshape(rows, tp_count * columns)
+    pieces = pieces.reshape(tp_count, 2, rows, columns // 2).transpose(2, 0, 1, 3)
+    return pieces.reshape(rows, tp_count * columns)
 
 
 def local(
@@ -129,7 +144,7 @@
     dispatch, combine = slot_tables(routes, route_gates)
     hidden_cols = lax.dynamic_slice_in_dim(hidden_in, offset, columns, 1).astype(jnp.float32)
     pieces = lax.all_to_all(pieces, "tp", split_axis=0, concat_axis=0, tiled=True)
-    summed_cols = jnp.sum(pieces, axis=0) + hidden_cols
+    summed_cols = unstack_halves(jnp.sum(pieces, axis=0)) + hidden_cols
     summed = gather_cols(summed_cols, tp_count)
     mean_square = jnp.mean(summed * summed, axis=-1, keepdims=True)
     normed = (summed * lax.rsqrt(mean_square + 1e-06) * norm_gain[None, :]).astype(jnp.bfloat16)

time: 123 us -> 122 us (level)
  no operation moved by 1% of the time
where the time goes in v4:
time: 122 us
  blocking collectives  50.7 us (42%)
  waiting for transfers between devices  38.2 us (31%)
  starting transfers between devices  16.7 us (14%)
  local copies, waits for them, and re-layouts  5.59 us (5%)
  matrix products  4.22 us (3%)
  Pallas kernels  3.82 us (3%)
  other arithmetic  2.23 us (2%)
    all_to_all x1, blocking collectives, local(): lax.all_to_all(outbound, 'req', split_axis=0, concat_axis=0, tiled=True)  39.8 us
    all_to_all x1, waiting for transfers between devices, local(): lax.all_to_all(produced.astype(jnp.bfloat16).reshape(packed), 'req', spli...  22.7 us
    all_to_all x1, blocking collectives, scatter_sum(): lax.all_to_all(pieces, 'tp', split_axis=0, concat_axis=0, tiled=True)  10.9 us
    all_to_all x1, waiting for transfers between devices, gather_cols(): lax.all_to_all(pieces, 'tp', split_axis=0, concat_axis=0, tiled=True)  8.18 us
    all_to_all x1, waiting for transfers between devices, local(): lax.all_to_all(pieces, 'tp', split_axis=0, concat_axis=0, tiled=True)  7.39 us
    all_to_all x1, starting transfers between devices, local(): lax.all_to_all(pieces, 'tp', split_axis=0, concat_axis=0, tiled=True)  6.82 us
    all_to_all x1, starting transfers between devices, local(): lax.all_to_all(produced.astype(jnp.bfloat16).reshape(packed), 'req', spli...  6.49 us
    pallas_call x1, Pallas kernels, attend_project(): pl.pallas_call(kernel, out_shape=jax.ShapeDtypeStruct((tp_count, 2 * toke...  3.82 us
  transfers between devices with their start and end apart: 3, of which 3 were waited for; matrix products, arithmetic and copies ran while one was open for 1% of the time, Pallas kernels for 0%

profile of v4, /device:TPU:7, one launch (start us, length us, event | category | flops | bytes accessed | tf_op | source)
XLA Modules:
  0.0 121.7 jit_solution(266513063527106761)
XLA Ops:
  0.0 3.8 %shard_map.136 = f32[8,40,128]{2,1,0:T(8,128)} custom-call(s32[4]{0:T(128)} %len_ref.1, bf16[20,256]{1,0:T(8,128)(2,1)} %q_ref.1, bf16[20,256]{1,0:T(8,128)(2,1)} %nk_ref.1, bf16[20,256]{1,0:T(8,128)(2,1)} %nv_ref.1, bf16[1536,256]{1,0:T(8,128)(2,1)} %bitcast.59, bf16[1536,256]{1,0:T(8,128)(2,1)} %bitcast.60, bf16[256,2048]{1,0:T(8,128)(2,1)} %ow_ref.1), custom_call_target="tpu_custom_call" | custom-call | tf_op jit(solution)/shard_map/pallas_call | solution.py:78
  3.8 6.8 %all-to-all-start = ((f32[8,40,128]{2,1,0:T(8,128)}), f32[8,40,128]{2,1,0:T(8,128)S(1)}, u32[]{:S(2)}, u32[]{:S(2)}) async-start(f32[8,40,128]{2,1,0:T(8,128)} %shard_map.136), calls=%async_computation | async-start | bytes 327680 | tf_op jit(solution)/shard_map/all_to_all | solution.py:146
  10.7 0.1 copy.46
  10.8 0.1 eq.28
  10.9 0.2 reduce_window_sum.11
  11.1 0.2 select_reduce_fusion.1
  11.3 0.1 reduce_sum.49
  11.4 0.1 copy.47
  11.5 7.4 %all-to-all-done = f32[8,40,128]{2,1,0:T(8,128)S(1)} async-done(((f32[8,40,128]{2,1,0:T(8,128)}), f32[8,40,128]{2,1,0:T(8,128)S(1)}, u32[]{:S(2)}, u32[]{:S(2)}) %all-to-all-start) | async-done | bytes 163872 | tf_op jit(solution)/shard_map/all_to_all | solution.py:146
  18.9 0.7 maximum_add_fusion
  19.6 0.7 broadcast_in_dim.16
  20.3 3.4 %all-to-all-start.1 = ((f32[8,40,128]{2,1,0:T(8,128)}), f32[8,40,128]{2,1,0:T(8,128)S(1)}, u32[]{:S(2)}, u32[]{:S(2)}) async-start(f32[8,40,128]{2,1,0:T(8,128)} %broadcast_in_dim.16), calls=%async_computation.1 | async-start | bytes 327680 | tf_op jit(solution)/shard_map/all_to_all | solution.py:115
  23.8 8.2 %all-to-all-done.1 = f32[8,40,128]{2,1,0:T(8,128)S(1)} async-done(((f32[8,40,128]{2,1,0:T(8,128)}), f32[8,40,128]{2,1,0:T(8,128)S(1)}, u32[]{:S(2)}, u32[]{:S(2)}) %all-to-all-start.1) | async-done | bytes 163872 | tf_op jit(solution)/shard_map/all_to_all | solution.py:115
  32.0 0.1 copy.49
  32.2 0.2 multiply_reduce_fusion
  32.4 0.1 reshape.72
  32.5 0.4 convolution_convert_fusion.1
  33.0 0.4 reshape.73
  33.3 39.8 %all_to_all.25 = bf16[64,48,128]{2,1,0:T(8,128)(2,1)S(1)} all-to-all(bf16[64,48,128]{2,1,0:T(8,128)(2,1)S(1)} %reshape.73), channel_id=1, replica_groups=mesh['req'=64,'tp'=8] {'req'}, dimensions={0} | all-to-all | bytes 1572864 | tf_op jit(solution)/shard_map/all_to_all | solution.py:154
  73.1 0.2 reshape.74
  73.4 0.9 copy-done.4
  74.2 1.0 convolution_bitcast_fusion.1
  75.3 2.4 %fusion = bf16[64,1,3,2048]{3,0,2,1:T(8,128)(2,1)S(1)} fusion(bf16[1,176,2048]{2,1,0:T(8,128)(2,1)S(1)} %copy-done, bf16[1,2048,176]{1,2,0:T(8,128)(2,1)} %param.26, bf16[64,3,2048]{2,1,0:T(4,128)(2,1)S(1)} %reshape.74, f32[64,1,3,176]{3,0,2,1:T(8,128)S(1)} %convolution_bitcast_fusion.1), kind=kOutput, calls=%fused_computation.2 | convolution fusion | flops 277420032 | bytes 3149824 | tf_op jit(solution)/shard_map/secf,efd->secd/dot_general | solution.py:90
  77.6 0.7 copy.52
  78.3 1.7 %reshape.79 = bf16[64,48,128]{2,1,0:T(8,128)(2,1)} reshape(bf16[64,1,3,2048]{3,2,0,1:T(4,128)(2,1)S(1)} %copy.52) | data formatting | bytes 1572864 | tf_op jit(solution)/shard_map/reshape | solution.py:162
  80.0 6.5 %all-to-all-start.3 = ((bf16[64,48,128]{2,1,0:T(8,128)(2,1)}), bf16[64,48,128]{2,1,0:T(8,128)(2,1)S(1)}, u32[]{:S(2)}, u32[]{:S(2)}) async-start(bf16[64,48,128]{2,1,0:T(8,128)(2,1)} %reshape.79), calls=%async_computation.3 | async-start | bytes 1572864 | tf_op jit(solution)/shard_map/all_to_all | solution.py:161
  86.5 0.1 select_reduce_fusion
  86.6 22.7 %all-to-all-done.3 = bf16[64,48,128]{2,1,0:T(8,128)(2,1)S(1)} async-done(((bf16[64,48,128]{2,1,0:T(8,128)(2,1)}), bf16[64,48,128]{2,1,0:T(8,128)(2,1)S(1)}, u32[]{:S(2)}, u32[]{:S(2)}) %all-to-all-start.3) | async-done | bytes 786464 | tf_op jit(solution)/shard_map/all_to_all | solution.py:161
  109.3 0.3 reshape.80
  109.6 0.4 convolution_convert_fusion.2
  110.1 10.9 %all_to_all.26 = bf16[8,40,128]{2,1,0:T(8,128)(2,1)S(1)} all-to-all(bf16[8,40,128]{2,1,0:T(8,128)(2,1)S(1)} %copy.54), channel_id=1, replica_groups=mesh['req'=64,'tp'=8] {'tp'}, dimensions={0} | all-to-all | bytes 163840 | tf_op jit(solution)/shard_map/all_to_all | solution.py:107
  121.1 0.6 fusion.22
  (23 shorter events, 0.4 us)
Async XLA Ops:
  0.0 75.2 %copy-start = (bf16[1,176,2048]{2,1,0:T(8,128)(2,1)S(1)}, bf16[1,176,2048]{2,1,0:T(8,128)(2,1)}, u32[]{:S(2)}) copy-start(bf16[1,176,2048]{2,1,0:T(8,128)(2,1)} %param.27) | copy-start | bytes 2162692
  0.0 10.6 %copy-start.1 = (s32[20,6]{0,1:T(8,128)S(1)}, s32[20,6]{0,1:T(8,128)}, u32[]{:S(2)}) copy-start(s32[20,6]{0,1:T(8,128)} %param.23) | copy-start | bytes 1444
  3.8 15.0 %all-to-all-start = ((f32[8,40,128]{2,1,0:T(8,128)}), f32[8,40,128]{2,1,0:T(8,128)S(1)}, u32[]{:S(2)}, u32[]{:S(2)}) async-start(f32[8,40,128]{2,1,0:T(8,128)} %shard_map.136), calls=%async_computation | async-start | bytes 327680 | tf_op jit(solution)/shard_map/all_to_all | solution.py:146
  11.5 21.1 %copy-start.2 = (f32[2048]{0:T(1024)S(1)}, f32[2048]{0:T(1024)}, u32[]{:S(2)}) copy-start(f32[2048]{0:T(1024)} %param.22) | copy-start | bytes 24580
  20.3 11.7 %all-to-all-start.1 = ((f32[8,40,128]{2,1,0:T(8,128)}), f32[8,40,128]{2,1,0:T(8,128)S(1)}, u32[]{:S(2)}, u32[]{:S(2)}) async-start(f32[8,40,128]{2,1,0:T(8,128)} %broadcast_in_dim.16), calls=%async_computation.1 | async-start | bytes 327680 | tf_op jit(solution)/shard_map/all_to_all | solution.py:115
  73.1 1.1 copy-start.4
  80.0 6.5 %copy-start.3 = (f32[20,6]{0,1:T(8,128)S(1)}, f32[20,6]{0,1:T(8,128)}, u32[]{:S(2)}) copy-start(f32[20,6]{0,1:T(8,128)} %param.24) | copy-start | bytes 1444
  80.0 29.3 %all-to-all-start.3 = ((bf16[64,48,128]{2,1,0:T(8,128)(2,1)}), bf16[64,48,128]{2,1,0:T(8,128)(2,1)S(1)}, u32[]{:S(2)}, u32[]{:S(2)}) async-start(bf16[64,48,128]{2,1,0:T(8,128)(2,1)} %reshape.79), calls=%async_computation.3 | async-start | bytes 1572864 | tf_op jit(solution)/shard_map/all_to_all | solution.py:161

commit v5 on v4

--- a/solution.py
+++ b/solution.py
@@ -84,10 +84,28 @@
 
 
 def expert_apply(slot_rows, gate_weight, up_weight, down_weight):
-    gated = jnp.einsum("secd,edf->secf", slot_rows, gate_weight, preferred_element_type=jnp.float32)
-    upward = jnp.einsum("secd,edf->secf", slot_rows, up_weight, preferred_element_type=jnp.float32)
-    activation = (jax.nn.silu(gated) * upward).astype(jnp.bfloat16)
-    return jnp.einsum("secf,efd->secd", activation, down_weight, preferred_element_type=jnp.float32)
+    slots, width = slot_rows.shape
+    hidden = gate_weight.shape[-1]
+
+    def kernel(x_ref, wg_ref, wu_ref, wd_ref, out_ref):
+        rows = x_ref[...]
+        gated = jnp.dot(rows, wg_ref[...], preferred_element_type=jnp.float32)
+        upward = jnp.dot(rows, wu_ref[...], preferred_element_type=jnp.float32)
+        activation = (gated / (1.0 + jnp.exp(-gated)) * upward).astype(jnp.bfloat16)
+        out_ref[...] = jnp.dot(activation, wd_ref[...], preferred_element_type=jnp.float32).astype(jnp.bfloat16)
+
+    vmem = pl.BlockSpec(memory_space=pltpu.VMEM)
+    return pl.pallas_call(
+        kernel,
+        out_shape=jax.ShapeDtypeStruct((slots, width), jnp.bfloat16),
+        in_specs=[vmem] * 4,
+        out_specs=vmem,
+    )(
+        slot_rows,
+        gate_weight.reshape(width, hidden),
+        up_weight.reshape(width, hidden),
+        down_weight.reshape(hidden, width),
+    )
 
 
 def stack_halves(value):
@@ -153,14 +171,11 @@
     outbound = outbound.reshape(packed)
     arrived = lax.all_to_all(outbound, "req", split_axis=0, concat_axis=0, tiled=True)
     produced = expert_apply(
-        arrived.reshape(holders, 1, CAP, model_width),
-        gate_weight,
-        up_weight,
-        down_weight,
+        arrived.reshape(holders * CAP, model_width), gate_weight, up_weight, down_weight
     )
     returned = lax.all_to_all(
-        produced.astype(jnp.bfloat16).reshape(packed), "req", split_axis=0, concat_axis=0, tiled=True
-    ).astype(produced.dtype)
+        produced.reshape(packed), "req", split_axis=0, concat_axis=0, tiled=True
+    ).astype(jnp.float32)
     expert_sum = jnp.dot(
         combine,
         returned.reshape(-1, model_width),

time: 122 us -> 124 us (1.016)
  blocking collectives: 50.7 us -> 10.9 us
  waiting for transfers between devices: 38.2 us -> 58.4 us
  starting transfers between devices: 16.7 us -> 34 us
  Pallas kernels: 3.82 us -> 7.53 us
  local copies, waits for them, and re-layouts: 5.59 us -> 9.04 us
  matrix products: 4.22 us -> 0.84 us
    all_to_all x1 -> x0, blocking collectives: 39.8 us -> none  [local(): lax.all_to_all(outbound, 'req', split_axis=0, concat_axis=0, tiled=True)]
    all_to_all x1 -> x2, waiting for transfers between devices: 22.7 us -> 42.8 us  [the longest x1 22.7 us: local(): lax.all_to_all(produced.reshape(packed), 'req', split_axis=0, concat_axis...]
    all_to_all x1 -> x2, starting transfers between devices: 6.49 us -> 23.8 us  [the longest x1 17.3 us: local(): lax.all_to_all(outbound, 'req', split_axis=0, concat_axis=0, tiled=True)]
    pallas_call x0 -> x1, Pallas kernels: none -> 3.78 us  [expert_apply(): pl.pallas_call(kernel, out_shape=jax.ShapeDtypeStruct((slots, width), jnp...]
    dot_general x2 -> x0, matrix products: 3.38 us -> none  [the longest x1 2.37 us: expert_apply(): jnp.einsum('secf,efd->secd', activation, down_weight, preferred_element_t...]
    unnamed x11 -> x13, local copies, waits for them, and re-layouts: 0.97 us -> 2.73 us
    reshape x1 -> x2, local copies, waits for them, and re-layouts: 1.68 us -> 3.37 us  [the longest x1 2.17 us: local(): produced.reshape(packed)]
  transfers between devices with their start and end apart: 3 -> 4, of which waited for: 3 -> 4; matrix products, arithmetic and copies ran while one was open for 1% -> 3% of each run, Pallas kernels for 0% -> 0%
where the time goes in v5:
time: 124 us; the launch traced here: 123 us
  waiting for transfers between devices  58.4 us (47%)
  starting transfers between devices  34 us (27%)
  blocking collectives  10.9 us (9%)
  local copies, waits for them, and re-layouts  9.04 us (7%)
  Pallas kernels  7.53 us (6%)
  other arithmetic  2.23 us (2%)
    all_to_all x1, waiting for transfers between devices, local(): lax.all_to_all(produced.reshape(packed), 'req', split_axis=0, concat_axis...  22.7 us
    all_to_all x1, waiting for transfers between devices, local(): lax.all_to_all(outbound, 'req', split_axis=0, concat_axis=0, tiled=True)  20.1 us
    all_to_all x1, starting transfers between devices, local(): lax.all_to_all(outbound, 'req', split_axis=0, concat_axis=0, tiled=True)  17.3 us
    all_to_all x1, blocking collectives, scatter_sum(): lax.all_to_all(pieces, 'tp', split_axis=0, concat_axis=0, tiled=True)  10.9 us
    all_to_all x1, waiting for transfers between devices, gather_cols(): lax.all_to_all(pieces, 'tp', split_axis=0, concat_axis=0, tiled=True)  8.18 us
    all_to_all x1, waiting for transfers between devices, local(): lax.all_to_all(pieces, 'tp', split_axis=0, concat_axis=0, tiled=True)  7.4 us
    all_to_all x1, starting transfers between devices, local(): lax.all_to_all(pieces, 'tp', split_axis=0, concat_axis=0, tiled=True)  6.82 us
    all_to_all x1, starting transfers between devices, local(): lax.all_to_all(produced.reshape(packed), 'req', split_axis=0, concat_axis...  6.5 us
  transfers between devices with their start and end apart: 4, of which 4 were waited for; matrix products, arithmetic and copies ran while one was open for 3% of the time, Pallas kernels for 0%

profile of v5, /device:TPU:7, one launch (start us, length us, event | category | flops | bytes accessed | tf_op | source)
XLA Modules:
  0.0 123.1 jit_solution(12242186985078190546)
XLA Ops:
  0.0 3.8 %shard_map.136 = f32[8,40,128]{2,1,0:T(8,128)} custom-call(s32[4]{0:T(128)} %len_ref.1, bf16[20,256]{1,0:T(8,128)(2,1)} %q_ref.1, bf16[20,256]{1,0:T(8,128)(2,1)} %nk_ref.1, bf16[20,256]{1,0:T(8,128)(2,1)} %nv_ref.1, bf16[1536,256]{1,0:T(8,128)(2,1)} %bitcast.18, bf16[1536,256]{1,0:T(8,128)(2,1)} %bitcast.19, bf16[256,2048]{1,0:T(8,128)(2,1)} %ow_ref.1), custom_call_target="tpu_custom_call" | custom-call | tf_op jit(solution)/shard_map/pallas_call | solution.py:78
  3.8 6.8 %all-to-all-start = ((f32[8,40,128]{2,1,0:T(8,128)}), f32[8,40,128]{2,1,0:T(8,128)S(1)}, u32[]{:S(2)}, u32[]{:S(2)}) async-start(f32[8,40,128]{2,1,0:T(8,128)} %shard_map.136), calls=%async_computation | async-start | bytes 327680 | tf_op jit(solution)/shard_map/all_to_all | solution.py:164
  10.6 0.1 copy.45
  10.7 0.1 eq.28
  10.9 0.2 reduce_window_sum.11
  11.0 0.2 select_reduce_fusion.1
  11.2 0.1 reduce_sum.49
  11.3 0.1 copy.46
  11.4 7.4 %all-to-all-done = f32[8,40,128]{2,1,0:T(8,128)S(1)} async-done(((f32[8,40,128]{2,1,0:T(8,128)}), f32[8,40,128]{2,1,0:T(8,128)S(1)}, u32[]{:S(2)}, u32[]{:S(2)}) %all-to-all-start) | async-done | bytes 163872 | tf_op jit(solution)/shard_map/all_to_all | solution.py:164
  18.8 0.7 maximum_add_fusion
  19.6 0.7 broadcast_in_dim.16
  20.2 3.4 %all-to-all-start.1 = ((f32[8,40,128]{2,1,0:T(8,128)}), f32[8,40,128]{2,1,0:T(8,128)S(1)}, u32[]{:S(2)}, u32[]{:S(2)}) async-start(f32[8,40,128]{2,1,0:T(8,128)} %broadcast_in_dim.16), calls=%async_computation.1 | async-start | bytes 327680 | tf_op jit(solution)/shard_map/all_to_all | solution.py:133
  23.7 8.2 %all-to-all-done.1 = f32[8,40,128]{2,1,0:T(8,128)S(1)} async-done(((f32[8,40,128]{2,1,0:T(8,128)}), f32[8,40,128]{2,1,0:T(8,128)S(1)}, u32[]{:S(2)}, u32[]{:S(2)}) %all-to-all-start.1) | async-done | bytes 163872 | tf_op jit(solution)/shard_map/all_to_all | solution.py:133
  32.0 0.1 copy.48
  32.1 0.2 multiply_reduce_fusion
  32.3 0.1 reshape.61
  32.5 0.4 convolution_convert_fusion
  32.9 1.3 %reshape.62 = bf16[64,48,128]{2,1,0:T(8,128)(2,1)} reshape(bf16[192,2048]{1,0:T(8,128)(2,1)S(1)} %convolution_convert_fusion) | data formatting | bytes 1572864 | tf_op jit(solution)/shard_map/reshape | solution.py:171
  34.2 17.3 %all-to-all-start.2 = ((bf16[64,48,128]{2,1,0:T(8,128)(2,1)}), bf16[64,48,128]{2,1,0:T(8,128)(2,1)S(1)}, u32[]{:S(2)}, u32[]{:S(2)}) async-start(bf16[64,48,128]{2,1,0:T(8,128)(2,1)} %reshape.62), calls=%async_computation.2 | async-start | bytes 1572864 | tf_op jit(solution)/shard_map/all_to_all | solution.py:172
  51.5 1.3 %copy.49 = bf16[1,2048,176]{2,1,0:T(8,128)(2,1)} copy(bf16[1,2048,176]{1,2,0:T(8,128)(2,1)S(1)} %copy-done) | data formatting | bytes 1441792 | tf_op args[11]
  52.8 1.3 %copy.50 = bf16[1,2048,176]{2,1,0:T(8,128)(2,1)} copy(bf16[1,2048,176]{1,2,0:T(8,128)(2,1)S(1)} %copy-done.1) | data formatting | bytes 1441792 | tf_op args[12]
  54.1 20.1 %all-to-all-done.2 = bf16[64,48,128]{2,1,0:T(8,128)(2,1)S(1)} async-done(((bf16[64,48,128]{2,1,0:T(8,128)(2,1)}), bf16[64,48,128]{2,1,0:T(8,128)(2,1)S(1)}, u32[]{:S(2)}, u32[]{:S(2)}) %all-to-all-start.2) | async-done | bytes 786464 | tf_op jit(solution)/shard_map/all_to_all | solution.py:172
  74.3 1.2 reshape.63.x_ref
  75.5 3.8 %shard_map.137 = bf16[192,2048]{1,0:T(8,128)(2,1)} custom-call(bf16[192,2048]{1,0:T(8,128)(2,1)} %reshape.63.x_ref, bf16[2048,176]{1,0:T(8,128)(2,1)} %bitcast.14, bf16[2048,176]{1,0:T(8,128)(2,1)} %bitcast.15, bf16[176,2048]{1,0:T(8,128)(2,1)} %bitcast.20), custom_call_target="tpu_custom_call" | custom-call | tf_op jit(solution)/shard_map/pallas_call | solution.py:98
  79.3 2.2 %reshape.67 = bf16[64,48,128]{2,1,0:T(8,128)(2,1)} reshape(bf16[192,2048]{1,0:T(8,128)(2,1)} %shard_map.137) | data formatting | bytes 1572864 | tf_op jit(solution)/shard_map/reshape | solution.py:177
  81.5 6.5 %all-to-all-start.3 = ((bf16[64,48,128]{2,1,0:T(8,128)(2,1)}), bf16[64,48,128]{2,1,0:T(8,128)(2,1)S(1)}, u32[]{:S(2)}, u32[]{:S(2)}) async-start(bf16[64,48,128]{2,1,0:T(8,128)(2,1)} %reshape.67), calls=%async_computation.3 | async-start | bytes 1572864 | tf_op jit(solution)/shard_map/all_to_all | solution.py:176
  88.0 0.1 select_reduce_fusion
  88.1 22.7 %all-to-all-done.3 = bf16[64,48,128]{2,1,0:T(8,128)(2,1)S(1)} async-done(((bf16[64,48,128]{2,1,0:T(8,128)(2,1)}), bf16[64,48,128]{2,1,0:T(8,128)(2,1)S(1)}, u32[]{:S(2)}, u32[]{:S(2)}) %all-to-all-start.3) | async-done | bytes 786464 | tf_op jit(solution)/shard_map/all_to_all | solution.py:176
  110.7 0.3 reshape.68
  111.1 0.4 convolution_convert_fusion.1
  111.6 10.9 %all_to_all.25 = bf16[8,40,128]{2,1,0:T(8,128)(2,1)S(1)} all-to-all(bf16[8,40,128]{2,1,0:T(8,128)(2,1)S(1)} %copy.52), channel_id=1, replica_groups=mesh['req'=64,'tp'=8] {'tp'}, dimensions={0} | all-to-all | bytes 163840 | tf_op jit(solution)/shard_map/all_to_all | solution.py:125
  122.5 0.6 fusion.4
  (24 shorter events, 0.4 us)
Async XLA Ops:
  0.0 10.6 %copy-start.2 = (s32[20,6]{0,1:T(8,128)S(1)}, s32[20,6]{0,1:T(8,128)}, u32[]{:S(2)}) copy-start(s32[20,6]{0,1:T(8,128)} %param.23) | copy-start | bytes 1444
  3.8 15.0 %all-to-all-start = ((f32[8,40,128]{2,1,0:T(8,128)}), f32[8,40,128]{2,1,0:T(8,128)S(1)}, u32[]{:S(2)}, u32[]{:S(2)}) async-start(f32[8,40,128]{2,1,0:T(8,128)} %shard_map.136), calls=%async_computation | async-start | bytes 327680 | tf_op jit(solution)/shard_map/all_to_all | solution.py:164
  11.4 21.1 %copy-start.3 = (f32[2048]{0:T(1024)S(1)}, f32[2048]{0:T(1024)}, u32[]{:S(2)}) copy-start(f32[2048]{0:T(1024)} %param.22) | copy-start | bytes 24580
  20.2 11.7 %all-to-all-start.1 = ((f32[8,40,128]{2,1,0:T(8,128)}), f32[8,40,128]{2,1,0:T(8,128)S(1)}, u32[]{:S(2)}, u32[]{:S(2)}) async-start(f32[8,40,128]{2,1,0:T(8,128)} %broadcast_in_dim.16), calls=%async_computation.1 | async-start | bytes 327680 | tf_op jit(solution)/shard_map/all_to_all | solution.py:133
  34.2 17.3 %copy-start = (bf16[1,2048,176]{1,2,0:T(8,128)(2,1)S(1)}, bf16[1,2048,176]{1,2,0:T(8,128)(2,1)}, u32[]{:S(2)}) copy-start(bf16[1,2048,176]{1,2,0:T(8,128)(2,1)} %param.25) | copy-start | bytes 2162692
  34.2 40.1 %all-to-all-start.2 = ((bf16[64,48,128]{2,1,0:T(8,128)(2,1)}), bf16[64,48,128]{2,1,0:T(8,128)(2,1)S(1)}, u32[]{:S(2)}, u32[]{:S(2)}) async-start(bf16[64,48,128]{2,1,0:T(8,128)(2,1)} %reshape.62), calls=%async_computation.2 | async-start | bytes 1572864 | tf_op jit(solution)/shard_map/all_to_all | solution.py:172
  51.5 1.3 %copy-start.1 = (bf16[1,2048,176]{1,2,0:T(8,128)(2,1)S(1)}, bf16[1,2048,176]{1,2,0:T(8,128)(2,1)}, u32[]{:S(2)}) copy-start(bf16[1,2048,176]{1,2,0:T(8,128)(2,1)} %param.26) | copy-start | bytes 2162692
  81.4 6.5 %copy-start.4 = (f32[20,6]{0,1:T(8,128)S(1)}, f32[20,6]{0,1:T(8,128)}, u32[]{:S(2)}) copy-start(f32[20,6]{0,1:T(8,128)} %param.24) | copy-start | bytes 1444
  81.5 29.3 %all-to-all-start.3 = ((bf16[64,48,128]{2,1,0:T(8,128)(2,1)}), bf16[64,48,128]{2,1,0:T(8,128)(2,1)S(1)}, u32[]{:S(2)}, u32[]{:S(2)}) async-start(bf16[64,48,128]{2,1,0:T(8,128)(2,1)} %reshape.67), calls=%async_computation.3 | async-start | bytes 1572864 | tf_op jit(solution)/shard_map/all_to_all | solution.py:176

commit v6 on v4

--- a/solution.py
+++ b/solution.py
@@ -87,7 +87,15 @@
     gated = jnp.einsum("secd,edf->secf", slot_rows, gate_weight, preferred_element_type=jnp.float32)
     upward = jnp.einsum("secd,edf->secf", slot_rows, up_weight, preferred_element_type=jnp.float32)
     activation = (jax.nn.silu(gated) * upward).astype(jnp.bfloat16)
-    return jnp.einsum("secf,efd->secd", activation, down_weight, preferred_element_type=jnp.float32)
+    slots = activation.shape[0] * activation.shape[1] * activation.shape[2]
+    hidden = activation.shape[3]
+    width = down_weight.shape[2]
+    return jnp.einsum(
+        "sf,fkl->skl",
+        activation.reshape(slots, hidden),
+        down_weight.reshape(hidden, width // 128, 128),
+        preferred_element_type=jnp.float32,
+    )
 
 
 def stack_halves(value):
@@ -160,7 +168,7 @@
     )
     returned = lax.all_to_all(
         produced.astype(jnp.bfloat16).reshape(packed), "req", split_axis=0, concat_axis=0, tiled=True
-    ).astype(produced.dtype)
+    ).astype(jnp.float32)
     expert_sum = jnp.dot(
         combine,
         returned.reshape(-1, model_width),

time: 122 us -> 121 us (level)
  blocking collectives: 50.7 us -> 10.9 us
  waiting for transfers between devices: 38.2 us -> 60.9 us
  starting transfers between devices: 16.7 us -> 34 us
    all_to_all x1 -> x0, blocking collectives: 39.8 us -> none  [local(): lax.all_to_all(outbound, 'req', split_axis=0, concat_axis=0, tiled=True)]
    all_to_all x0 -> x1, waiting for transfers between devices: none -> 22.6 us  [local(): lax.all_to_all(outbound, 'req', split_axis=0, concat_axis=0, tiled=True)]
    all_to_all x0 -> x1, starting transfers between devices: none -> 17.3 us  [local(): lax.all_to_all(outbound, 'req', split_axis=0, concat_axis=0, tiled=True)]
    reshape x1, local copies, waits for them, and re-layouts: 1.68 us -> 0.09 us  [expert_apply(): activation.reshape(slots, hidden)]
  transfers between devices with their start and end apart: 3 -> 4, of which waited for: 3 -> 4; matrix products, arithmetic and copies ran while one was open for 1% -> 1% of each run, Pallas kernels for 0% -> 0%
where the time goes in v6:
time: 121 us; the launch traced here: 120 us
  waiting for transfers between devices  60.9 us (50%)
  starting transfers between devices  34 us (28%)
  blocking collectives  10.9 us (9%)
  local copies, waits for them, and re-layouts  5.05 us (4%)
  Pallas kernels  3.82 us (3%)
  matrix products  3.24 us (3%)
  other arithmetic  2.23 us (2%)
    all_to_all x1, waiting for transfers between devices, local(): lax.all_to_all(produced.astype(jnp.bfloat16).reshape(packed), 'req', spli...  22.7 us
    all_to_all x1, waiting for transfers between devices, local(): lax.all_to_all(outbound, 'req', split_axis=0, concat_axis=0, tiled=True)  22.6 us
    all_to_all x1, starting transfers between devices, local(): lax.all_to_all(outbound, 'req', split_axis=0, concat_axis=0, tiled=True)  17.3 us
    all_to_all x1, blocking collectives, scatter_sum(): lax.all_to_all(pieces, 'tp', split_axis=0, concat_axis=0, tiled=True)  10.9 us
    all_to_all x1, waiting for transfers between devices, gather_cols(): lax.all_to_all(pieces, 'tp', split_axis=0, concat_axis=0, tiled=True)  8.18 us
    all_to_all x1, waiting for transfers between devices, local(): lax.all_to_all(pieces, 'tp', split_axis=0, concat_axis=0, tiled=True)  7.39 us
    all_to_all x1, starting transfers between devices, local(): lax.all_to_all(pieces, 'tp', split_axis=0, concat_axis=0, tiled=True)  6.82 us
    all_to_all x1, starting transfers between devices, local(): lax.all_to_all(produced.astype(jnp.bfloat16).reshape(packed), 'req', spli...  6.49 us
  transfers between devices with their start and end apart: 4, of which 4 were waited for; matrix products, arithmetic and copies ran while one was open for 1% of the time, Pallas kernels for 0%

profile of v6, /device:TPU:7, one launch (start us, length us, event | category | flops | bytes accessed | tf_op | source)
XLA Modules:
  0.0 120.4 jit_solution(8717330201791810834)
XLA Ops:
  0.0 3.8 %shard_map.136 = f32[8,40,128]{2,1,0:T(8,128)} custom-call(s32[4]{0:T(128)} %len_ref.1, bf16[20,256]{1,0:T(8,128)(2,1)} %q_ref.1, bf16[20,256]{1,0:T(8,128)(2,1)} %nk_ref.1, bf16[20,256]{1,0:T(8,128)(2,1)} %nv_ref.1, bf16[1536,256]{1,0:T(8,128)(2,1)} %bitcast.47, bf16[1536,256]{1,0:T(8,128)(2,1)} %bitcast.48, bf16[256,2048]{1,0:T(8,128)(2,1)} %ow_ref.1), custom_call_target="tpu_custom_call" | custom-call | tf_op jit(solution)/shard_map/pallas_call | solution.py:78
  3.8 6.8 %all-to-all-start = ((f32[8,40,128]{2,1,0:T(8,128)}), f32[8,40,128]{2,1,0:T(8,128)S(1)}, u32[]{:S(2)}, u32[]{:S(2)}) async-start(f32[8,40,128]{2,1,0:T(8,128)} %shard_map.136), calls=%async_computation | async-start | bytes 327680 | tf_op jit(solution)/shard_map/all_to_all | solution.py:154
  10.7 0.1 copy.56
  10.8 0.1 eq.28
  10.9 0.2 reduce_window_sum.11
  11.1 0.2 select_reduce_fusion.1
  11.3 0.1 reduce_sum.49
  11.5 7.4 %all-to-all-done = f32[8,40,128]{2,1,0:T(8,128)S(1)} async-done(((f32[8,40,128]{2,1,0:T(8,128)}), f32[8,40,128]{2,1,0:T(8,128)S(1)}, u32[]{:S(2)}, u32[]{:S(2)}) %all-to-all-start) | async-done | bytes 163872 | tf_op jit(solution)/shard_map/all_to_all | solution.py:154
  18.9 0.7 maximum_add_fusion
  19.6 0.7 broadcast_in_dim.16
  20.3 3.4 %all-to-all-start.1 = ((f32[8,40,128]{2,1,0:T(8,128)}), f32[8,40,128]{2,1,0:T(8,128)S(1)}, u32[]{:S(2)}, u32[]{:S(2)}) async-start(f32[8,40,128]{2,1,0:T(8,128)} %broadcast_in_dim.16), calls=%async_computation.1 | async-start | bytes 327680 | tf_op jit(solution)/shard_map/all_to_all | solution.py:123
  23.8 8.2 %all-to-all-done.1 = f32[8,40,128]{2,1,0:T(8,128)S(1)} async-done(((f32[8,40,128]{2,1,0:T(8,128)}), f32[8,40,128]{2,1,0:T(8,128)S(1)}, u32[]{:S(2)}, u32[]{:S(2)}) %all-to-all-start.1) | async-done | bytes 163872 | tf_op jit(solution)/shard_map/all_to_all | solution.py:123
  32.0 0.1 copy.59
  32.2 0.2 multiply_reduce_fusion
  32.4 0.1 reshape.70
  32.5 0.4 convolution_convert_fusion
  33.0 1.2 %reshape.71 = bf16[64,48,128]{2,1,0:T(8,128)(2,1)} reshape(bf16[192,2048]{1,0:T(8,128)(2,1)S(1)} %convolution_convert_fusion) | data formatting | bytes 1572864 | tf_op jit(solution)/shard_map/reshape | solution.py:161
  34.2 17.3 %all-to-all-start.2 = ((bf16[64,48,128]{2,1,0:T(8,128)(2,1)}), bf16[64,48,128]{2,1,0:T(8,128)(2,1)S(1)}, u32[]{:S(2)}, u32[]{:S(2)}) async-start(bf16[64,48,128]{2,1,0:T(8,128)(2,1)} %reshape.71), calls=%async_computation.2 | async-start | bytes 1572864 | tf_op jit(solution)/shard_map/all_to_all | solution.py:162
  51.6 0.1 copy.70
  51.7 22.6 %all-to-all-done.2 = bf16[64,48,128]{2,1,0:T(8,128)(2,1)S(1)} async-done(((bf16[64,48,128]{2,1,0:T(8,128)(2,1)}), bf16[64,48,128]{2,1,0:T(8,128)(2,1)S(1)}, u32[]{:S(2)}, u32[]{:S(2)}) %all-to-all-start.2) | async-done | bytes 786464 | tf_op jit(solution)/shard_map/all_to_all | solution.py:162
  74.3 0.2 reshape.72
  74.6 1.0 convolution_bitcast_fusion.1
  75.7 1.0 fusion.1
  76.9 0.4 convolution_convert_fusion.2
  77.3 1.4 %copy.65 = bf16[192,16,128]{2,1,0:T(8,128)(2,1)} copy(bf16[192,16,128]{2,0,1:T(8,128)(2,1)S(1)} %convolution_convert_fusion.2) | data formatting | bytes 1572864 | tf_op jit(solution)/shard_map/convert_element_type | solution.py:170
  78.7 6.5 %all-to-all-start.3 = ((bf16[64,48,128]{2,1,0:T(8,128)(2,1)}), bf16[64,48,128]{2,1,0:T(8,128)(2,1)S(1)}, u32[]{:S(2)}, u32[]{:S(2)}) async-start(bf16[64,48,128]{2,1,0:T(8,128)(2,1)} %bitcast.18), calls=%async_computation.3 | async-start | bytes 1572864 | tf_op jit(solution)/shard_map/all_to_all | solution.py:169
  85.2 0.1 select_reduce_fusion
  85.3 22.7 %all-to-all-done.3 = bf16[64,48,128]{2,1,0:T(8,128)(2,1)S(1)} async-done(((bf16[64,48,128]{2,1,0:T(8,128)(2,1)}), bf16[64,48,128]{2,1,0:T(8,128)(2,1)S(1)}, u32[]{:S(2)}, u32[]{:S(2)}) %all-to-all-start.3) | async-done | bytes 786464 | tf_op jit(solution)/shard_map/all_to_all | solution.py:169
  108.0 0.3 reshape.78
  108.3 0.4 convolution_convert_fusion.1
  108.8 10.9 %all_to_all.25 = bf16[8,40,128]{2,1,0:T(8,128)(2,1)S(1)} all-to-all(bf16[8,40,128]{2,1,0:T(8,128)(2,1)S(1)} %copy.67), channel_id=1, replica_groups=mesh['req'=64,'tp'=8] {'tp'}, dimensions={0} | all-to-all | bytes 163840 | tf_op jit(solution)/shard_map/all_to_all | solution.py:115
  119.7 0.6 fusion.12
  (29 shorter events, 0.7 us)
Async XLA Ops:
  0.0 74.6 %copy-start = (bf16[1,2048,176]{1,2,0:T(8,128)(2,1)S(1)}, bf16[1,2048,176]{1,2,0:T(8,128)(2,1)}, u32[]{:S(2)}) copy-start(bf16[1,2048,176]{1,2,0:T(8,128)(2,1)} %param.25) | copy-start | bytes 2162692
  0.0 10.6 %copy-start.2 = (s32[20,6]{0,1:T(8,128)S(1)}, s32[20,6]{0,1:T(8,128)}, u32[]{:S(2)}) copy-start(s32[20,6]{0,1:T(8,128)} %param.23) | copy-start | bytes 1444
  3.8 15.0 %all-to-all-start = ((f32[8,40,128]{2,1,0:T(8,128)}), f32[8,40,128]{2,1,0:T(8,128)S(1)}, u32[]{:S(2)}, u32[]{:S(2)}) async-start(f32[8,40,128]{2,1,0:T(8,128)} %shard_map.136), calls=%async_computation | async-start | bytes 327680 | tf_op jit(solution)/shard_map/all_to_all | solution.py:154
  11.5 21.1 %copy-start.3 = (f32[2048]{0:T(1024)S(1)}, f32[2048]{0:T(1024)}, u32[]{:S(2)}) copy-start(f32[2048]{0:T(1024)} %param.22) | copy-start | bytes 24580
  20.3 11.7 %all-to-all-start.1 = ((f32[8,40,128]{2,1,0:T(8,128)}), f32[8,40,128]{2,1,0:T(8,128)S(1)}, u32[]{:S(2)}, u32[]{:S(2)}) async-start(f32[8,40,128]{2,1,0:T(8,128)} %broadcast_in_dim.16), calls=%async_computation.1 | async-start | bytes 327680 | tf_op jit(solution)/shard_map/all_to_all | solution.py:123
  34.2 17.3 %copy-start.1 = (bf16[1,176,2048]{2,1,0:T(8,128)(2,1)S(1)}, bf16[1,176,2048]{2,1,0:T(8,128)(2,1)}, u32[]{:S(2)}) copy-start(bf16[1,176,2048]{2,1,0:T(8,128)(2,1)} %param.27) | copy-start | bytes 2162692
  34.2 40.1 %all-to-all-start.2 = ((bf16[64,48,128]{2,1,0:T(8,128)(2,1)}), bf16[64,48,128]{2,1,0:T(8,128)(2,1)S(1)}, u32[]{:S(2)}, u32[]{:S(2)}) async-start(bf16[64,48,128]{2,1,0:T(8,128)(2,1)} %reshape.71), calls=%async_computation.2 | async-start | bytes 1572864 | tf_op jit(solution)/shard_map/all_to_all | solution.py:162
  74.6 1.1 copy-start.5
  78.7 6.5 %copy-start.4 = (f32[20,6]{0,1:T(8,128)S(1)}, f32[20,6]{0,1:T(8,128)}, u32[]{:S(2)}) copy-start(f32[20,6]{0,1:T(8,128)} %param.24) | copy-start | bytes 1444
  78.7 29.3 %all-to-all-start.3 = ((bf16[64,48,128]{2,1,0:T(8,128)(2,1)}), bf16[64,48,128]{2,1,0:T(8,128)(2,1)S(1)}, u32[]{:S(2)}, u32[]{:S(2)}) async-start(bf16[64,48,128]{2,1,0:T(8,128)(2,1)} %bitcast.18), calls=%async_computation.3 | async-start | bytes 1572864 | tf_op jit(solution)/shard_map/all_to_all | solution.py:169

commit v7 on v6

--- a/solution.py
+++ b/solution.py
@@ -36,6 +36,7 @@
     flat_v = cache_values.reshape(req_count * cache_len, width)
 
     def kernel(len_ref, q_ref, nk_ref, nv_ref, ck_ref, cv_ref, ow_ref, out_ref):
+        head = pl.program_id(0)
         row = lax.broadcasted_iota(jnp.int32, (tokens, 1), 0)
         lo = jnp.zeros((tokens, 1), jnp.int32)
         hi = jnp.zeros((tokens, 1), jnp.int32)
@@ -50,36 +51,50 @@
         fresh_at = lax.broadcasted_iota(jnp.int32, (tokens, tokens), 1)
         live_n = (fresh_at >= first) & (fresh_at <= row)
         dims = (((1,), (1,)), ((), ()))
-        heads = []
-        for h in range(head_count):
-            cols = slice(h * HD, (h + 1) * HD)
-            q = q_ref[:, cols]
-            sc = lax.dot_general(q, ck_ref[:, cols], dims, preferred_element_type=jnp.float32) * HD ** (-0.5)
-            sn = lax.dot_general(q, nk_ref[:, cols], dims, preferred_element_type=jnp.float32) * HD ** (-0.5)
-            sc = jnp.where(live_c, sc, -1e30)
-            sn = jnp.where(live_n, sn, -1e30)
-            top = jnp.maximum(jnp.max(sc, axis=1, keepdims=True), jnp.max(sn, axis=1, keepdims=True))
-            ec = jnp.exp(sc - top)
-            en = jnp.exp(sn - top)
-            total = jnp.sum(ec, axis=1, keepdims=True) + jnp.sum(en, axis=1, keepdims=True)
-            wc = (ec / total).astype(jnp.bfloat16)
-            wn = (en / total).astype(jnp.bfloat16)
-            att = jnp.dot(wc, cv_ref[:, cols], preferred_element_type=jnp.float32)
-            att = att + jnp.dot(wn, nv_ref[:, cols], preferred_element_type=jnp.float32)
-            heads.append(att.astype(jnp.bfloat16))
-        attended = jnp.concatenate(heads, axis=1)
-        partial = jnp.dot(attended, ow_ref[...], preferred_element_type=jnp.float32)
+        q = q_ref[...]
+        sc = lax.dot_general(q, ck_ref[...], dims, preferred_element_type=jnp.float32) * HD ** (-0.5)
+        sn = lax.dot_general(q, nk_ref[...], dims, preferred_element_type=jnp.float32) * HD ** (-0.5)
+        sc = jnp.where(live_c, sc, -1e30)
+        sn = jnp.where(live_n, sn, -1e30)
+        top = jnp.maximum(jnp.max(sc, axis=1, keepdims=True), jnp.max(sn, axis=1, keepdims=True))
+        ec = jnp.exp(sc - top)
+        en = jnp.exp(sn - top)
+        total = jnp.sum(ec, axis=1, keepdims=True) + jnp.sum(en, axis=1, keepdims=True)
+        wc = (ec / total).astype(jnp.bfloat16)
+        wn = (en / total).astype(jnp.bfloat16)
+        att = jnp.dot(wc, cv_ref[...], preferred_element_type=jnp.float32)
+        att = att + jnp.dot(wn, nv_ref[...], preferred_element_type=jnp.float32)
+        partial = jnp.dot(att.astype(jnp.bfloat16), ow_ref[...], preferred_element_type=jnp.float32)
         half = columns // 2
-        for k in range(tp_count):
-            out_ref[k, 0:tokens, :] = partial[:, k * columns:k * columns + half]
-            out_ref[k, tokens:2 * tokens, :] = partial[:, k * columns + half:(k + 1) * columns]
-
-    vmem = pl.BlockSpec(memory_space=pltpu.VMEM)
+
+        @pl.when(head == 0)
+        def _():
+            for k in range(tp_count):
+                out_ref[k, 0:tokens, :] = partial[:, k * columns:k * columns + half]
+                out_ref[k, tokens:2 * tokens, :] = partial[:, k * columns + half:(k + 1) * columns]
+
+        @pl.when(head > 0)
+        def _():
+            for k in range(tp_count):
+                out_ref[k, 0:tokens, :] += partial[:, k * columns:k * columns + half]
+                out_ref[k, tokens:2 * tokens, :] += partial[:, k * columns + half:(k + 1) * columns]
+
+    token_block = pl.BlockSpec((tokens, HD), lambda h: (0, h))
+    cache_block = pl.BlockSpec((req_count * cache_len, HD), lambda h: (0, h))
     return pl.pallas_call(
         kernel,
+        grid=(head_count,),
         out_shape=jax.ShapeDtypeStruct((tp_count, 2 * tokens, columns // 2), jnp.float32),
-        in_specs=[pl.BlockSpec(memory_space=pltpu.SMEM)] + [vmem] * 6,
-        out_specs=vmem,
+        in_specs=[
+            pl.BlockSpec(memory_space=pltpu.SMEM),
+            token_block,
+            token_block,
+            token_block,
+            cache_block,
+            cache_block,
+            pl.BlockSpec((HD, model_width), lambda h: (h, 0)),
+        ],
+        out_specs=pl.BlockSpec((tp_count, 2 * tokens, columns // 2), lambda h: (0, 0, 0)),
     )(cache_lengths, queries, new_keys, new_values, flat_k, flat_v, out_weight)
 
 

time: 121 us -> 121 us (level)
  no operation moved by 1% of the time
where the time goes in v7:
time: 121 us; the launch traced here: 120 us
  waiting for transfers between devices  60.9 us (50%)
  starting transfers between devices  34 us (28%)
  blocking collectives  10.9 us (9%)
  local copies, waits for them, and re-layouts  5.05 us (4%)
  Pallas kernels  3.7 us (3%)
  matrix products  3.24 us (3%)
  other arithmetic  2.23 us (2%)
    all_to_all x1, waiting for transfers between devices, local(): lax.all_to_all(produced.astype(jnp.bfloat16).reshape(packed), 'req', spli...  22.7 us
    all_to_all x1, waiting for transfers between devices, local(): lax.all_to_all(outbound, 'req', split_axis=0, concat_axis=0, tiled=True)  22.6 us
    all_to_all x1, starting transfers between devices, local(): lax.all_to_all(outbound, 'req', split_axis=0, concat_axis=0, tiled=True)  17.3 us
    all_to_all x1, blocking collectives, scatter_sum(): lax.all_to_all(pieces, 'tp', split_axis=0, concat_axis=0, tiled=True)  10.9 us
    all_to_all x1, waiting for transfers between devices, gather_cols(): lax.all_to_all(pieces, 'tp', split_axis=0, concat_axis=0, tiled=True)  8.18 us
    all_to_all x1, waiting for transfers between devices, local(): lax.all_to_all(pieces, 'tp', split_axis=0, concat_axis=0, tiled=True)  7.4 us
    all_to_all x1, starting transfers between devices, local(): lax.all_to_all(pieces, 'tp', split_axis=0, concat_axis=0, tiled=True)  6.82 us
    all_to_all x1, starting transfers between devices, local(): lax.all_to_all(produced.astype(jnp.bfloat16).reshape(packed), 'req', spli...  6.49 us
  transfers between devices with their start and end apart: 4, of which 4 were waited for; matrix products, arithmetic and copies ran while one was open for 1% of the time, Pallas kernels for 0%

profile of v7, /device:TPU:7, one launch (start us, length us, event | category | flops | bytes accessed | tf_op | source)
XLA Modules:
  0.0 120.2 jit_solution(8417130070814299027)
XLA Ops:
  0.0 3.7 %shard_map.136 = f32[8,40,128]{2,1,0:T(8,128)} custom-call(s32[4]{0:T(128)} %len_ref.1, bf16[20,256]{1,0:T(8,128)(2,1)} %q_ref.1, bf16[20,256]{1,0:T(8,128)(2,1)} %nk_ref.1, bf16[20,256]{1,0:T(8,128)(2,1)} %nv_ref.1, bf16[1536,256]{1,0:T(8,128)(2,1)} %bitcast.47, bf16[1536,256]{1,0:T(8,128)(2,1)} %bitcast.48, bf16[256,2048]{1,0:T(8,128)(2,1)} %ow_ref.1), custom_call_target="tpu_custom_call" | custom-call | tf_op jit(solution)/shard_map/pallas_call | solution.py:84
  3.7 6.8 %all-to-all-start = ((f32[8,40,128]{2,1,0:T(8,128)}), f32[8,40,128]{2,1,0:T(8,128)S(1)}, u32[]{:S(2)}, u32[]{:S(2)}) async-start(f32[8,40,128]{2,1,0:T(8,128)} %shard_map.136), calls=%async_computation | async-start | bytes 327680 | tf_op jit(solution)/shard_map/all_to_all | solution.py:169
  10.5 0.1 copy.56
  10.6 0.1 eq.28
  10.8 0.2 reduce_window_sum.11
  11.0 0.2 select_reduce_fusion.1
  11.2 0.1 reduce_sum.49
  11.3 7.4 %all-to-all-done = f32[8,40,128]{2,1,0:T(8,128)S(1)} async-done(((f32[8,40,128]{2,1,0:T(8,128)}), f32[8,40,128]{2,1,0:T(8,128)S(1)}, u32[]{:S(2)}, u32[]{:S(2)}) %all-to-all-start) | async-done | bytes 163872 | tf_op jit(solution)/shard_map/all_to_all | solution.py:169
  18.8 0.7 maximum_add_fusion
  19.5 0.7 broadcast_in_dim.16
  20.2 3.4 %all-to-all-start.1 = ((f32[8,40,128]{2,1,0:T(8,128)}), f32[8,40,128]{2,1,0:T(8,128)S(1)}, u32[]{:S(2)}, u32[]{:S(2)}) async-start(f32[8,40,128]{2,1,0:T(8,128)} %broadcast_in_dim.16), calls=%async_computation.1 | async-start | bytes 327680 | tf_op jit(solution)/shard_map/all_to_all | solution.py:138
  23.7 8.2 %all-to-all-done.1 = f32[8,40,128]{2,1,0:T(8,128)S(1)} async-done(((f32[8,40,128]{2,1,0:T(8,128)}), f32[8,40,128]{2,1,0:T(8,128)S(1)}, u32[]{:S(2)}, u32[]{:S(2)}) %all-to-all-start.1) | async-done | bytes 163872 | tf_op jit(solution)/shard_map/all_to_all | solution.py:138
  31.9 0.1 copy.59
  32.0 0.2 multiply_reduce_fusion
  32.3 0.1 reshape.70
  32.4 0.4 convolution_convert_fusion
  32.9 1.2 %reshape.71 = bf16[64,48,128]{2,1,0:T(8,128)(2,1)} reshape(bf16[192,2048]{1,0:T(8,128)(2,1)S(1)} %convolution_convert_fusion) | data formatting | bytes 1572864 | tf_op jit(solution)/shard_map/reshape | solution.py:176
  34.1 17.3 %all-to-all-start.2 = ((bf16[64,48,128]{2,1,0:T(8,128)(2,1)}), bf16[64,48,128]{2,1,0:T(8,128)(2,1)S(1)}, u32[]{:S(2)}, u32[]{:S(2)}) async-start(bf16[64,48,128]{2,1,0:T(8,128)(2,1)} %reshape.71), calls=%async_computation.2 | async-start | bytes 1572864 | tf_op jit(solution)/shard_map/all_to_all | solution.py:177
  51.4 0.1 copy.70
  51.6 22.6 %all-to-all-done.2 = bf16[64,48,128]{2,1,0:T(8,128)(2,1)S(1)} async-done(((bf16[64,48,128]{2,1,0:T(8,128)(2,1)}), bf16[64,48,128]{2,1,0:T(8,128)(2,1)S(1)}, u32[]{:S(2)}, u32[]{:S(2)}) %all-to-all-start.2) | async-done | bytes 786464 | tf_op jit(solution)/shard_map/all_to_all | solution.py:177
  74.2 0.2 reshape.72
  74.5 1.0 convolution_bitcast_fusion.1
  75.6 1.0 fusion.1
  76.8 0.4 convolution_convert_fusion.2
  77.2 1.4 %copy.65 = bf16[192,16,128]{2,1,0:T(8,128)(2,1)} copy(bf16[192,16,128]{2,0,1:T(8,128)(2,1)S(1)} %convolution_convert_fusion.2) | data formatting | bytes 1572864 | tf_op jit(solution)/shard_map/convert_element_type | solution.py:185
  78.6 6.5 %all-to-all-start.3 = ((bf16[64,48,128]{2,1,0:T(8,128)(2,1)}), bf16[64,48,128]{2,1,0:T(8,128)(2,1)S(1)}, u32[]{:S(2)}, u32[]{:S(2)}) async-start(bf16[64,48,128]{2,1,0:T(8,128)(2,1)} %bitcast.18), calls=%async_computation.3 | async-start | bytes 1572864 | tf_op jit(solution)/shard_map/all_to_all | solution.py:184
  85.1 0.1 select_reduce_fusion
  85.2 22.7 %all-to-all-done.3 = bf16[64,48,128]{2,1,0:T(8,128)(2,1)S(1)} async-done(((bf16[64,48,128]{2,1,0:T(8,128)(2,1)}), bf16[64,48,128]{2,1,0:T(8,128)(2,1)S(1)}, u32[]{:S(2)}, u32[]{:S(2)}) %all-to-all-start.3) | async-done | bytes 786464 | tf_op jit(solution)/shard_map/all_to_all | solution.py:184
  107.8 0.3 reshape.78
  108.2 0.4 convolution_convert_fusion.1
  108.7 10.9 %all_to_all.25 = bf16[8,40,128]{2,1,0:T(8,128)(2,1)S(1)} all-to-all(bf16[8,40,128]{2,1,0:T(8,128)(2,1)S(1)} %copy.67), channel_id=1, replica_groups=mesh['req'=64,'tp'=8] {'tp'}, dimensions={0} | all-to-all | bytes 163840 | tf_op jit(solution)/shard_map/all_to_all | solution.py:130
  119.6 0.6 fusion.12
  (29 shorter events, 0.7 us)
Async XLA Ops:
  0.0 74.5 %copy-start = (bf16[1,2048,176]{1,2,0:T(8,128)(2,1)S(1)}, bf16[1,2048,176]{1,2,0:T(8,128)(2,1)}, u32[]{:S(2)}) copy-start(bf16[1,2048,176]{1,2,0:T(8,128)(2,1)} %param.25) | copy-start | bytes 2162692
  0.0 10.5 %copy-start.2 = (s32[20,6]{0,1:T(8,128)S(1)}, s32[20,6]{0,1:T(8,128)}, u32[]{:S(2)}) copy-start(s32[20,6]{0,1:T(8,128)} %param.23) | copy-start | bytes 1444
  3.7 15.0 %all-to-all-start = ((f32[8,40,128]{2,1,0:T(8,128)}), f32[8,40,128]{2,1,0:T(8,128)S(1)}, u32[]{:S(2)}, u32[]{:S(2)}) async-start(f32[8,40,128]{2,1,0:T(8,128)} %shard_map.136), calls=%async_computation | async-start | bytes 327680 | tf_op jit(solution)/shard_map/all_to_all | solution.py:169
  11.3 21.1 %copy-start.3 = (f32[2048]{0:T(1024)S(1)}, f32[2048]{0:T(1024)}, u32[]{:S(2)}) copy-start(f32[2048]{0:T(1024)} %param.22) | copy-start | bytes 24580
  20.2 11.7 %all-to-all-start.1 = ((f32[8,40,128]{2,1,0:T(8,128)}), f32[8,40,128]{2,1,0:T(8,128)S(1)}, u32[]{:S(2)}, u32[]{:S(2)}) async-start(f32[8,40,128]{2,1,0:T(8,128)} %broadcast_in_dim.16), calls=%async_computation.1 | async-start | bytes 327680 | tf_op jit(solution)/shard_map/all_to_all | solution.py:138
  34.1 17.3 %copy-start.1 = (bf16[1,176,2048]{2,1,0:T(8,128)(2,1)S(1)}, bf16[1,176,2048]{2,1,0:T(8,128)(2,1)}, u32[]{:S(2)}) copy-start(bf16[1,176,2048]{2,1,0:T(8,128)(2,1)} %param.27) | copy-start | bytes 2162692
  34.1 40.1 %all-to-all-start.2 = ((bf16[64,48,128]{2,1,0:T(8,128)(2,1)}), bf16[64,48,128]{2,1,0:T(8,128)(2,1)S(1)}, u32[]{:S(2)}, u32[]{:S(2)}) async-start(bf16[64,48,128]{2,1,0:T(8,128)(2,1)} %reshape.71), calls=%async_computation.2 | async-start | bytes 1572864 | tf_op jit(solution)/shard_map/all_to_all | solution.py:177
  74.5 1.1 copy-start.5
  78.5 6.5 %copy-start.4 = (f32[20,6]{0,1:T(8,128)S(1)}, f32[20,6]{0,1:T(8,128)}, u32[]{:S(2)}) copy-start(f32[20,6]{0,1:T(8,128)} %param.24) | copy-start | bytes 1444
  78.6 29.3 %all-to-all-start.3 = ((bf16[64,48,128]{2,1,0:T(8,128)(2,1)}), bf16[64,48,128]{2,1,0:T(8,128)(2,1)S(1)}, u32[]{:S(2)}, u32[]{:S(2)}) async-start(bf16[64,48,128]{2,1,0:T(8,128)(2,1)} %bitcast.18), calls=%async_computation.3 | async-start | bytes 1572864 | tf_op jit(solution)/shard_map/all_to_all | solution.py:184

commit v8 on v6

--- a/solution.py
+++ b/solution.py
@@ -84,15 +84,13 @@
 
 
 def expert_apply(slot_rows, gate_weight, up_weight, down_weight):
-    gated = jnp.einsum("secd,edf->secf", slot_rows, gate_weight, preferred_element_type=jnp.float32)
-    upward = jnp.einsum("secd,edf->secf", slot_rows, up_weight, preferred_element_type=jnp.float32)
+    width, hidden = gate_weight.shape[1], gate_weight.shape[2]
+    gated = jnp.dot(slot_rows, gate_weight.reshape(width, hidden), preferred_element_type=jnp.float32)
+    upward = jnp.dot(slot_rows, up_weight.reshape(width, hidden), preferred_element_type=jnp.float32)
     activation = (jax.nn.silu(gated) * upward).astype(jnp.bfloat16)
-    slots = activation.shape[0] * activation.shape[1] * activation.shape[2]
-    hidden = activation.shape[3]
-    width = down_weight.shape[2]
     return jnp.einsum(
         "sf,fkl->skl",
-        activation.reshape(slots, hidden),
+        activation,
         down_weight.reshape(hidden, width // 128, 128),
         preferred_element_type=jnp.float32,
     )
@@ -116,13 +114,12 @@
     return unstack_halves(jnp.sum(pieces.astype(jnp.float32), axis=0))
 
 
-def gather_cols(value, tp_count):
-    rows, columns = value.shape
-    stacked = stack_halves(value)
+def gather_stacked(stacked, tp_count):
+    rows, half = stacked.shape[0] // 2, stacked.shape[1]
     pieces = jnp.broadcast_to(stacked[None], (tp_count,) + stacked.shape)
     pieces = lax.all_to_all(pieces, "tp", split_axis=0, concat_axis=0, tiled=True)
-    pieces = pieces.reshape(tp_count, 2, rows, columns // 2).transpose(2, 0, 1, 3)
-    return pieces.reshape(rows, tp_count * columns)
+    pieces = pieces.reshape(tp_count, 2, rows, half).transpose(2, 0, 1, 3)
+    return pieces.reshape(rows, tp_count * 2 * half)
 
 
 def local(
@@ -152,8 +149,9 @@
     dispatch, combine = slot_tables(routes, route_gates)
     hidden_cols = lax.dynamic_slice_in_dim(hidden_in, offset, columns, 1).astype(jnp.float32)
     pieces = lax.all_to_all(pieces, "tp", split_axis=0, concat_axis=0, tiled=True)
-    summed_cols = unstack_halves(jnp.sum(pieces, axis=0)) + hidden_cols
-    summed = gather_cols(summed_cols, tp_count)
+    summed_stacked = jnp.sum(pieces, axis=0) + stack_halves(hidden_cols)
+    summed_cols = unstack_halves(summed_stacked)
+    summed = gather_stacked(summed_stacked, tp_count)
     mean_square = jnp.mean(summed * summed, axis=-1, keepdims=True)
     normed = (summed * lax.rsqrt(mean_square + 1e-06) * norm_gain[None, :]).astype(jnp.bfloat16)
     outbound = jnp.dot(dispatch, normed, preferred_element_type=jnp.float32).astype(jnp.bfloat16)
@@ -161,7 +159,7 @@
     outbound = outbound.reshape(packed)
     arrived = lax.all_to_all(outbound, "req", split_axis=0, concat_axis=0, tiled=True)
     produced = expert_apply(
-        arrived.reshape(holders, 1, CAP, model_width),
+        arrived.reshape(holders * CAP, model_width),
         gate_weight,
         up_weight,
         down_weight,

time: 121 us -> 122 us (level)
  blocking collectives: 10.9 us -> 0 us
  waiting for transfers between devices: 60.9 us -> 67.7 us
  starting transfers between devices: 34 us -> 37.4 us
  local copies, waits for them, and re-layouts: 5.05 us -> 6.39 us
    all_to_all x1 -> x0, blocking collectives: 10.9 us -> none  [scatter_sum(): lax.all_to_all(pieces, 'tp', split_axis=0, concat_axis=0, tiled=True)]
    all_to_all x1 -> x2, waiting for transfers between devices: 8.18 us -> 16.6 us  [the longest x1 8.42 us: scatter_sum(): lax.all_to_all(pieces, 'tp', split_axis=0, concat_axis=0, tiled=True)]
    all_to_all x1 -> x2, starting transfers between devices: 3.38 us -> 6.74 us  [the longest x1 3.38 us: gather_stacked(): lax.all_to_all(pieces, 'tp', split_axis=0, concat_axis=0, tiled=True)]
    dot_general x3 -> x2, matrix products: 2.4 us -> 2.63 us  [the longest x1 2.25 us: expert_apply(): jnp.einsum('sf,fkl->skl', activation, down_weight.reshape(hidden, width /...]
  transfers between devices with their start and end apart: 4 -> 5, of which waited for: 4 -> 5; matrix products, arithmetic and copies ran while one was open for 1% -> 2% of each run, Pallas kernels for 0% -> 0%
where the time goes in v8:
time: 122 us; the launch traced here: 121 us
  waiting for transfers between devices  67.7 us (55%)
  starting transfers between devices  37.4 us (31%)
  local copies, waits for them, and re-layouts  6.39 us (5%)
  Pallas kernels  3.82 us (3%)
  matrix products  3.47 us (3%)
  other arithmetic  2.23 us (2%)
    all_to_all x1, waiting for transfers between devices, local(): lax.all_to_all(produced.astype(jnp.bfloat16).reshape(packed), 'req', spli...  22.7 us
    all_to_all x1, waiting for transfers between devices, local(): lax.all_to_all(outbound, 'req', split_axis=0, concat_axis=0, tiled=True)  21.7 us
    all_to_all x1, starting transfers between devices, local(): lax.all_to_all(outbound, 'req', split_axis=0, concat_axis=0, tiled=True)  17.3 us
    all_to_all x1, waiting for transfers between devices, scatter_sum(): lax.all_to_all(pieces, 'tp', split_axis=0, concat_axis=0, tiled=True)  8.42 us
    all_to_all x1, waiting for transfers between devices, gather_stacked(): lax.all_to_all(pieces, 'tp', split_axis=0, concat_axis=0, tiled=True)  8.18 us
    all_to_all x1, starting transfers between devices, local(): lax.all_to_all(pieces, 'tp', split_axis=0, concat_axis=0, tiled=True)  6.82 us
    all_to_all x1, waiting for transfers between devices, local(): lax.all_to_all(pieces, 'tp', split_axis=0, concat_axis=0, tiled=True)  6.67 us
    all_to_all x1, starting transfers between devices, local(): lax.all_to_all(produced.astype(jnp.bfloat16).reshape(packed), 'req', spli...  6.49 us
  transfers between devices with their start and end apart: 5, of which 5 were waited for; matrix products, arithmetic and copies ran while one was open for 2% of the time, Pallas kernels for 0%

profile of v8, /device:TPU:7, one launch (start us, length us, event | category | flops | bytes accessed | tf_op | source)
XLA Modules:
  0.0 121.2 jit_solution(810012604076307762)
XLA Ops:
  0.0 3.8 %shard_map.136 = f32[8,40,128]{2,1,0:T(8,128)} custom-call(s32[4]{0:T(128)} %len_ref.1, bf16[20,256]{1,0:T(8,128)(2,1)} %q_ref.1, bf16[20,256]{1,0:T(8,128)(2,1)} %nk_ref.1, bf16[20,256]{1,0:T(8,128)(2,1)} %nv_ref.1, bf16[1536,256]{1,0:T(8,128)(2,1)} %bitcast.30, bf16[1536,256]{1,0:T(8,128)(2,1)} %bitcast.31, bf16[256,2048]{1,0:T(8,128)(2,1)} %ow_ref.1), custom_call_target="tpu_custom_call" | custom-call | tf_op jit(solution)/shard_map/pallas_call | solution.py:78
  3.8 6.8 %all-to-all-start = ((f32[8,40,128]{2,1,0:T(8,128)}), f32[8,40,128]{2,1,0:T(8,128)S(1)}, u32[]{:S(2)}, u32[]{:S(2)}) async-start(f32[8,40,128]{2,1,0:T(8,128)} %shard_map.136), calls=%async_computation | async-start | bytes 327680 | tf_op jit(solution)/shard_map/all_to_all | solution.py:151
  10.7 0.1 copy.44
  10.8 0.1 eq.28
  10.9 0.2 reduce_window_sum.11
  11.1 0.2 select_reduce_fusion.1
  11.5 0.7 dynamic-slice_convert_fusion
  12.2 6.7 %all-to-all-done = f32[8,40,128]{2,1,0:T(8,128)S(1)} async-done(((f32[8,40,128]{2,1,0:T(8,128)}), f32[8,40,128]{2,1,0:T(8,128)S(1)}, u32[]{:S(2)}, u32[]{:S(2)}) %all-to-all-start) | async-done | bytes 163872 | tf_op jit(solution)/shard_map/all_to_all | solution.py:151
  18.9 0.7 broadcast_in_dim.16
  19.6 3.4 %all-to-all-start.1 = ((f32[8,40,128]{2,1,0:T(8,128)}), f32[8,40,128]{2,1,0:T(8,128)S(1)}, u32[]{:S(2)}, u32[]{:S(2)}) async-start(f32[8,40,128]{2,1,0:T(8,128)} %broadcast_in_dim.16), calls=%async_computation.1 | async-start | bytes 327680 | tf_op jit(solution)/shard_map/all_to_all | solution.py:120
  23.1 8.2 %all-to-all-done.1 = f32[8,40,128]{2,1,0:T(8,128)S(1)} async-done(((f32[8,40,128]{2,1,0:T(8,128)}), f32[8,40,128]{2,1,0:T(8,128)S(1)}, u32[]{:S(2)}, u32[]{:S(2)}) %all-to-all-start.1) | async-done | bytes 163872 | tf_op jit(solution)/shard_map/all_to_all | solution.py:120
  31.3 0.1 copy.47
  31.4 0.2 multiply_reduce_fusion
  31.7 0.1 reshape.77
  31.8 0.4 convolution_convert_fusion
  32.2 1.2 %reshape.78 = bf16[64,48,128]{2,1,0:T(8,128)(2,1)} reshape(bf16[192,2048]{1,0:T(8,128)(2,1)S(1)} %convolution_convert_fusion) | data formatting | bytes 1572864 | tf_op jit(solution)/shard_map/reshape | solution.py:159
  33.5 17.3 %all-to-all-start.2 = ((bf16[64,48,128]{2,1,0:T(8,128)(2,1)}), bf16[64,48,128]{2,1,0:T(8,128)(2,1)S(1)}, u32[]{:S(2)}, u32[]{:S(2)}) async-start(bf16[64,48,128]{2,1,0:T(8,128)(2,1)} %reshape.78), calls=%async_computation.2 | async-start | bytes 1572864 | tf_op jit(solution)/shard_map/all_to_all | solution.py:160
  50.8 1.0 copy.52
  51.9 21.7 %all-to-all-done.2 = bf16[64,48,128]{2,1,0:T(8,128)(2,1)S(1)} async-done(((bf16[64,48,128]{2,1,0:T(8,128)(2,1)}), bf16[64,48,128]{2,1,0:T(8,128)(2,1)S(1)}, u32[]{:S(2)}, u32[]{:S(2)}) %all-to-all-start.2) | async-done | bytes 786464 | tf_op jit(solution)/shard_map/all_to_all | solution.py:160
  73.6 0.3 reshape.79
  73.9 0.4 fusion.4
  74.3 2.3 %convolution_convert_fusion.2 = bf16[192,16,128]{2,0,1:T(8,128)(2,1)S(1)} fusion(bf16[192,2048]{1,0:T(8,128)(2,1)S(1)} %reshape.79, bf16[1,2048,176]{1,2,0:T(8,128)(2,1)S(1)} %copy-done, bf16[176,16,128]{2,1,0:T(8,128)(2,1)} %bitcast.33, f32[192,176]{0,1:T(8,128)S(1)} %fusion.4), kind=kOutput, calls=%fused_computation.2 | convolution fusion | flops 277420032 | bytes 3149824 | tf_op jit(solution)/shard_map/sf,fkl->skl/dot_general | solution.py:91
  76.6 1.4 %copy.49 = bf16[192,16,128]{2,1,0:T(8,128)(2,1)} copy(bf16[192,16,128]{2,0,1:T(8,128)(2,1)S(1)} %convolution_convert_fusion.2) | data formatting | bytes 1572864 | tf_op jit(solution)/shard_map/convert_element_type | solution.py:168
  78.0 6.5 %all-to-all-start.3 = ((bf16[64,48,128]{2,1,0:T(8,128)(2,1)}), bf16[64,48,128]{2,1,0:T(8,128)(2,1)S(1)}, u32[]{:S(2)}, u32[]{:S(2)}) async-start(bf16[64,48,128]{2,1,0:T(8,128)(2,1)} %bitcast.8), calls=%async_computation.3 | async-start | bytes 1572864 | tf_op jit(solution)/shard_map/all_to_all | solution.py:167
  84.5 0.1 select_reduce_fusion
  84.6 22.7 %all-to-all-done.3 = bf16[64,48,128]{2,1,0:T(8,128)(2,1)S(1)} async-done(((bf16[64,48,128]{2,1,0:T(8,128)(2,1)}), bf16[64,48,128]{2,1,0:T(8,128)(2,1)S(1)}, u32[]{:S(2)}, u32[]{:S(2)}) %all-to-all-start.3) | async-done | bytes 786464 | tf_op jit(solution)/shard_map/all_to_all | solution.py:167
  107.3 0.3 reshape.84
  107.6 0.4 convolution_convert_fusion.1
  108.1 0.6 copy.51
  108.7 3.4 %all-to-all-start.4 = ((bf16[8,40,128]{2,1,0:T(8,128)(2,1)}), bf16[8,40,128]{2,1,0:T(8,128)(2,1)S(1)}, u32[]{:S(2)}, u32[]{:S(2)}) async-start(bf16[8,40,128]{2,1,0:T(8,128)(2,1)} %copy.51), calls=%async_computation.4 | async-start | bytes 163840 | tf_op jit(solution)/shard_map/all_to_all | solution.py:113
  112.1 8.4 %all-to-all-done.4 = bf16[8,40,128]{2,1,0:T(8,128)(2,1)S(1)} async-done(((bf16[8,40,128]{2,1,0:T(8,128)(2,1)}), bf16[8,40,128]{2,1,0:T(8,128)(2,1)S(1)}, u32[]{:S(2)}, u32[]{:S(2)}) %all-to-all-start.4) | async-done | bytes 81952 | tf_op jit(solution)/shard_map/all_to_all | solution.py:113
  120.6 0.6 fusion.17
  (27 shorter events, 0.5 us)
Async XLA Ops:
  0.0 74.3 %copy-start = (bf16[1,2048,176]{1,2,0:T(8,128)(2,1)S(1)}, bf16[1,2048,176]{1,2,0:T(8,128)(2,1)}, u32[]{:S(2)}) copy-start(bf16[1,2048,176]{1,2,0:T(8,128)(2,1)} %param.26) | copy-start | bytes 2162692
  0.0 10.6 %copy-start.3 = (s32[20,6]{0,1:T(8,128)S(1)}, s32[20,6]{0,1:T(8,128)}, u32[]{:S(2)}) copy-start(s32[20,6]{0,1:T(8,128)} %param.23) | copy-start | bytes 1444
  3.8 15.0 %all-to-all-start = ((f32[8,40,128]{2,1,0:T(8,128)}), f32[8,40,128]{2,1,0:T(8,128)S(1)}, u32[]{:S(2)}, u32[]{:S(2)}) async-start(f32[8,40,128]{2,1,0:T(8,128)} %shard_map.136), calls=%async_computation | async-start | bytes 327680 | tf_op jit(solution)/shard_map/all_to_all | solution.py:151
  11.3 20.5 %copy-start.4 = (f32[2048]{0:T(1024)S(1)}, f32[2048]{0:T(1024)}, u32[]{:S(2)}) copy-start(f32[2048]{0:T(1024)} %param.22) | copy-start | bytes 24580
  19.6 11.7 %all-to-all-start.1 = ((f32[8,40,128]{2,1,0:T(8,128)}), f32[8,40,128]{2,1,0:T(8,128)S(1)}, u32[]{:S(2)}, u32[]{:S(2)}) async-start(f32[8,40,128]{2,1,0:T(8,128)} %broadcast_in_dim.16), calls=%async_computation.1 | async-start | bytes 327680 | tf_op jit(solution)/shard_map/all_to_all | solution.py:120
  33.5 17.3 %copy-start.2 = (bf16[1,176,2048]{2,1,0:T(8,128)(2,1)S(1)}, bf16[1,176,2048]{2,1,0:T(8,128)(2,1)}, u32[]{:S(2)}) copy-start(bf16[1,176,2048]{2,1,0:T(8,128)(2,1)} %param.27) | copy-start | bytes 2162692
  33.5 40.1 %all-to-all-start.2 = ((bf16[64,48,128]{2,1,0:T(8,128)(2,1)}), bf16[64,48,128]{2,1,0:T(8,128)(2,1)S(1)}, u32[]{:S(2)}, u32[]{:S(2)}) async-start(bf16[64,48,128]{2,1,0:T(8,128)(2,1)} %reshape.78), calls=%async_computation.2 | async-start | bytes 1572864 | tf_op jit(solution)/shard_map/all_to_all | solution.py:160
  51.9 22.1 %copy-start.1 = (bf16[1,2048,176]{1,2,0:T(8,128)(2,1)S(1)}, bf16[1,2048,176]{1,2,0:T(8,128)(2,1)}, u32[]{:S(2)}) copy-start(bf16[1,2048,176]{1,2,0:T(8,128)(2,1)} %param.25) | copy-start | bytes 2162692
  78.0 6.5 %copy-start.5 = (f32[20,6]{0,1:T(8,128)S(1)}, f32[20,6]{0,1:T(8,128)}, u32[]{:S(2)}) copy-start(f32[20,6]{0,1:T(8,128)} %param.24) | copy-start | bytes 1444
  78.0 29.3 %all-to-all-start.3 = ((bf16[64,48,128]{2,1,0:T(8,128)(2,1)}), bf16[64,48,128]{2,1,0:T(8,128)(2,1)S(1)}, u32[]{:S(2)}, u32[]{:S(2)}) async-start(bf16[64,48,128]{2,1,0:T(8,128)(2,1)} %bitcast.8), calls=%async_computation.3 | async-start | bytes 1572864 | tf_op jit(solution)/shard_map/all_to_all | solution.py:167
  108.7 11.8 %all-to-all-start.4 = ((bf16[8,40,128]{2,1,0:T(8,128)(2,1)}), bf16[8,40,128]{2,1,0:T(8,128)(2,1)S(1)}, u32[]{:S(2)}, u32[]{:S(2)}) async-start(bf16[8,40,128]{2,1,0:T(8,128)(2,1)} %copy.51), calls=%async_computation.4 | async-start | bytes 163840 | tf_op jit(solution)/shard_map/all_to_all | solution.py:113

commit v9 on v6

--- a/solution.py
+++ b/solution.py
@@ -156,7 +156,14 @@
     summed = gather_cols(summed_cols, tp_count)
     mean_square = jnp.mean(summed * summed, axis=-1, keepdims=True)
     normed = (summed * lax.rsqrt(mean_square + 1e-06) * norm_gain[None, :]).astype(jnp.bfloat16)
-    outbound = jnp.dot(dispatch, normed, preferred_element_type=jnp.float32).astype(jnp.bfloat16)
+    token_count = normed.shape[0]
+    slot_token = jnp.dot(
+        dispatch, jnp.arange(1, token_count + 1, dtype=jnp.bfloat16), preferred_element_type=jnp.float32
+    ).astype(jnp.int32)
+    row_tiles = jnp.concatenate(
+        [jnp.zeros((1, model_width // 128, 128), normed.dtype), normed.reshape(token_count, model_width // 128, 128)]
+    )
+    outbound = jnp.take(row_tiles, slot_token, axis=0, mode="clip")
     packed = (holders, CAP * model_width // 128, 128)
     outbound = outbound.reshape(packed)
     arrived = lax.all_to_all(outbound, "req", split_axis=0, concat_axis=0, tiled=True)

time: 121 us -> 121 us (level)
    gather x0 -> x1, local copies, waits for them, and re-layouts: none -> 1.63 us  [local(): outbound = jnp.take(row_tiles, slot_token, axis=0, mode='clip')]
    reshape x2 -> x0, local copies, waits for them, and re-layouts: 1.37 us -> none  [the longest x1 1.24 us: local(): outbound = outbound.reshape(packed)]
where the time goes in v9:
time: 121 us; the launch traced here: 120 us
  waiting for transfers between devices  60.7 us (50%)
  starting transfers between devices  34 us (28%)
  blocking collectives  10.9 us (9%)
  local copies, waits for them, and re-layouts  5.33 us (4%)
  Pallas kernels  3.82 us (3%)
  matrix products  2.93 us (2%)
  other arithmetic  2.36 us (2%)
    all_to_all x1, waiting for transfers between devices, local(): lax.all_to_all(produced.astype(jnp.bfloat16).reshape(packed), 'req', spli...  22.7 us
    all_to_all x1, waiting for transfers between devices, local(): lax.all_to_all(outbound, 'req', split_axis=0, concat_axis=0, tiled=True)  22.6 us
    all_to_all x1, starting transfers between devices, local(): lax.all_to_all(outbound, 'req', split_axis=0, concat_axis=0, tiled=True)  17.3 us
    all_to_all x1, blocking collectives, scatter_sum(): lax.all_to_all(pieces, 'tp', split_axis=0, concat_axis=0, tiled=True)  10.9 us
    all_to_all x1, waiting for transfers between devices, gather_cols(): lax.all_to_all(pieces, 'tp', split_axis=0, concat_axis=0, tiled=True)  8.15 us
    all_to_all x1, waiting for transfers between devices, local(): lax.all_to_all(pieces, 'tp', split_axis=0, concat_axis=0, tiled=True)  7.27 us
    all_to_all x1, starting transfers between devices, local(): lax.all_to_all(pieces, 'tp', split_axis=0, concat_axis=0, tiled=True)  6.82 us
    all_to_all x1, starting transfers between devices, local(): lax.all_to_all(produced.astype(jnp.bfloat16).reshape(packed), 'req', spli...  6.49 us
  transfers between devices with their start and end apart: 4, of which 4 were waited for; matrix products, arithmetic and copies ran while one was open for 1% of the time, Pallas kernels for 0%

profile of v9, /device:TPU:7, one launch (start us, length us, event | category | flops | bytes accessed | tf_op | source)
XLA Modules:
  0.0 120.3 jit_solution(11880738214875244985)
XLA Ops:
  0.0 3.8 %shard_map.136 = f32[8,40,128]{2,1,0:T(8,128)} custom-call(s32[4]{0:T(128)} %len_ref.1, bf16[20,256]{1,0:T(8,128)(2,1)} %q_ref.1, bf16[20,256]{1,0:T(8,128)(2,1)} %nk_ref.1, bf16[20,256]{1,0:T(8,128)(2,1)} %nv_ref.1, bf16[1536,256]{1,0:T(8,128)(2,1)} %bitcast.54, bf16[1536,256]{1,0:T(8,128)(2,1)} %bitcast.55, bf16[256,2048]{1,0:T(8,128)(2,1)} %ow_ref.1), custom_call_target="tpu_custom_call" | custom-call | tf_op jit(solution)/shard_map/pallas_call | solution.py:78
  3.8 6.8 %all-to-all-start = ((f32[8,40,128]{2,1,0:T(8,128)}), f32[8,40,128]{2,1,0:T(8,128)S(1)}, u32[]{:S(2)}, u32[]{:S(2)}) async-start(f32[8,40,128]{2,1,0:T(8,128)} %shard_map.136), calls=%async_computation | async-start | bytes 327680 | tf_op jit(solution)/shard_map/all_to_all | solution.py:154
  10.7 0.1 copy.56
  11.0 0.2 reduce_window_sum.11
  11.1 0.2 select_reduce_fusion.1
  11.3 0.1 reduce_sum.49
  11.5 0.1 fusion.7
  11.6 7.3 %all-to-all-done = f32[8,40,128]{2,1,0:T(8,128)S(1)} async-done(((f32[8,40,128]{2,1,0:T(8,128)}), f32[8,40,128]{2,1,0:T(8,128)S(1)}, u32[]{:S(2)}, u32[]{:S(2)}) %all-to-all-start) | async-done | bytes 163872 | tf_op jit(solution)/shard_map/all_to_all | solution.py:154
  18.9 0.7 maximum_add_fusion
  19.6 0.7 broadcast_in_dim.30
  20.3 3.4 %all-to-all-start.1 = ((f32[8,40,128]{2,1,0:T(8,128)}), f32[8,40,128]{2,1,0:T(8,128)S(1)}, u32[]{:S(2)}, u32[]{:S(2)}) async-start(f32[8,40,128]{2,1,0:T(8,128)} %broadcast_in_dim.30), calls=%async_computation.1 | async-start | bytes 327680 | tf_op jit(solution)/shard_map/all_to_all | solution.py:123
  23.7 0.1 fusion.11
  23.8 8.1 %all-to-all-done.1 = f32[8,40,128]{2,1,0:T(8,128)S(1)} async-done(((f32[8,40,128]{2,1,0:T(8,128)}), f32[8,40,128]{2,1,0:T(8,128)S(1)}, u32[]{:S(2)}, u32[]{:S(2)}) %all-to-all-start.1) | async-done | bytes 163872 | tf_op jit(solution)/shard_map/all_to_all | solution.py:123
  32.0 0.1 copy.59
  32.2 0.2 multiply_reduce_fusion
  32.4 0.1 multiply_convert_fusion
  32.5 1.6 %gather_fusion = bf16[192,16,128]{2,1,0:T(8,128)(2,1)} fusion(bf16[21,16,128]{2,1,0:T(8,128)(2,1)S(1)} %concatenate.14, s32[1024]{0:T(1024)S(1)} %pad_clamp_fusion), kind=kCustom, calls=%fused_computation | custom fusion | bytes 1573632 | tf_op jit(solution)/shard_map/jit(_take)/gather | solution.py:166
  34.2 17.3 %all-to-all-start.2 = ((bf16[64,48,128]{2,1,0:T(8,128)(2,1)}), bf16[64,48,128]{2,1,0:T(8,128)(2,1)S(1)}, u32[]{:S(2)}, u32[]{:S(2)}) async-start(bf16[64,48,128]{2,1,0:T(8,128)(2,1)} %bitcast.9), calls=%async_computation.2 | async-start | bytes 1572864 | tf_op jit(solution)/shard_map/all_to_all | solution.py:169
  51.5 0.1 copy.70
  51.6 22.6 %all-to-all-done.2 = bf16[64,48,128]{2,1,0:T(8,128)(2,1)S(1)} async-done(((bf16[64,48,128]{2,1,0:T(8,128)(2,1)}), bf16[64,48,128]{2,1,0:T(8,128)(2,1)S(1)}, u32[]{:S(2)}, u32[]{:S(2)}) %all-to-all-start.2) | async-done | bytes 786464 | tf_op jit(solution)/shard_map/all_to_all | solution.py:169
  74.3 0.2 reshape.84
  74.5 1.0 convolution_bitcast_fusion.1
  75.6 1.0 fusion.1
  76.8 0.4 convolution_convert_fusion.1
  77.2 1.4 %copy.65 = bf16[192,16,128]{2,1,0:T(8,128)(2,1)} copy(bf16[192,16,128]{2,0,1:T(8,128)(2,1)S(1)} %convolution_convert_fusion.1) | data formatting | bytes 1572864 | tf_op jit(solution)/shard_map/convert_element_type | solution.py:177
  78.6 6.5 %all-to-all-start.3 = ((bf16[64,48,128]{2,1,0:T(8,128)(2,1)}), bf16[64,48,128]{2,1,0:T(8,128)(2,1)S(1)}, u32[]{:S(2)}, u32[]{:S(2)}) async-start(bf16[64,48,128]{2,1,0:T(8,128)(2,1)} %bitcast.23), calls=%async_computation.3 | async-start | bytes 1572864 | tf_op jit(solution)/shard_map/all_to_all | solution.py:176
  85.1 0.1 select_reduce_fusion
  85.2 22.7 %all-to-all-done.3 = bf16[64,48,128]{2,1,0:T(8,128)(2,1)S(1)} async-done(((bf16[64,48,128]{2,1,0:T(8,128)(2,1)}), bf16[64,48,128]{2,1,0:T(8,128)(2,1)S(1)}, u32[]{:S(2)}, u32[]{:S(2)}) %all-to-all-start.3) | async-done | bytes 786464 | tf_op jit(solution)/shard_map/all_to_all | solution.py:176
  107.9 0.3 reshape.90
  108.2 0.4 convolution_convert_fusion
  108.8 10.9 %all_to_all.25 = bf16[8,40,128]{2,1,0:T(8,128)(2,1)S(1)} all-to-all(bf16[8,40,128]{2,1,0:T(8,128)(2,1)S(1)} %copy.67), channel_id=1, replica_groups=mesh['req'=64,'tp'=8] {'tp'}, dimensions={0} | all-to-all | bytes 163840 | tf_op jit(solution)/shard_map/all_to_all | solution.py:115
  119.7 0.6 fusion.10
  (32 shorter events, 0.8 us)
Async XLA Ops:
  0.0 74.5 %copy-start = (bf16[1,2048,176]{1,2,0:T(8,128)(2,1)S(1)}, bf16[1,2048,176]{1,2,0:T(8,128)(2,1)}, u32[]{:S(2)}) copy-start(bf16[1,2048,176]{1,2,0:T(8,128)(2,1)} %param.25) | copy-start | bytes 2162692
  0.0 10.7 %copy-start.2 = (s32[20,6]{0,1:T(8,128)S(1)}, s32[20,6]{0,1:T(8,128)}, u32[]{:S(2)}) copy-start(s32[20,6]{0,1:T(8,128)} %param.23) | copy-start | bytes 1444
  3.8 15.0 %all-to-all-start = ((f32[8,40,128]{2,1,0:T(8,128)}), f32[8,40,128]{2,1,0:T(8,128)S(1)}, u32[]{:S(2)}, u32[]{:S(2)}) async-start(f32[8,40,128]{2,1,0:T(8,128)} %shard_map.136), calls=%async_computation | async-start | bytes 327680 | tf_op jit(solution)/shard_map/all_to_all | solution.py:154
  10.6 21.8 %copy-start.3 = (f32[2048]{0:T(1024)S(1)}, f32[2048]{0:T(1024)}, u32[]{:S(2)}) copy-start(f32[2048]{0:T(1024)} %param.22) | copy-start | bytes 24580
  20.3 11.7 %all-to-all-start.1 = ((f32[8,40,128]{2,1,0:T(8,128)}), f32[8,40,128]{2,1,0:T(8,128)S(1)}, u32[]{:S(2)}, u32[]{:S(2)}) async-start(f32[8,40,128]{2,1,0:T(8,128)} %broadcast_in_dim.30), calls=%async_computation.1 | async-start | bytes 327680 | tf_op jit(solution)/shard_map/all_to_all | solution.py:123
  34.2 17.3 %copy-start.1 = (bf16[1,176,2048]{2,1,0:T(8,128)(2,1)S(1)}, bf16[1,176,2048]{2,1,0:T(8,128)(2,1)}, u32[]{:S(2)}) copy-start(bf16[1,176,2048]{2,1,0:T(8,128)(2,1)} %param.27) | copy-start | bytes 2162692
  34.2 40.1 %all-to-all-start.2 = ((bf16[64,48,128]{2,1,0:T(8,128)(2,1)}), bf16[64,48,128]{2,1,0:T(8,128)(2,1)S(1)}, u32[]{:S(2)}, u32[]{:S(2)}) async-start(bf16[64,48,128]{2,1,0:T(8,128)(2,1)} %bitcast.9), calls=%async_computation.2 | async-start | bytes 1572864 | tf_op jit(solution)/shard_map/all_to_all | solution.py:169
  74.5 1.1 copy-start.5
  78.6 6.5 %copy-start.4 = (f32[20,6]{0,1:T(8,128)S(1)}, f32[20,6]{0,1:T(8,128)}, u32[]{:S(2)}) copy-start(f32[20,6]{0,1:T(8,128)} %param.24) | copy-start | bytes 1444
  78.6 29.3 %all-to-all-start.3 = ((bf16[64,48,128]{2,1,0:T(8,128)(2,1)}), bf16[64,48,128]{2,1,0:T(8,128)(2,1)S(1)}, u32[]{:S(2)}, u32[]{:S(2)}) async-start(bf16[64,48,128]{2,1,0:T(8,128)(2,1)} %bitcast.23), calls=%async_computation.3 | async-start | bytes 1572864 | tf_op jit(solution)/shard_map/all_to_all | solution.py:176

commit v10 on v9

--- a/solution.py
+++ b/solution.py
@@ -23,7 +23,7 @@
     matches = slot_ids[None, :, :] == slot_range[:, None, None]
     dispatch = jnp.any(matches, axis=-1).astype(jnp.bfloat16)
     combine = jnp.sum(jnp.where(matches, local_gates[None, :, :], 0.0), axis=-1).T
-    return (dispatch, combine)
+    return (dispatch, combine, slot_ids)
 
 
 def attend_project(queries, new_keys, new_values, cache_keys, cache_values, cache_lengths, out_weight, tp_count):
@@ -149,7 +149,7 @@
     columns = model_width // tp_count
     offset = lax.axis_index("tp") * columns
     holders = lax.axis_size("req")
-    dispatch, combine = slot_tables(routes, route_gates)
+    dispatch, combine, slot_ids = slot_tables(routes, route_gates)
     hidden_cols = lax.dynamic_slice_in_dim(hidden_in, offset, columns, 1).astype(jnp.float32)
     pieces = lax.all_to_all(pieces, "tp", split_axis=0, concat_axis=0, tiled=True)
     summed_cols = unstack_halves(jnp.sum(pieces, axis=0)) + hidden_cols
@@ -175,13 +175,12 @@
     )
     returned = lax.all_to_all(
         produced.astype(jnp.bfloat16).reshape(packed), "req", split_axis=0, concat_axis=0, tiled=True
-    ).astype(jnp.float32)
-    expert_sum = jnp.dot(
-        combine,
-        returned.reshape(-1, model_width),
-        precision=lax.Precision.HIGHEST,
-        preferred_element_type=jnp.float32,
-    )
+    )
+    route_rows = jnp.take(
+        returned.reshape(holders * CAP, model_width // 128, 128), slot_ids.reshape(-1), axis=0, mode="clip"
+    )
+    route_rows = route_rows.reshape(routes.shape + (model_width // 128, 128)).astype(jnp.float32)
+    expert_sum = jnp.sum(route_rows * route_gates[:, :, None, None], axis=1).reshape(-1, model_width)
     expert_cols = scatter_sum(expert_sum.astype(jnp.bfloat16), tp_count)
     return (summed_cols + expert_cols).astype(jnp.bfloat16)
 

time: 121 us -> 121 us (level)
  no operation moved by 1% of the time
where the time goes in v10:
time: 121 us; the launch traced here: 120 us
  waiting for transfers between devices  60.6 us (50%)
  starting transfers between devices  34 us (28%)
  blocking collectives  10.9 us (9%)
  local copies, waits for them, and re-layouts  5.83 us (5%)
  Pallas kernels  3.82 us (3%)
  matrix products  2.52 us (2%)
  other arithmetic  2.44 us (2%)
    all_to_all x1, waiting for transfers between devices, local(): lax.all_to_all(outbound, 'req', split_axis=0, concat_axis=0, tiled=True)  22.6 us
    all_to_all x1, waiting for transfers between devices, local(): lax.all_to_all(produced.astype(jnp.bfloat16).reshape(packed), 'req', spli...  22.6 us
    all_to_all x1, starting transfers between devices, local(): lax.all_to_all(outbound, 'req', split_axis=0, concat_axis=0, tiled=True)  17.3 us
    all_to_all x1, blocking collectives, scatter_sum(): lax.all_to_all(pieces, 'tp', split_axis=0, concat_axis=0, tiled=True)  10.9 us
    all_to_all x1, waiting for transfers between devices, gather_cols(): lax.all_to_all(pieces, 'tp', split_axis=0, concat_axis=0, tiled=True)  8.15 us
    all_to_all x1, waiting for transfers between devices, local(): lax.all_to_all(pieces, 'tp', split_axis=0, concat_axis=0, tiled=True)  7.27 us
    all_to_all x1, starting transfers between devices, local(): lax.all_to_all(pieces, 'tp', split_axis=0, concat_axis=0, tiled=True)  6.82 us
    all_to_all x1, starting transfers between devices, local(): lax.all_to_all(produced.astype(jnp.bfloat16).reshape(packed), 'req', spli...  6.49 us
  transfers between devices with their start and end apart: 4, of which 4 were waited for; matrix products, arithmetic and copies ran while one was open for 1% of the time, Pallas kernels for 0%

profile of v10, /device:TPU:7, one launch (start us, length us, event | category | flops | bytes accessed | tf_op | source)
XLA Modules:
  0.0 120.4 jit_solution(9002162540629654114)
XLA Ops:
  0.0 3.8 %shard_map.136 = f32[8,40,128]{2,1,0:T(8,128)} custom-call(s32[4]{0:T(128)} %len_ref.1, bf16[20,256]{1,0:T(8,128)(2,1)} %q_ref.1, bf16[20,256]{1,0:T(8,128)(2,1)} %nk_ref.1, bf16[20,256]{1,0:T(8,128)(2,1)} %nv_ref.1, bf16[1536,256]{1,0:T(8,128)(2,1)} %bitcast.64, bf16[1536,256]{1,0:T(8,128)(2,1)} %bitcast.65, bf16[256,2048]{1,0:T(8,128)(2,1)} %ow_ref.1), custom_call_target="tpu_custom_call" | custom-call | tf_op jit(solution)/shard_map/pallas_call | solution.py:78
  3.8 6.8 %all-to-all-start = ((f32[8,40,128]{2,1,0:T(8,128)}), f32[8,40,128]{2,1,0:T(8,128)S(1)}, u32[]{:S(2)}, u32[]{:S(2)}) async-start(f32[8,40,128]{2,1,0:T(8,128)} %shard_map.136), calls=%async_computation | async-start | bytes 327680 | tf_op jit(solution)/shard_map/all_to_all | solution.py:154
  10.7 0.1 copy.55
  10.9 0.2 reduce_window_sum.11
  11.1 0.2 select_reduce_fusion
  11.3 0.1 reduce_sum.52
  11.5 0.1 fusion.8
  11.6 7.3 %all-to-all-done = f32[8,40,128]{2,1,0:T(8,128)S(1)} async-done(((f32[8,40,128]{2,1,0:T(8,128)}), f32[8,40,128]{2,1,0:T(8,128)S(1)}, u32[]{:S(2)}, u32[]{:S(2)}) %all-to-all-start) | async-done | bytes 163872 | tf_op jit(solution)/shard_map/all_to_all | solution.py:154
  18.9 0.7 maximum_add_fusion
  19.6 0.7 broadcast_in_dim.6
  20.3 3.4 %all-to-all-start.1 = ((f32[8,40,128]{2,1,0:T(8,128)}), f32[8,40,128]{2,1,0:T(8,128)S(1)}, u32[]{:S(2)}, u32[]{:S(2)}) async-start(f32[8,40,128]{2,1,0:T(8,128)} %broadcast_in_dim.6), calls=%async_computation.1 | async-start | bytes 327680 | tf_op jit(solution)/shard_map/all_to_all | solution.py:123
  23.7 0.1 fusion.13
  23.8 8.1 %all-to-all-done.1 = f32[8,40,128]{2,1,0:T(8,128)S(1)} async-done(((f32[8,40,128]{2,1,0:T(8,128)}), f32[8,40,128]{2,1,0:T(8,128)S(1)}, u32[]{:S(2)}, u32[]{:S(2)}) %all-to-all-start.1) | async-done | bytes 163872 | tf_op jit(solution)/shard_map/all_to_all | solution.py:123
  32.0 0.1 copy.54
  32.2 0.2 multiply_reduce_fusion
  32.4 0.1 multiply_convert_fusion
  32.5 1.6 %gather_fusion = bf16[192,16,128]{2,1,0:T(8,128)(2,1)} fusion(bf16[21,16,128]{2,1,0:T(8,128)(2,1)S(1)} %concatenate.14, s32[1024]{0:T(1024)S(1)} %pad_clamp_fusion.1), kind=kCustom, calls=%fused_computation | custom fusion | bytes 1573632 | tf_op jit(solution)/shard_map/jit(_take)/gather | solution.py:166
  34.2 17.3 %all-to-all-start.2 = ((bf16[64,48,128]{2,1,0:T(8,128)(2,1)}), bf16[64,48,128]{2,1,0:T(8,128)(2,1)S(1)}, u32[]{:S(2)}, u32[]{:S(2)}) async-start(bf16[64,48,128]{2,1,0:T(8,128)(2,1)} %bitcast.9), calls=%async_computation.2 | async-start | bytes 1572864 | tf_op jit(solution)/shard_map/all_to_all | solution.py:169
  51.5 0.1 copy.69
  51.6 22.6 %all-to-all-done.2 = bf16[64,48,128]{2,1,0:T(8,128)(2,1)S(1)} async-done(((bf16[64,48,128]{2,1,0:T(8,128)(2,1)}), bf16[64,48,128]{2,1,0:T(8,128)(2,1)S(1)}, u32[]{:S(2)}, u32[]{:S(2)}) %all-to-all-start.2) | async-done | bytes 786464 | tf_op jit(solution)/shard_map/all_to_all | solution.py:169
  74.3 0.2 reshape.107
  74.5 1.0 convolution_bitcast_fusion.1
  75.6 1.0 fusion.1
  76.8 0.4 convolution_convert_fusion
  77.2 1.4 %copy.63 = bf16[192,16,128]{2,1,0:T(8,128)(2,1)} copy(bf16[192,16,128]{2,0,1:T(8,128)(2,1)S(1)} %convolution_convert_fusion) | data formatting | bytes 1572864 | tf_op jit(solution)/shard_map/convert_element_type | solution.py:177
  78.6 6.5 %all-to-all-start.3 = ((bf16[64,48,128]{2,1,0:T(8,128)(2,1)}), bf16[64,48,128]{2,1,0:T(8,128)(2,1)S(1)}, u32[]{:S(2)}, u32[]{:S(2)}) async-start(bf16[64,48,128]{2,1,0:T(8,128)(2,1)} %bitcast.23), calls=%async_computation.3 | async-start | bytes 1572864 | tf_op jit(solution)/shard_map/all_to_all | solution.py:176
  85.2 0.1 copy.64
  85.3 22.6 %all-to-all-done.3 = bf16[64,48,128]{2,1,0:T(8,128)(2,1)S(1)} async-done(((bf16[64,48,128]{2,1,0:T(8,128)(2,1)}), bf16[64,48,128]{2,1,0:T(8,128)(2,1)S(1)}, u32[]{:S(2)}, u32[]{:S(2)}) %all-to-all-start.3) | async-done | bytes 786464 | tf_op jit(solution)/shard_map/all_to_all | solution.py:176
  107.9 0.7 gather_fusion.1
  108.6 0.2 fusion.2
  108.9 10.9 %all_to_all.25 = bf16[8,40,128]{2,1,0:T(8,128)(2,1)S(1)} all-to-all(bf16[8,40,128]{2,1,0:T(8,128)(2,1)S(1)} %copy.66), channel_id=1, replica_groups=mesh['req'=64,'tp'=8] {'tp'}, dimensions={0} | all-to-all | bytes 163840 | tf_op jit(solution)/shard_map/all_to_all | solution.py:115
  119.8 0.6 fusion.11
  (34 shorter events, 0.8 us)
Async XLA Ops:
  0.0 74.5 %copy-start = (bf16[1,2048,176]{1,2,0:T(8,128)(2,1)S(1)}, bf16[1,2048,176]{1,2,0:T(8,128)(2,1)}, u32[]{:S(2)}) copy-start(bf16[1,2048,176]{1,2,0:T(8,128)(2,1)} %param.25) | copy-start | bytes 2162692
  0.0 10.6 %copy-start.3 = (s32[20,6]{0,1:T(8,128)S(1)}, s32[20,6]{0,1:T(8,128)}, u32[]{:S(2)}) copy-start(s32[20,6]{0,1:T(8,128)} %param.23) | copy-start | bytes 1444
  3.8 15.0 %all-to-all-start = ((f32[8,40,128]{2,1,0:T(8,128)}), f32[8,40,128]{2,1,0:T(8,128)S(1)}, u32[]{:S(2)}, u32[]{:S(2)}) async-start(f32[8,40,128]{2,1,0:T(8,128)} %shard_map.136), calls=%async_computation | async-start | bytes 327680 | tf_op jit(solution)/shard_map/all_to_all | solution.py:154
  10.8 21.6 %copy-start.2 = (f32[2048]{0:T(1024)S(1)}, f32[2048]{0:T(1024)}, u32[]{:S(2)}) copy-start(f32[2048]{0:T(1024)} %param.22) | copy-start | bytes 24580
  20.3 11.7 %all-to-all-start.1 = ((f32[8,40,128]{2,1,0:T(8,128)}), f32[8,40,128]{2,1,0:T(8,128)S(1)}, u32[]{:S(2)}, u32[]{:S(2)}) async-start(f32[8,40,128]{2,1,0:T(8,128)} %broadcast_in_dim.6), calls=%async_computation.1 | async-start | bytes 327680 | tf_op jit(solution)/shard_map/all_to_all | solution.py:123
  34.1 17.3 %copy-start.1 = (bf16[1,176,2048]{2,1,0:T(8,128)(2,1)S(1)}, bf16[1,176,2048]{2,1,0:T(8,128)(2,1)}, u32[]{:S(2)}) copy-start(bf16[1,176,2048]{2,1,0:T(8,128)(2,1)} %param.27) | copy-start | bytes 2162692
  34.2 40.1 %all-to-all-start.2 = ((bf16[64,48,128]{2,1,0:T(8,128)(2,1)}), bf16[64,48,128]{2,1,0:T(8,128)(2,1)S(1)}, u32[]{:S(2)}, u32[]{:S(2)}) async-start(bf16[64,48,128]{2,1,0:T(8,128)(2,1)} %bitcast.9), calls=%async_computation.2 | async-start | bytes 1572864 | tf_op jit(solution)/shard_map/all_to_all | solution.py:169
  74.5 1.1 copy-start.5
  78.6 6.6 %copy-start.4 = (f32[20,6]{0,1:T(8,128)S(1)}, f32[20,6]{0,1:T(8,128)}, u32[]{:S(2)}) copy-start(f32[20,6]{0,1:T(8,128)} %param.24) | copy-start | bytes 1444
  78.6 29.3 %all-to-all-start.3 = ((bf16[64,48,128]{2,1,0:T(8,128)(2,1)}), bf16[64,48,128]{2,1,0:T(8,128)(2,1)S(1)}, u32[]{:S(2)}, u32[]{:S(2)}) async-start(bf16[64,48,128]{2,1,0:T(8,128)(2,1)} %bitcast.23), calls=%async_computation.3 | async-start | bytes 1572864 | tf_op jit(solution)/shard_map/all_to_all | solution.py:176

commit v11 on v7

--- a/solution.py
+++ b/solution.py
@@ -171,7 +171,14 @@
     summed = gather_cols(summed_cols, tp_count)
     mean_square = jnp.mean(summed * summed, axis=-1, keepdims=True)
     normed = (summed * lax.rsqrt(mean_square + 1e-06) * norm_gain[None, :]).astype(jnp.bfloat16)
-    outbound = jnp.dot(dispatch, normed, preferred_element_type=jnp.float32).astype(jnp.bfloat16)
+    token_count = normed.shape[0]
+    slot_token = jnp.dot(
+        dispatch, jnp.arange(1, token_count + 1, dtype=jnp.bfloat16), preferred_element_type=jnp.float32
+    ).astype(jnp.int32)
+    row_tiles = jnp.concatenate(
+        [jnp.zeros((1, model_width // 128, 128), normed.dtype), normed.reshape(token_count, model_width // 128, 128)]
+    )
+    outbound = jnp.take(row_tiles, slot_token, axis=0, mode="clip")
     packed = (holders, CAP * model_width // 128, 128)
     outbound = outbound.reshape(packed)
     arrived = lax.all_to_all(outbound, "req", split_axis=0, concat_axis=0, tiled=True)

time: 121 us -> 121 us (level)
    gather x0 -> x1, local copies, waits for them, and re-layouts: none -> 1.63 us  [local(): outbound = jnp.take(row_tiles, slot_token, axis=0, mode='clip')]
    reshape x2 -> x0, local copies, waits for them, and re-layouts: 1.37 us -> none  [the longest x1 1.24 us: local(): outbound = outbound.reshape(packed)]
where the time goes in v11:
time: 121 us; the launch traced here: 120 us
  waiting for transfers between devices  60.7 us (50%)
  starting transfers between devices  34 us (28%)
  blocking collectives  10.9 us (9%)
  local copies, waits for them, and re-layouts  5.32 us (4%)
  Pallas kernels  3.7 us (3%)
  matrix products  2.94 us (2%)
  other arithmetic  2.36 us (2%)
    all_to_all x1, waiting for transfers between devices, local(): lax.all_to_all(produced.astype(jnp.bfloat16).reshape(packed), 'req', spli...  22.7 us
    all_to_all x1, waiting for transfers between devices, local(): lax.all_to_all(outbound, 'req', split_axis=0, concat_axis=0, tiled=True)  22.6 us
    all_to_all x1, starting transfers between devices, local(): lax.all_to_all(outbound, 'req', split_axis=0, concat_axis=0, tiled=True)  17.3 us
    all_to_all x1, blocking collectives, scatter_sum(): lax.all_to_all(pieces, 'tp', split_axis=0, concat_axis=0, tiled=True)  10.9 us
    all_to_all x1, waiting for transfers between devices, gather_cols(): lax.all_to_all(pieces, 'tp', split_axis=0, concat_axis=0, tiled=True)  8.15 us
    all_to_all x1, waiting for transfers between devices, local(): lax.all_to_all(pieces, 'tp', split_axis=0, concat_axis=0, tiled=True)  7.28 us
    all_to_all x1, starting transfers between devices, local(): lax.all_to_all(pieces, 'tp', split_axis=0, concat_axis=0, tiled=True)  6.82 us
    all_to_all x1, starting transfers between devices, local(): lax.all_to_all(produced.astype(jnp.bfloat16).reshape(packed), 'req', spli...  6.48 us
  transfers between devices with their start and end apart: 4, of which 4 were waited for; matrix products, arithmetic and copies ran while one was open for 1% of the time, Pallas kernels for 0%

profile of v11, /device:TPU:7, one launch (start us, length us, event | category | flops | bytes accessed | tf_op | source)
XLA Modules:
  0.0 120.2 jit_solution(16985422130395170745)
XLA Ops:
  0.0 3.7 %shard_map.136 = f32[8,40,128]{2,1,0:T(8,128)} custom-call(s32[4]{0:T(128)} %len_ref.1, bf16[20,256]{1,0:T(8,128)(2,1)} %q_ref.1, bf16[20,256]{1,0:T(8,128)(2,1)} %nk_ref.1, bf16[20,256]{1,0:T(8,128)(2,1)} %nv_ref.1, bf16[1536,256]{1,0:T(8,128)(2,1)} %bitcast.54, bf16[1536,256]{1,0:T(8,128)(2,1)} %bitcast.55, bf16[256,2048]{1,0:T(8,128)(2,1)} %ow_ref.1), custom_call_target="tpu_custom_call" | custom-call | tf_op jit(solution)/shard_map/pallas_call | solution.py:84
  3.7 6.8 %all-to-all-start = ((f32[8,40,128]{2,1,0:T(8,128)}), f32[8,40,128]{2,1,0:T(8,128)S(1)}, u32[]{:S(2)}, u32[]{:S(2)}) async-start(f32[8,40,128]{2,1,0:T(8,128)} %shard_map.136), calls=%async_computation | async-start | bytes 327680 | tf_op jit(solution)/shard_map/all_to_all | solution.py:169
  10.5 0.1 copy.56
  10.8 0.2 reduce_window_sum.11
  11.0 0.2 select_reduce_fusion.1
  11.2 0.1 reduce_sum.49
  11.4 0.1 fusion.7
  11.5 7.3 %all-to-all-done = f32[8,40,128]{2,1,0:T(8,128)S(1)} async-done(((f32[8,40,128]{2,1,0:T(8,128)}), f32[8,40,128]{2,1,0:T(8,128)S(1)}, u32[]{:S(2)}, u32[]{:S(2)}) %all-to-all-start) | async-done | bytes 163872 | tf_op jit(solution)/shard_map/all_to_all | solution.py:169
  18.8 0.7 maximum_add_fusion
  19.5 0.7 broadcast_in_dim.30
  20.2 3.4 %all-to-all-start.1 = ((f32[8,40,128]{2,1,0:T(8,128)}), f32[8,40,128]{2,1,0:T(8,128)S(1)}, u32[]{:S(2)}, u32[]{:S(2)}) async-start(f32[8,40,128]{2,1,0:T(8,128)} %broadcast_in_dim.30), calls=%async_computation.1 | async-start | bytes 327680 | tf_op jit(solution)/shard_map/all_to_all | solution.py:138
  23.6 0.1 fusion.11
  23.7 8.1 %all-to-all-done.1 = f32[8,40,128]{2,1,0:T(8,128)S(1)} async-done(((f32[8,40,128]{2,1,0:T(8,128)}), f32[8,40,128]{2,1,0:T(8,128)S(1)}, u32[]{:S(2)}, u32[]{:S(2)}) %all-to-all-start.1) | async-done | bytes 163872 | tf_op jit(solution)/shard_map/all_to_all | solution.py:138
  31.9 0.1 copy.59
  32.0 0.2 multiply_reduce_fusion
  32.3 0.1 multiply_convert_fusion
  32.4 1.6 %gather_fusion = bf16[192,16,128]{2,1,0:T(8,128)(2,1)} fusion(bf16[21,16,128]{2,1,0:T(8,128)(2,1)S(1)} %concatenate.14, s32[1024]{0:T(1024)S(1)} %pad_clamp_fusion), kind=kCustom, calls=%fused_computation | custom fusion | bytes 1573632 | tf_op jit(solution)/shard_map/jit(_take)/gather | solution.py:181
  34.0 17.3 %all-to-all-start.2 = ((bf16[64,48,128]{2,1,0:T(8,128)(2,1)}), bf16[64,48,128]{2,1,0:T(8,128)(2,1)S(1)}, u32[]{:S(2)}, u32[]{:S(2)}) async-start(bf16[64,48,128]{2,1,0:T(8,128)(2,1)} %bitcast.9), calls=%async_computation.2 | async-start | bytes 1572864 | tf_op jit(solution)/shard_map/all_to_all | solution.py:184
  51.4 0.1 copy.70
  51.5 22.6 %all-to-all-done.2 = bf16[64,48,128]{2,1,0:T(8,128)(2,1)S(1)} async-done(((bf16[64,48,128]{2,1,0:T(8,128)(2,1)}), bf16[64,48,128]{2,1,0:T(8,128)(2,1)S(1)}, u32[]{:S(2)}, u32[]{:S(2)}) %all-to-all-start.2) | async-done | bytes 786464 | tf_op jit(solution)/shard_map/all_to_all | solution.py:184
  74.1 0.2 reshape.84
  74.4 1.0 convolution_bitcast_fusion.1
  75.5 1.0 fusion.1
  76.7 0.4 convolution_convert_fusion.1
  77.1 1.4 %copy.65 = bf16[192,16,128]{2,1,0:T(8,128)(2,1)} copy(bf16[192,16,128]{2,0,1:T(8,128)(2,1)S(1)} %convolution_convert_fusion.1) | data formatting | bytes 1572864 | tf_op jit(solution)/shard_map/convert_element_type | solution.py:192
  78.5 6.5 %all-to-all-start.3 = ((bf16[64,48,128]{2,1,0:T(8,128)(2,1)}), bf16[64,48,128]{2,1,0:T(8,128)(2,1)S(1)}, u32[]{:S(2)}, u32[]{:S(2)}) async-start(bf16[64,48,128]{2,1,0:T(8,128)(2,1)} %bitcast.23), calls=%async_computation.3 | async-start | bytes 1572864 | tf_op jit(solution)/shard_map/all_to_all | solution.py:191
  85.0 0.1 select_reduce_fusion
  85.1 22.7 %all-to-all-done.3 = bf16[64,48,128]{2,1,0:T(8,128)(2,1)S(1)} async-done(((bf16[64,48,128]{2,1,0:T(8,128)(2,1)}), bf16[64,48,128]{2,1,0:T(8,128)(2,1)S(1)}, u32[]{:S(2)}, u32[]{:S(2)}) %all-to-all-start.3) | async-done | bytes 786464 | tf_op jit(solution)/shard_map/all_to_all | solution.py:191
  107.8 0.3 reshape.90
  108.1 0.4 convolution_convert_fusion
  108.6 10.9 %all_to_all.25 = bf16[8,40,128]{2,1,0:T(8,128)(2,1)S(1)} all-to-all(bf16[8,40,128]{2,1,0:T(8,128)(2,1)S(1)} %copy.67), channel_id=1, replica_groups=mesh['req'=64,'tp'=8] {'tp'}, dimensions={0} | all-to-all | bytes 163840 | tf_op jit(solution)/shard_map/all_to_all | solution.py:130
  119.5 0.6 fusion.10
  (32 shorter events, 0.8 us)
Async XLA Ops:
  0.0 74.4 %copy-start = (bf16[1,2048,176]{1,2,0:T(8,128)(2,1)S(1)}, bf16[1,2048,176]{1,2,0:T(8,128)(2,1)}, u32[]{:S(2)}) copy-start(bf16[1,2048,176]{1,2,0:T(8,128)(2,1)} %param.25) | copy-start | bytes 2162692
  0.0 10.5 %copy-start.2 = (s32[20,6]{0,1:T(8,128)S(1)}, s32[20,6]{0,1:T(8,128)}, u32[]{:S(2)}) copy-start(s32[20,6]{0,1:T(8,128)} %param.23) | copy-start | bytes 1444
  3.7 15.0 %all-to-all-start = ((f32[8,40,128]{2,1,0:T(8,128)}), f32[8,40,128]{2,1,0:T(8,128)S(1)}, u32[]{:S(2)}, u32[]{:S(2)}) async-start(f32[8,40,128]{2,1,0:T(8,128)} %shard_map.136), calls=%async_computation | async-start | bytes 327680 | tf_op jit(solution)/shard_map/all_to_all | solution.py:169
  10.5 21.8 %copy-start.3 = (f32[2048]{0:T(1024)S(1)}, f32[2048]{0:T(1024)}, u32[]{:S(2)}) copy-start(f32[2048]{0:T(1024)} %param.22) | copy-start | bytes 24580
  20.2 11.7 %all-to-all-start.1 = ((f32[8,40,128]{2,1,0:T(8,128)}), f32[8,40,128]{2,1,0:T(8,128)S(1)}, u32[]{:S(2)}, u32[]{:S(2)}) async-start(f32[8,40,128]{2,1,0:T(8,128)} %broadcast_in_dim.30), calls=%async_computation.1 | async-start | bytes 327680 | tf_op jit(solution)/shard_map/all_to_all | solution.py:138
  34.0 17.3 %copy-start.1 = (bf16[1,176,2048]{2,1,0:T(8,128)(2,1)S(1)}, bf16[1,176,2048]{2,1,0:T(8,128)(2,1)}, u32[]{:S(2)}) copy-start(bf16[1,176,2048]{2,1,0:T(8,128)(2,1)} %param.27) | copy-start | bytes 2162692
  34.0 40.1 %all-to-all-start.2 = ((bf16[64,48,128]{2,1,0:T(8,128)(2,1)}), bf16[64,48,128]{2,1,0:T(8,128)(2,1)S(1)}, u32[]{:S(2)}, u32[]{:S(2)}) async-start(bf16[64,48,128]{2,1,0:T(8,128)(2,1)} %bitcast.9), calls=%async_computation.2 | async-start | bytes 1572864 | tf_op jit(solution)/shard_map/all_to_all | solution.py:184
  74.4 1.1 copy-start.5
  78.5 6.5 %copy-start.4 = (f32[20,6]{0,1:T(8,128)S(1)}, f32[20,6]{0,1:T(8,128)}, u32[]{:S(2)}) copy-start(f32[20,6]{0,1:T(8,128)} %param.24) | copy-start | bytes 1444
  78.5 29.3 %all-to-all-start.3 = ((bf16[64,48,128]{2,1,0:T(8,128)(2,1)}), bf16[64,48,128]{2,1,0:T(8,128)(2,1)S(1)}, u32[]{:S(2)}, u32[]{:S(2)}) async-start(bf16[64,48,128]{2,1,0:T(8,128)(2,1)} %bitcast.23), calls=%async_computation.3 | async-start | bytes 1572864 | tf_op jit(solution)/shard_map/all_to_all | solution.py:191

commit v12 on v9

--- a/solution.py
+++ b/solution.py
@@ -26,7 +26,7 @@
     return (dispatch, combine)
 
 
-def attend_project(queries, new_keys, new_values, cache_keys, cache_values, cache_lengths, out_weight, tp_count):
+def attend_project(queries, new_keys, new_values, cache_keys, cache_values, cache_lengths, out_weight, tp_count, hidden_in, me):
     req_count, cache_len, width = cache_keys.shape
     tokens = queries.shape[0]
     model_width = out_weight.shape[1]
@@ -35,7 +35,7 @@
     flat_k = cache_keys.reshape(req_count * cache_len, width)
     flat_v = cache_values.reshape(req_count * cache_len, width)
 
-    def kernel(len_ref, q_ref, nk_ref, nv_ref, ck_ref, cv_ref, ow_ref, out_ref):
+    def kernel(len_ref, me_ref, q_ref, nk_ref, nv_ref, ck_ref, cv_ref, ow_ref, hid_ref, out_ref):
         row = lax.broadcasted_iota(jnp.int32, (tokens, 1), 0)
         lo = jnp.zeros((tokens, 1), jnp.int32)
         hi = jnp.zeros((tokens, 1), jnp.int32)
@@ -71,16 +71,19 @@
         partial = jnp.dot(attended, ow_ref[...], preferred_element_type=jnp.float32)
         half = columns // 2
         for k in range(tp_count):
-            out_ref[k, 0:tokens, :] = partial[:, k * columns:k * columns + half]
-            out_ref[k, tokens:2 * tokens, :] = partial[:, k * columns + half:(k + 1) * columns]
+            own = jnp.where(me_ref[0] == k, 1.0, 0.0)
+            lo_cols = slice(k * columns, k * columns + half)
+            hi_cols = slice(k * columns + half, (k + 1) * columns)
+            out_ref[k, 0:tokens, :] = partial[:, lo_cols] + own * hid_ref[:, lo_cols].astype(jnp.float32)
+            out_ref[k, tokens:2 * tokens, :] = partial[:, hi_cols] + own * hid_ref[:, hi_cols].astype(jnp.float32)
 
     vmem = pl.BlockSpec(memory_space=pltpu.VMEM)
     return pl.pallas_call(
         kernel,
         out_shape=jax.ShapeDtypeStruct((tp_count, 2 * tokens, columns // 2), jnp.float32),
-        in_specs=[pl.BlockSpec(memory_space=pltpu.SMEM)] + [vmem] * 6,
+        in_specs=[pl.BlockSpec(memory_space=pltpu.SMEM)] * 2 + [vmem] * 7,
         out_specs=vmem,
-    )(cache_lengths, queries, new_keys, new_values, flat_k, flat_v, out_weight)
+    )(cache_lengths, me, queries, new_keys, new_values, flat_k, flat_v, out_weight, hidden_in)
 
 
 def expert_apply(slot_rows, gate_weight, up_weight, down_weight):
@@ -144,7 +147,8 @@
     model_width = out_weight.shape[1]
     tp_count = lax.axis_size("tp")
     pieces = attend_project(
-        queries, new_keys, new_values, cache_keys, cache_values, cache_lengths, out_weight, tp_count
+        queries, new_keys, new_values, cache_keys, cache_values, cache_lengths, out_weight, tp_count,
+        hidden_in, lax.axis_index("tp").astype(jnp.int32).reshape(1),
     )
     columns = model_width // tp_count
     offset = lax.axis_index("tp") * columns
@@ -152,7 +156,7 @@
     dispatch, combine = slot_tables(routes, route_gates)
     hidden_cols = lax.dynamic_slice_in_dim(hidden_in, offset, columns, 1).astype(jnp.float32)
     pieces = lax.all_to_all(pieces, "tp", split_axis=0, concat_axis=0, tiled=True)
-    summed_cols = unstack_halves(jnp.sum(pieces, axis=0)) + hidden_cols
+    summed_cols = unstack_halves(jnp.sum(pieces, axis=0))
     summed = gather_cols(summed_cols, tp_count)
     mean_square = jnp.mean(summed * summed, axis=-1, keepdims=True)
     normed = (summed * lax.rsqrt(mean_square + 1e-06) * norm_gain[None, :]).astype(jnp.bfloat16)

time: 121 us -> 122 us (level)
  blocking collectives: 10.9 us -> 0 us
  waiting for transfers between devices: 60.7 us -> 69.1 us
  starting transfers between devices: 34 us -> 37.5 us
    all_to_all x1 -> x0, blocking collectives: 10.9 us -> none  [scatter_sum(): lax.all_to_all(pieces, 'tp', split_axis=0, concat_axis=0, tiled=True)]
    all_to_all x0 -> x1, waiting for transfers between devices: none -> 8.42 us  [scatter_sum(): lax.all_to_all(pieces, 'tp', split_axis=0, concat_axis=0, tiled=True)]
    all_to_all x0 -> x1, starting transfers between devices: none -> 3.36 us  [scatter_sum(): lax.all_to_all(pieces, 'tp', split_axis=0, concat_axis=0, tiled=True)]
  transfers between devices with their start and end apart: 4 -> 5, of which waited for: 4 -> 5; matrix products, arithmetic and copies ran while one was open for 1% -> 1% of each run, Pallas kernels for 0% -> 0%
where the time goes in v12:
time: 122 us; the launch traced here: 121 us
  waiting for transfers between devices  69.1 us (57%)
  starting transfers between devices  37.5 us (31%)
  local copies, waits for them, and re-layouts  5.94 us (5%)
  Pallas kernels  3.81 us (3%)
  matrix products  2.94 us (2%)
  other arithmetic  1.62 us (1%)
    all_to_all x1, waiting for transfers between devices, local(): lax.all_to_all(produced.astype(jnp.bfloat16).reshape(packed), 'req', spli...  22.7 us
    all_to_all x1, waiting for transfers between devices, local(): lax.all_to_all(outbound, 'req', split_axis=0, concat_axis=0, tiled=True)  22.6 us
    all_to_all x1, starting transfers between devices, local(): lax.all_to_all(outbound, 'req', split_axis=0, concat_axis=0, tiled=True)  17.3 us
    all_to_all x1, waiting for transfers between devices, scatter_sum(): lax.all_to_all(pieces, 'tp', split_axis=0, concat_axis=0, tiled=True)  8.42 us
    all_to_all x1, waiting for transfers between devices, gather_cols(): lax.all_to_all(pieces, 'tp', split_axis=0, concat_axis=0, tiled=True)  8.15 us
    all_to_all x1, waiting for transfers between devices, local(): lax.all_to_all(pieces, 'tp', split_axis=0, concat_axis=0, tiled=True)  7.29 us
    all_to_all x1, starting transfers between devices, local(): lax.all_to_all(pieces, 'tp', split_axis=0, concat_axis=0, tiled=True)  6.95 us
    all_to_all x1, starting transfers between devices, local(): lax.all_to_all(produced.astype(jnp.bfloat16).reshape(packed), 'req', spli...  6.49 us
  transfers between devices with their start and end apart: 5, of which 5 were waited for; matrix products, arithmetic and copies ran while one was open for 1% of the time, Pallas kernels for 0%

profile of v12, /device:TPU:7, one launch (start us, length us, event | category | flops | bytes accessed | tf_op | source)
XLA Modules:
  0.0 121.2 jit_solution(964882054023397392)
XLA Ops:
  0.0 3.8 %shard_map.136 = f32[8,40,128]{2,1,0:T(8,128)} custom-call(s32[4]{0:T(128)} %len_ref.1, s32[1]{0:T(128)} %bitcast.me_ref, bf16[20,256]{1,0:T(8,128)(2,1)} %q_ref.1, bf16[20,256]{1,0:T(8,128)(2,1)} %nk_ref.1, bf16[20,256]{1,0:T(8,128)(2,1)} %nv_ref.1, bf16[1536,256]{1,0:T(8,128)(2,1)} %bitcast.55, bf16[1536,256]{1,0:T(8,128)(2,1)} %bitcast.56, ...), custom_call_target="tpu_custom_call" | custom-call | tf_op jit(solution)/shard_map/pallas_call | solution.py:81
  3.8 7.0 %all-to-all-start = ((f32[8,40,128]{2,1,0:T(8,128)}), f32[8,40,128]{2,1,0:T(8,128)S(1)}, u32[]{:S(2)}, u32[]{:S(2)}) async-start(f32[8,40,128]{2,1,0:T(8,128)} %shard_map.136), calls=%async_computation | async-start | bytes 327680 | tf_op jit(solution)/shard_map/all_to_all | solution.py:158
  10.8 0.1 copy.56
  11.1 0.2 reduce_window_sum.11
  11.2 0.2 select_reduce_fusion.1
  11.6 0.1 fusion.7
  11.7 7.3 %all-to-all-done = f32[8,40,128]{2,1,0:T(8,128)S(1)} async-done(((f32[8,40,128]{2,1,0:T(8,128)}), f32[8,40,128]{2,1,0:T(8,128)S(1)}, u32[]{:S(2)}, u32[]{:S(2)}) %all-to-all-start) | async-done | bytes 163872 | tf_op jit(solution)/shard_map/all_to_all | solution.py:158
  19.0 0.7 broadcast_in_dim.30
  19.7 3.4 %all-to-all-start.1 = ((f32[8,40,128]{2,1,0:T(8,128)}), f32[8,40,128]{2,1,0:T(8,128)S(1)}, u32[]{:S(2)}, u32[]{:S(2)}) async-start(f32[8,40,128]{2,1,0:T(8,128)} %broadcast_in_dim.30), calls=%async_computation.1 | async-start | bytes 327680 | tf_op jit(solution)/shard_map/all_to_all | solution.py:126
  23.1 0.1 fusion.11
  23.2 8.1 %all-to-all-done.1 = f32[8,40,128]{2,1,0:T(8,128)S(1)} async-done(((f32[8,40,128]{2,1,0:T(8,128)}), f32[8,40,128]{2,1,0:T(8,128)S(1)}, u32[]{:S(2)}, u32[]{:S(2)}) %all-to-all-start.1) | async-done | bytes 163872 | tf_op jit(solution)/shard_map/all_to_all | solution.py:126
  31.4 0.1 copy.59
  31.5 0.2 multiply_reduce_fusion
  31.8 0.1 multiply_convert_fusion
  31.9 1.6 %gather_fusion = bf16[192,16,128]{2,1,0:T(8,128)(2,1)} fusion(bf16[21,16,128]{2,1,0:T(8,128)(2,1)S(1)} %concatenate.11, s32[1024]{0:T(1024)S(1)} %pad_clamp_fusion), kind=kCustom, calls=%fused_computation | custom fusion | bytes 1573632 | tf_op jit(solution)/shard_map/jit(_take)/gather | solution.py:170
  33.5 17.3 %all-to-all-start.2 = ((bf16[64,48,128]{2,1,0:T(8,128)(2,1)}), bf16[64,48,128]{2,1,0:T(8,128)(2,1)S(1)}, u32[]{:S(2)}, u32[]{:S(2)}) async-start(bf16[64,48,128]{2,1,0:T(8,128)(2,1)} %bitcast.10), calls=%async_computation.2 | async-start | bytes 1572864 | tf_op jit(solution)/shard_map/all_to_all | solution.py:173
  50.9 0.1 copy.70
  51.0 22.6 %all-to-all-done.2 = bf16[64,48,128]{2,1,0:T(8,128)(2,1)S(1)} async-done(((bf16[64,48,128]{2,1,0:T(8,128)(2,1)}), bf16[64,48,128]{2,1,0:T(8,128)(2,1)S(1)}, u32[]{:S(2)}, u32[]{:S(2)}) %all-to-all-start.2) | async-done | bytes 786464 | tf_op jit(solution)/shard_map/all_to_all | solution.py:173
  73.6 0.2 reshape.88
  73.9 1.0 convolution_bitcast_fusion.1
  75.0 1.0 fusion.1
  76.2 0.4 convolution_convert_fusion.1
  76.6 1.4 %copy.65 = bf16[192,16,128]{2,1,0:T(8,128)(2,1)} copy(bf16[192,16,128]{2,0,1:T(8,128)(2,1)S(1)} %convolution_convert_fusion.1) | data formatting | bytes 1572864 | tf_op jit(solution)/shard_map/convert_element_type | solution.py:181
  78.0 6.5 %all-to-all-start.3 = ((bf16[64,48,128]{2,1,0:T(8,128)(2,1)}), bf16[64,48,128]{2,1,0:T(8,128)(2,1)S(1)}, u32[]{:S(2)}, u32[]{:S(2)}) async-start(bf16[64,48,128]{2,1,0:T(8,128)(2,1)} %bitcast.24), calls=%async_computation.3 | async-start | bytes 1572864 | tf_op jit(solution)/shard_map/all_to_all | solution.py:180
  84.5 0.1 select_reduce_fusion
  84.6 22.7 %all-to-all-done.3 = bf16[64,48,128]{2,1,0:T(8,128)(2,1)S(1)} async-done(((bf16[64,48,128]{2,1,0:T(8,128)(2,1)}), bf16[64,48,128]{2,1,0:T(8,128)(2,1)S(1)}, u32[]{:S(2)}, u32[]{:S(2)}) %all-to-all-start.3) | async-done | bytes 786464 | tf_op jit(solution)/shard_map/all_to_all | solution.py:180
  107.3 0.3 reshape.94
  107.6 0.4 convolution_convert_fusion
  108.1 0.6 copy.67
  108.7 3.4 %all-to-all-start.4 = ((bf16[8,40,128]{2,1,0:T(8,128)(2,1)}), bf16[8,40,128]{2,1,0:T(8,128)(2,1)S(1)}, u32[]{:S(2)}, u32[]{:S(2)}) async-start(bf16[8,40,128]{2,1,0:T(8,128)(2,1)} %copy.67), calls=%async_computation.4 | async-start | bytes 163840 | tf_op jit(solution)/shard_map/all_to_all | solution.py:118
  112.1 8.4 %all-to-all-done.4 = bf16[8,40,128]{2,1,0:T(8,128)(2,1)S(1)} async-done(((bf16[8,40,128]{2,1,0:T(8,128)(2,1)}), bf16[8,40,128]{2,1,0:T(8,128)(2,1)S(1)}, u32[]{:S(2)}, u32[]{:S(2)}) %all-to-all-start.4) | async-done | bytes 81952 | tf_op jit(solution)/shard_map/all_to_all | solution.py:118
  120.6 0.6 fusion.10
  (30 shorter events, 0.8 us)
Async XLA Ops:
  0.0 73.9 %copy-start = (bf16[1,2048,176]{1,2,0:T(8,128)(2,1)S(1)}, bf16[1,2048,176]{1,2,0:T(8,128)(2,1)}, u32[]{:S(2)}) copy-start(bf16[1,2048,176]{1,2,0:T(8,128)(2,1)} %param.25) | copy-start | bytes 2162692
  0.0 10.8 %copy-start.2 = (s32[20,6]{0,1:T(8,128)S(1)}, s32[20,6]{0,1:T(8,128)}, u32[]{:S(2)}) copy-start(s32[20,6]{0,1:T(8,128)} %param.23) | copy-start | bytes 1444
  3.8 28.0 %copy-start.3 = (f32[2048]{0:T(1024)S(1)}, f32[2048]{0:T(1024)}, u32[]{:S(2)}) copy-start(f32[2048]{0:T(1024)} %param.22) | copy-start | bytes 24580
  3.8 15.2 %all-to-all-start = ((f32[8,40,128]{2,1,0:T(8,128)}), f32[8,40,128]{2,1,0:T(8,128)S(1)}, u32[]{:S(2)}, u32[]{:S(2)}) async-start(f32[8,40,128]{2,1,0:T(8,128)} %shard_map.136), calls=%async_computation | async-start | bytes 327680 | tf_op jit(solution)/shard_map/all_to_all | solution.py:158
  19.7 11.7 %all-to-all-start.1 = ((f32[8,40,128]{2,1,0:T(8,128)}), f32[8,40,128]{2,1,0:T(8,128)S(1)}, u32[]{:S(2)}, u32[]{:S(2)}) async-start(f32[8,40,128]{2,1,0:T(8,128)} %broadcast_in_dim.30), calls=%async_computation.1 | async-start | bytes 327680 | tf_op jit(solution)/shard_map/all_to_all | solution.py:126
  33.5 17.3 %copy-start.1 = (bf16[1,176,2048]{2,1,0:T(8,128)(2,1)S(1)}, bf16[1,176,2048]{2,1,0:T(8,128)(2,1)}, u32[]{:S(2)}) copy-start(bf16[1,176,2048]{2,1,0:T(8,128)(2,1)} %param.27) | copy-start | bytes 2162692
  33.5 40.1 %all-to-all-start.2 = ((bf16[64,48,128]{2,1,0:T(8,128)(2,1)}), bf16[64,48,128]{2,1,0:T(8,128)(2,1)S(1)}, u32[]{:S(2)}, u32[]{:S(2)}) async-start(bf16[64,48,128]{2,1,0:T(8,128)(2,1)} %bitcast.10), calls=%async_computation.2 | async-start | bytes 1572864 | tf_op jit(solution)/shard_map/all_to_all | solution.py:173
  73.9 1.1 copy-start.5
  78.0 6.5 %copy-start.4 = (f32[20,6]{0,1:T(8,128)S(1)}, f32[20,6]{0,1:T(8,128)}, u32[]{:S(2)}) copy-start(f32[20,6]{0,1:T(8,128)} %param.24) | copy-start | bytes 1444
  78.0 29.3 %all-to-all-start.3 = ((bf16[64,48,128]{2,1,0:T(8,128)(2,1)}), bf16[64,48,128]{2,1,0:T(8,128)(2,1)S(1)}, u32[]{:S(2)}, u32[]{:S(2)}) async-start(bf16[64,48,128]{2,1,0:T(8,128)(2,1)} %bitcast.24), calls=%async_computation.3 | async-start | bytes 1572864 | tf_op jit(solution)/shard_map/all_to_all | solution.py:180
  108.7 11.8 %all-to-all-start.4 = ((bf16[8,40,128]{2,1,0:T(8,128)(2,1)}), bf16[8,40,128]{2,1,0:T(8,128)(2,1)S(1)}, u32[]{:S(2)}, u32[]{:S(2)}) async-start(bf16[8,40,128]{2,1,0:T(8,128)(2,1)} %copy.67), calls=%async_computation.4 | async-start | bytes 163840 | tf_op jit(solution)/shard_map/all_to_all | solution.py:118
